TPU v7x, 256 devices: a whole 4x4x8 slice. The times are simulated.
256 devices in a mesh: sect: 2 (over y_lo), batch: 16 (over z, core), head: 8 (over x, y_hi).
Axes of the slice: x: 4, y: 4 (y_hi: 2, y_lo: 2; y = y_hi * 2 + y_lo), z: 8, core: 2. Of those that a mesh axis runs over, the one named last changes fastest.
Arguments:
- queries: bfloat16 [96, 16, 512], P('batch', 'head', 'sect'), may hold values from -51 to 51
- newest_key_value: bfloat16 [96, 4, 256], P('batch'), may hold values from -5 to 5
- page_cache: bfloat16 [96, 256, 64, 256], P('batch', ('sect', 'head')), may hold values from -4 to 4
- lengths: int32 [96], P('batch'), may hold values from 2048 to 4096, as said below
- page_ids: int32 [96, 4, 32], P('batch'), may hold values from 0 to 63, as said below
- out_weight: bfloat16 [8192, 4096], P(('sect', 'head'), 'batch'), may hold values from -0.0625 to 0.0625
- residual: bfloat16 [96, 4096], P(None, 'batch'), may hold values from -2 to 2
- norm_gain: float32 [4096], P('batch'), may hold values from 0.25 to 1.75
- expert_ids: int32 [96, 8], replicated, may hold values from 0 to 63, all different within a row; in each aligned block of 96 rows (0 to 95, 96 to 191, ...) at most 24 rows name the same one
- route_weight: float32 [96, 8], replicated, may hold values from 0.1 to 1
- gate_up_weight: bfloat16 [32, 4096, 2, 3072], P(('sect', 'batch'), None, None, 'head'), may hold values from -0.09375 to 0.09375
- down_weight: bfloat16 [32, 3072, 4096], P(('sect', 'batch'), 'head'), may hold values from -0.15625 to 0.15625
Outputs:
- layer_out: bfloat16 [96, 4096], P(None, 'batch')
Inputs may be any that keep to these rules, and one draw needn't show every extreme that they name: `lengths`: some sequence holds exactly 4096 cached tokens and some exactly 2048. `page_ids`: each row lists 32 different pages in ascending order, all below the number of pages that hold the sequence's cached tokens, and always the last of those pages. `expert_ids`: each row names 8 different experts; over all rows no expert is named by more than 24 rows, a bound that some block reaches.
All inputs are finite; a program needn't handle non-finite values.
Results may differ from a plain program's by a relative error of at most 0.025.
Values may be sent and summed in bfloat16 or wider, within the bound.
No kernel may reach another device: no remote copies, remote signals or barrier semaphores. Data moves between devices by JAX's collectives and lax.ppermute only.
A program may use at most 128 MiB of HBM per device.

v0:
```python
import math

import jax
import jax.numpy as jnp
from jax import lax
from jax.sharding import PartitionSpec as P

D = 4096
EXPERTS = 64


NEG_FILL = -1e30
NORM_EPS = 1e-06


def copy_for_each(shard, axis):
    copies = jnp.broadcast_to(shard, (lax.axis_size(axis), *shard.shape))
    return lax.all_to_all(copies, axis, split_axis=0, concat_axis=0, tiled=True)


def in_order(pieces, dim):
    lengths = list(pieces.shape[1:])
    lengths[dim] *= pieces.shape[0]
    return jnp.moveaxis(pieces, 0, dim).reshape(lengths)


def gathered_copies(shard, axis, dim):
    pieces = copy_for_each(shard, axis)
    return in_order(pieces, dim)


def from_partner(shard, axis, distance):
    return lax.ppermute(shard, axis, [(i, i ^ 1 << distance) for i in range(lax.axis_size(axis))])


def taken_together(shard, axis):
    return copy_for_each(shard, axis).astype(jnp.float32).sum(axis=0)


def of_everyone(shard, axis):
    return copy_for_each(shard, axis).sum(axis=0)


def merge_pair(first, second):
    first_max, first_sum, first_acc = first
    second_max, second_sum, second_acc = second
    joined = jnp.maximum(first_max, second_max)
    first_factor = jnp.exp(first_max - joined)
    second_factor = jnp.exp(second_max - joined)
    return (
        joined,
        first_sum * first_factor + second_sum * second_factor,
        first_acc * first_factor[..., None] + second_acc * second_factor[..., None],
    )


def head_slice(partial_value, begin_at, span_size):
    return tuple(
        (lax.dynamic_slice_in_dim(member, begin_at, span_size, 1) for member in partial_value)
    )


def on_device(
    queries,
    newest_key_value,
    page_cache,
    lengths,
    page_ids,
    out_weight,
    residual,
    norm_gain,
    expert_ids,
    route_weight,
    gate_up_weight,
    down_weight,
):
    seq_count = queries.shape[0]
    head_dim = newest_key_value.shape[2] // 2
    kv_heads = newest_key_value.shape[1]
    sect_size = lax.axis_size("sect")
    head_size = lax.axis_size("head")
    batch_size = lax.axis_size("batch")
    group_size = sect_size * head_size // kv_heads
    position = lax.axis_index("sect") * head_size + lax.axis_index("head")
    kv_index = position // group_size
    quarter = position % group_size
    local_pages = page_cache.shape[1]
    page_len = page_cache.shape[2]
    scaling = 1.0 / math.sqrt(head_dim)
    all_heads = gathered_copies(queries, "head", 1)
    kv_local = kv_index % (kv_heads // sect_size)
    group_query = lax.dynamic_slice_in_dim(all_heads, kv_local * head_dim, head_dim, 2)
    heads_dev = all_heads.shape[1] // group_size
    block_cols = heads_dev * head_dim
    chosen = lax.dynamic_index_in_dim(page_ids, kv_index, 1, keepdims=False)
    leading_page = quarter * local_pages
    page_number = jnp.broadcast_to(
        leading_page + jnp.arange(local_pages, dtype=jnp.int32), (seq_count, local_pages)
    )
    page_used = jnp.any(chosen[:, :, None] == page_number[:, None, :], axis=1)
    token_place = (
        page_number[:, :, None] * page_len + jnp.arange(page_len, dtype=jnp.int32)[None, None, :]
    )
    key_count = page_cache.shape[1] * page_len
    usable_pages = (page_used[:, :, None] & (token_place < lengths[:, None, None])).reshape(
        seq_count, key_count
    )
    gathered_keys = page_cache[..., :head_dim].reshape(seq_count, key_count, head_dim)
    gathered_values = page_cache[..., head_dim:].reshape(seq_count, key_count, head_dim)
    scores = (
        jnp.einsum("shd,skd->shk", group_query, gathered_keys, preferred_element_type=jnp.float32)
        * scaling
    )
    scores = jnp.where(usable_pages[:, None, :], scores, NEG_FILL)
    newest_entry = lax.dynamic_index_in_dim(newest_key_value, kv_index, 1, keepdims=False)
    fresh_score = (
        jnp.einsum(
            "shd,sd->sh",
            group_query,
            newest_entry[:, :head_dim],
            preferred_element_type=jnp.float32,
        )
        * scaling
    )
    leading = quarter == 0
    fresh_score = jnp.where(leading, fresh_score, NEG_FILL)
    running_max = jnp.maximum(jnp.max(scores, axis=2), fresh_score)
    weights = jnp.where(usable_pages[:, None, :], jnp.exp(scores - running_max[..., None]), 0.0)
    fresh_weight = jnp.where(leading, jnp.exp(fresh_score - running_max), 0.0)
    running_sum = jnp.sum(weights, axis=2) + fresh_weight
    weighted = jnp.einsum(
        "shk,skd->shd",
        weights.astype(jnp.bfloat16),
        gathered_values,
        preferred_element_type=jnp.float32,
    )
    weighted = weighted + fresh_weight.astype(jnp.bfloat16).astype(jnp.float32)[
        ..., None
    ] * newest_entry[:, None, head_dim:].astype(jnp.float32)
    partial_value = (running_max, running_sum, weighted)
    bit_count = group_size.bit_length() - 1
    for bit_index in reversed(range(bit_count)):
        half_heads = partial_value[0].shape[1] // 2
        keep_half = quarter >> bit_index & 1
        kept = head_slice(partial_value, keep_half * half_heads, half_heads)
        sent = head_slice(partial_value, (1 - keep_half) * half_heads, half_heads)
        partner = from_partner(sent, "head", bit_index)
        partial_value = merge_pair(kept, partner)
    attention = (
        (partial_value[2] / partial_value[1][..., None])
        .reshape(seq_count, block_cols)
        .astype(jnp.bfloat16)
    )
    head_terms = jnp.dot(
        gathered_copies(attention, "batch", 0), out_weight, preferred_element_type=jnp.float32
    )
    projected = taken_together(head_terms.astype(jnp.bfloat16), ("sect", "head")).astype(
        jnp.float32
    )
    hidden_state = residual.astype(jnp.float32) + projected
    squares = of_everyone(jnp.sum(hidden_state * hidden_state, axis=1), "batch")
    inverse = lax.rsqrt(squares / D + NORM_EPS)
    normed = (hidden_state * inverse[:, None] * norm_gain[None, :]).astype(jnp.bfloat16)
    token_count, top_count = expert_ids.shape
    capacity = 2 * token_count * top_count // EXPERTS
    pair_local = gate_up_weight.shape[0]
    flat_ids = expert_ids.reshape(-1)
    one_hot = (flat_ids[:, None] == jnp.arange(EXPERTS, dtype=jnp.int32)[None, :]).astype(jnp.int32)
    earlier = jnp.cumsum(one_hot, axis=0) - one_hot
    rank_in = jnp.sum(earlier * one_hot, axis=1)
    sub_half = lax.axis_index("head") // (head_size // 2)
    pair_first = lax.axis_index("sect") * (batch_size * pair_local)
    local_pair = flat_ids // 2 - pair_first
    in_sect = (local_pair >= 0) & (local_pair < batch_size * pair_local)
    full_slot = (
        (local_pair // pair_local * 2 + flat_ids % 2) * pair_local + local_pair % pair_local
    ) * capacity + rank_in
    full_slot = jnp.where(in_sect, full_slot, -1)
    slot_dev = pair_local * capacity
    slot_total = batch_size * 2 * slot_dev
    send_count = batch_size * slot_dev
    matches = (
        full_slot.reshape(token_count, top_count)[None, :, :]
        == jnp.arange(slot_total, dtype=jnp.int32)[:, None, None]
    )
    selector_full = (
        jnp.any(matches, axis=2).astype(jnp.bfloat16).reshape(batch_size, 2, slot_dev, token_count)
    )
    selector = lax.dynamic_index_in_dim(selector_full, sub_half, 1, keepdims=False).reshape(
        send_count, token_count
    )
    coefficient = route_weight / jnp.sum(route_weight, axis=1, keepdims=True)
    combine_full = jnp.sum(jnp.where(matches, coefficient[None, :, :], 0.0), axis=2).T
    cols_dev = normed.shape[1]
    outgoing = jnp.dot(selector, normed, preferred_element_type=jnp.float32).astype(jnp.bfloat16)
    outgoing = outgoing.reshape(batch_size, pair_local, capacity, cols_dev)
    arrived = lax.all_to_all(outgoing, "batch", split_axis=0, concat_axis=3, tiled=True)[0]
    mixture = jnp.einsum(
        "ecd,edgf->ecgf", arrived, gate_up_weight, preferred_element_type=jnp.float32
    )
    activated = (jax.nn.silu(mixture[:, :, 0]) * mixture[:, :, 1]).astype(jnp.bfloat16)
    expert_part = jnp.einsum(
        "ecf,efd->ecd", activated, down_weight, preferred_element_type=jnp.float32
    )
    leaving = expert_part.reshape(1, slot_dev, batch_size, cols_dev)
    came_back = (
        lax.all_to_all(
            leaving.astype(jnp.bfloat16), "batch", split_axis=2, concat_axis=0, tiled=True
        )
        .astype(leaving.dtype)
        .reshape(send_count, cols_dev)
    )
    weights_used = lax.dynamic_index_in_dim(
        combine_full.reshape(token_count, batch_size, 2, slot_dev), sub_half, 2, keepdims=False
    )
    weights_used = weights_used.reshape(token_count, send_count)
    combined = jnp.dot(weights_used, came_back, preferred_element_type=jnp.float32)
    expert_mix = taken_together(combined.astype(jnp.bfloat16), ("sect", "head")).astype(jnp.float32)
    return (hidden_state + expert_mix).astype(jnp.bfloat16)


def solution(mesh):
    placed = (
        P("batch", "head", "sect"),
        P("batch", None, None),
        P("batch", ("sect", "head"), None, None),
        P("batch"),
        P("batch", None, None),
        P(("sect", "head"), "batch"),
        P(None, "batch"),
        P("batch"),
        P(),
        P(),
        P(("sect", "batch"), None, None, "head"),
        P(("sect", "batch"), "head", None),
    )
    return jax.shard_map(
        on_device, mesh=mesh, in_specs=placed, out_specs=P(None, "batch"), check_vma=False
    )
```

profile of v0, /device:TPU:32, one launch (start us, length us, event | category | flops | bytes accessed | tf_op | source)
XLA Modules:
  0.0 139.0 jit_solution(15450377240270368381)
XLA Ops:
  0.0 1.4 broadcast_in_dim.73
  1.4 6.9 %all-to-all-start = ((bf16[8,6,2,256]{3,2,1,0:T(2,128)(2,1)}), bf16[8,6,2,256]{3,2,1,0:T(2,128)(2,1)S(1)}, u32[]{:S(2)}, u32[]{:S(2)}) async-start(bf16[8,6,2,256]{3,2,1,0:T(2,128)(2,1)} %broadcast_in_dim.73), calls=%async_computation | async-start | bytes 98304 | tf_op jit(solution)/shard_map/all_to_all | solution.py:18
  9.6 3.2 %fusion.52 = (bf16[6,16,64,128]{3,2,1,0:T(8,128)(2,1)S(1)}, bf16[6,16,64,128]{3,2,1,0:T(8,128)(2,1)S(1)}) fusion(bf16[6,16,64,256]{3,2,1,0:T(8,128)(2,1)} %param.14), kind=kLoop, calls=%fused_computation.107 | loop fusion | bytes 6291456 | tf_op jit(solution)/shard_map/slice | solution.py:109
  13.0 3.0 %all-to-all-done = bf16[8,6,2,256]{3,2,1,0:T(2,128)(2,1)S(1)} async-done(((bf16[8,6,2,256]{3,2,1,0:T(2,128)(2,1)}), bf16[8,6,2,256]{3,2,1,0:T(2,128)(2,1)S(1)}, u32[]{:S(2)}, u32[]{:S(2)}) %all-to-all-start) | async-done | bytes 49184 | tf_op jit(solution)/shard_map/all_to_all | solution.py:18
  17.9 1.5 %collective-permute-start.4 = (f32[6,8]{1,0:T(8,128)S(1)}, f32[6,8]{1,0:T(8,128)S(1)}, u32[]{:S(2)}, u32[]{:S(2)}) collective-permute-start(f32[6,8]{1,0:T(8,128)S(1)} %constant_dynamic-slice_fusion.4), channel_id=1, source_target_pairs={{0,2},{1,3},{2,0},{3,1},{4,6},{5,7},{6,4},{7,5},{8,10},{9,11},{10,... | collective-permute-start | bytes 584 | tf_op jit(solution)/shard_map/ppermute | solution.py:33
  21.6 1.4 %collective-permute-start.2 = (f32[6,4]{1,0:T(8,128)S(1)}, f32[6,4]{1,0:T(8,128)S(1)}, u32[]{:S(2)}, u32[]{:S(2)}) collective-permute-start(f32[6,4]{1,0:T(8,128)S(1)} %constant_dynamic-slice_fusion.7), channel_id=1, source_target_pairs={{0,1},{1,0},{2,3},{3,2},{4,5},{5,4},{6,7},{7,6},{8,9},{9,8},{10,11... | collective-permute-start | bytes 296 | tf_op jit(solution)/shard_map/ppermute | solution.py:33
  23.1 2.1 %collective-permute-start.5 = (f32[6,4]{1,0:T(8,128)S(1)}, f32[6,4]{1,0:T(8,128)S(1)}, u32[]{:S(2)}, u32[]{:S(2)}) collective-permute-start(f32[6,4]{1,0:T(8,128)S(1)} %constant_dynamic-slice_fusion.2), channel_id=1, source_target_pairs={{0,1},{1,0},{2,3},{3,2},{4,5},{5,4},{6,7},{7,6},{8,9},{9,8},{10,11... | collective-permute-start | bytes 296 | tf_op jit(solution)/shard_map/ppermute | solution.py:33
  25.3 1.5 %collective-permute-start.3 = (f32[6,4,128]{2,1,0:T(4,128)S(1)}, f32[6,4,128]{2,1,0:T(4,128)S(1)}, u32[]{:S(2)}, u32[]{:S(2)}) collective-permute-start(f32[6,4,128]{2,1,0:T(4,128)S(1)} %constant_dynamic-slice_fusion.6), channel_id=1, source_target_pairs={{0,1},{1,0},{2,3},{3,2},{4,5},{5,4},{6,7},{7,6},{8,9},{9,8},{10,11... | collective-permute-start | bytes 36872 | tf_op jit(solution)/shard_map/ppermute | solution.py:33
  26.8 1.4 %collective-permute-done.5 = f32[6,4]{1,0:T(8,128)S(1)} collective-permute-done((f32[6,4]{1,0:T(8,128)S(1)}, f32[6,4]{1,0:T(8,128)S(1)}, u32[]{:S(2)}, u32[]{:S(2)}) %collective-permute-start.5) | collective-permute-done | bytes 128 | tf_op jit(solution)/shard_map/ppermute | solution.py:33
  28.3 2.3 %collective-permute-done.3 = f32[6,4,128]{2,1,0:T(4,128)S(1)} collective-permute-done((f32[6,4,128]{2,1,0:T(4,128)S(1)}, f32[6,4,128]{2,1,0:T(4,128)S(1)}, u32[]{:S(2)}, u32[]{:S(2)}) %collective-permute-start.3) | collective-permute-done | bytes 12320 | tf_op jit(solution)/shard_map/ppermute | solution.py:33
  31.4 8.6 %all-to-all-start.1 = ((bf16[16,6,512]{2,1,0:T(8,128)(2,1)}), bf16[16,6,512]{2,1,0:T(8,128)(2,1)S(1)}, u32[]{:S(2)}, u32[]{:S(2)}) async-start(bf16[16,6,512]{2,1,0:T(8,128)(2,1)} %broadcast_in_dim.78), calls=%async_computation.1 | async-start | bytes 262144 | tf_op jit(solution)/shard_map/all_to_all | solution.py:18
  40.2 7.1 %all-to-all-done.1 = bf16[16,6,512]{2,1,0:T(8,128)(2,1)S(1)} async-done(((bf16[16,6,512]{2,1,0:T(8,128)(2,1)}), bf16[16,6,512]{2,1,0:T(8,128)(2,1)S(1)}, u32[]{:S(2)}, u32[]{:S(2)}) %all-to-all-start.1) | async-done | bytes 98336 | tf_op jit(solution)/shard_map/all_to_all | solution.py:18
  47.6 1.0 broadcast_in_dim.79
  48.6 4.9 %all-to-all-start.2 = ((bf16[16,96,256]{2,1,0:T(8,128)(2,1)}), bf16[16,96,256]{2,1,0:T(8,128)(2,1)S(1)}, u32[]{:S(2)}, u32[]{:S(2)}) async-start(bf16[16,96,256]{2,1,0:T(8,128)(2,1)} %broadcast_in_dim.79), calls=%async_computation.2 | async-start | bytes 1572864 | tf_op jit(solution)/shard_map/all_to_all | solution.py:18
  53.5 1.8 %reduce-window.6 = s32[64,6,128]{2,0,1:T(8,128)S(1)} reduce-window(s32[64,6,128]{2,0,1:T(8,128)S(1)} %fusion.16, s32[]{:T(128)} %constant.119.clone.1), window={size=1x1x128 pad=0_0x0_0x127_0}, to_apply=%region_4.5 | reduce-window | flops 6242304 | bytes 393220 | tf_op jit(solution)/shard_map/reduce-window
  55.9 0.8 fusion.2
  56.9 12.5 %all-to-all-done.2 = bf16[16,96,256]{2,1,0:T(8,128)(2,1)S(1)} async-done(((bf16[16,96,256]{2,1,0:T(8,128)(2,1)}), bf16[16,96,256]{2,1,0:T(8,128)(2,1)S(1)}, u32[]{:S(2)}, u32[]{:S(2)}) %all-to-all-start.2) | async-done | bytes 786464 | tf_op jit(solution)/shard_map/all_to_all | solution.py:18
  70.3 4.9 %all-to-all-start.3 = ((f32[16,1,96]{2,1,0:T(1,128)}), f32[16,1,96]{2,1,0:T(1,128)S(1)}, u32[]{:S(2)}, u32[]{:S(2)}) async-start(f32[16,1,96]{2,1,0:T(1,128)} %broadcast_in_dim.82), calls=%async_computation.3 | async-start | bytes 16384 | tf_op jit(solution)/shard_map/all_to_all | solution.py:18
  75.2 6.3 %all-to-all-done.3 = f32[16,1,96]{2,1,0:T(1,128)S(1)} async-done(((f32[16,1,96]{2,1,0:T(1,128)}), f32[16,1,96]{2,1,0:T(1,128)S(1)}, u32[]{:S(2)}, u32[]{:S(2)}) %all-to-all-start.3) | async-done | bytes 6176 | tf_op jit(solution)/shard_map/all_to_all | solution.py:18
  81.5 0.9 convolution_convert_fusion.1
  82.4 5.4 %all-to-all-start.4 = ((bf16[16,1,24,256]{3,2,1,0:T(8,128)(2,1)}), bf16[16,1,24,256]{3,2,1,0:T(8,128)(2,1)}, u32[]{:S(2)}, u32[]{:S(2)}) async-start(bf16[16,1,24,256]{3,2,1,0:T(8,128)(2,1)} %bitcast.15), calls=%async_computation.4 | async-start | bytes 393216 | tf_op jit(solution)/shard_map/all_to_all | solution.py:197
  87.8 3.4 %copy.102 = bf16[4096,384]{1,0:T(8,128)(2,1)S(1)} copy(bf16[4096,384]{0,1:T(8,128)(2,1)} %bitcast.99) | data formatting | bytes 6291456 | tf_op jit(solution)/shard_map/ecf,efd->ecd/dot_general | solution.py:202
  91.2 1.3 reduce_sum.78
  92.5 4.0 %all-to-all-done.4 = bf16[16,1,24,256]{3,2,1,0:T(8,128)(2,1)} async-done(((bf16[16,1,24,256]{3,2,1,0:T(8,128)(2,1)}), bf16[16,1,24,256]{3,2,1,0:T(8,128)(2,1)}, u32[]{:S(2)}, u32[]{:S(2)}) %all-to-all-start.4) | async-done | bytes 196640 | tf_op jit(solution)/shard_map/all_to_all | solution.py:197
  96.5 1.6 %copy.96 = bf16[1,1,24,16,256]{4,3,2,1,0:T(8,128)(2,1)} copy(bf16[1,1,24,16,256]{4,2,3,1,0:T(8,128)(2,1)} %bitcast.17) | data formatting | bytes 393216 | tf_op jit(solution)/shard_map/all_to_all | solution.py:197
  98.1 1.7 %reshape.200 = bf16[24,4096,1]{1,0,2:T(8,128)(2,1)} reshape(bf16[1,1,24,16,256]{4,3,2,1,0:T(8,128)(2,1)} %copy.96) | data formatting | bytes 393216 | tf_op jit(solution)/shard_map/reshape.7
  99.8 3.8 %fusion.5 = f32[1,24,2,384]{3,1,2,0:T(8,128)S(1)} fusion(bf16[24,4096,1]{1,0,2:T(8,128)(2,1)} %reshape.200, bf16[4096,2,384]{2,1,0:T(2,128)(2,1)} %bitcast.112), kind=kOutput, calls=%fused_computation.12 | convolution fusion | flops 150994944 | bytes 6561792 | tf_op jit(solution)/shard_map/ecd,edgf->ecgf/dot_general | solution.py:198
  103.6 1.9 %fusion.4 = bf16[1,24,16,256]{3,1,0,2:T(8,128)(2,1)} fusion(bf16[16,256,384]{2,1,0:T(8,128)(2,1)S(1)} %bitcast.96, f32[1,24,2,384]{3,1,2,0:T(8,128)S(1)} %fusion.5), kind=kOutput, calls=%fused_computation.11 | convolution fusion | flops 75651072 | bytes 3416064 | tf_op jit(solution)/shard_map/ecf,efd->ecd/dot_general | solution.py:202
  105.5 4.8 %all-to-all-start.5 = ((bf16[1,24,16,256]{3,1,0,2:T(8,128)(2,1)}), bf16[1,24,16,256]{3,1,0,2:T(8,128)(2,1)S(1)}, u32[]{:S(2)}, u32[]{:S(2)}) async-start(bf16[1,24,16,256]{3,1,0,2:T(8,128)(2,1)} %fusion.4), calls=%async_computation.5 | async-start | bytes 393216 | tf_op jit(solution)/shard_map/all_to_all | solution.py:207
  111.1 1.6 %select_reduce_fusion = bf16[768,96]{0,1:T(8,128)(2,1)S(1)} fusion(f32[96,8]{1,0:T(8,128)S(1)} %copy.91, s32[96,8]{1,0:T(8,128)} %copy-done.2), kind=kLoop, calls=%fused_computation.2 | loop fusion | flops 1695744 | bytes 153600 | tf_op jit(solution)/shard_map/reduce_sum | solution.py:193
  112.9 6.1 %all-to-all-done.5 = bf16[1,24,16,256]{3,1,0,2:T(8,128)(2,1)S(1)} async-done(((bf16[1,24,16,256]{3,1,0,2:T(8,128)(2,1)}), bf16[1,24,16,256]{3,1,0,2:T(8,128)(2,1)S(1)}, u32[]{:S(2)}, u32[]{:S(2)}) %all-to-all-start.5) | async-done | bytes 196640 | tf_op jit(solution)/shard_map/all_to_all | solution.py:207
  119.2 19.0 %all_to_all.56 = bf16[16,96,256]{2,1,0:T(8,128)(2,1)S(1)} all-to-all(bf16[16,96,256]{2,1,0:T(8,128)(2,1)S(1)} %broadcast_in_dim.83), channel_id=1, replica_groups=mesh['sect'=2,'batch'=16,'head'=8] {'sect','head'}, dimensions={0} | all-to-all | bytes 1572864 | tf_op jit(solution)/shard_map/all_to_all | solution.py:18
  (78 shorter events, 10.6 us)
Async XLA Ops:
  0.0 47.4 %copy-start = (bf16[512,256]{1,0:T(8,128)(2,1)S(1)}, bf16[512,256]{1,0:T(8,128)(2,1)}, u32[]{:S(2)}) copy-start(bf16[512,256]{1,0:T(8,128)(2,1)} %param.17) | copy-start | bytes 786436
  1.4 14.7 %all-to-all-start = ((bf16[8,6,2,256]{3,2,1,0:T(2,128)(2,1)}), bf16[8,6,2,256]{3,2,1,0:T(2,128)(2,1)S(1)}, u32[]{:S(2)}, u32[]{:S(2)}) async-start(bf16[8,6,2,256]{3,2,1,0:T(2,128)(2,1)} %broadcast_in_dim.73), calls=%async_computation | async-start | bytes 98304 | tf_op jit(solution)/shard_map/all_to_all | solution.py:18
  9.6 3.2 %copy-start.4 = (bf16[6,4,256]{2,1,0:T(4,128)(2,1)S(1)}, bf16[6,4,256]{2,1,0:T(4,128)(2,1)}, u32[]{:S(2)}) copy-start(bf16[6,4,256]{2,1,0:T(4,128)(2,1)} %param.13) | copy-start | bytes 36868
  9.6 3.3 %copy-start.6 = (s32[6]{0:T(128)S(1)}, s32[6]{0:T(128)}, u32[]{:S(2)}) copy-start(s32[6]{0:T(128)} %param.15) | copy-start | bytes 76
  16.3 23.7 %copy-start.3 = (s32[96,8]{0,1:T(8,128)S(1)}, s32[96,8]{0,1:T(8,128)}, u32[]{:S(2)}) copy-start(s32[96,8]{0,1:T(8,128)} %param.20) | copy-start | bytes 9220
  17.2 3.6 %collective-permute-start = (f32[6,8]{1,0:T(8,128)S(1)}, f32[6,8]{1,0:T(8,128)S(1)}, u32[]{:S(2)}, u32[]{:S(2)}) collective-permute-start(f32[6,8]{1,0:T(8,128)S(1)} %constant_dynamic-slice_fusion.10), channel_id=1, source_target_pairs={{0,2},{1,3},{2,0},{3,1},{4,6},{5,7},{6,4},{7,5},{8,10},{9,11},{10,... | collective-permute-start | bytes 584 | tf_op jit(solution)/shard_map/ppermute | solution.py:33
  17.9 3.6 %collective-permute-start.4 = (f32[6,8]{1,0:T(8,128)S(1)}, f32[6,8]{1,0:T(8,128)S(1)}, u32[]{:S(2)}, u32[]{:S(2)}) collective-permute-start(f32[6,8]{1,0:T(8,128)S(1)} %constant_dynamic-slice_fusion.4), channel_id=1, source_target_pairs={{0,2},{1,3},{2,0},{3,1},{4,6},{5,7},{6,4},{7,5},{8,10},{9,11},{10,... | collective-permute-start | bytes 584 | tf_op jit(solution)/shard_map/ppermute | solution.py:33
  19.7 5.5 %collective-permute-start.1 = (f32[6,8,128]{2,1,0:T(8,128)S(1)}, f32[6,8,128]{2,1,0:T(8,128)S(1)}, u32[]{:S(2)}, u32[]{:S(2)}) collective-permute-start(f32[6,8,128]{2,1,0:T(8,128)S(1)} %constant_dynamic-slice_fusion.9), channel_id=1, source_target_pairs={{0,2},{1,3},{2,0},{3,1},{4,6},{5,7},{6,4},{7,5},{8,10},{9,11},{10,... | collective-permute-start | bytes 73736 | tf_op jit(solution)/shard_map/ppermute | solution.py:33
  21.6 5.2 %collective-permute-start.2 = (f32[6,4]{1,0:T(8,128)S(1)}, f32[6,4]{1,0:T(8,128)S(1)}, u32[]{:S(2)}, u32[]{:S(2)}) collective-permute-start(f32[6,4]{1,0:T(8,128)S(1)} %constant_dynamic-slice_fusion.7), channel_id=1, source_target_pairs={{0,1},{1,0},{2,3},{3,2},{4,5},{5,4},{6,7},{7,6},{8,9},{9,8},{10,11... | collective-permute-start | bytes 296 | tf_op jit(solution)/shard_map/ppermute | solution.py:33
  23.1 5.1 %collective-permute-start.5 = (f32[6,4]{1,0:T(8,128)S(1)}, f32[6,4]{1,0:T(8,128)S(1)}, u32[]{:S(2)}, u32[]{:S(2)}) collective-permute-start(f32[6,4]{1,0:T(8,128)S(1)} %constant_dynamic-slice_fusion.2), channel_id=1, source_target_pairs={{0,1},{1,0},{2,3},{3,2},{4,5},{5,4},{6,7},{7,6},{8,9},{9,8},{10,11... | collective-permute-start | bytes 296 | tf_op jit(solution)/shard_map/ppermute | solution.py:33
  25.3 5.3 %collective-permute-start.3 = (f32[6,4,128]{2,1,0:T(4,128)S(1)}, f32[6,4,128]{2,1,0:T(4,128)S(1)}, u32[]{:S(2)}, u32[]{:S(2)}) collective-permute-start(f32[6,4,128]{2,1,0:T(4,128)S(1)} %constant_dynamic-slice_fusion.6), channel_id=1, source_target_pairs={{0,1},{1,0},{2,3},{3,2},{4,5},{5,4},{6,7},{7,6},{8,9},{9,8},{10,11... | collective-permute-start | bytes 36872 | tf_op jit(solution)/shard_map/ppermute | solution.py:33
  31.4 16.0 %all-to-all-start.1 = ((bf16[16,6,512]{2,1,0:T(8,128)(2,1)}), bf16[16,6,512]{2,1,0:T(8,128)(2,1)S(1)}, u32[]{:S(2)}, u32[]{:S(2)}) async-start(bf16[16,6,512]{2,1,0:T(8,128)(2,1)} %broadcast_in_dim.78), calls=%async_computation.1 | async-start | bytes 262144 | tf_op jit(solution)/shard_map/all_to_all | solution.py:18
  47.6 22.0 %copy-start.1 = (bf16[96,256]{1,0:T(8,128)(2,1)S(1)}, bf16[96,256]{1,0:T(8,128)(2,1)}, u32[]{:S(2)}) copy-start(bf16[96,256]{1,0:T(8,128)(2,1)} %param.18) | copy-start | bytes 147460
  47.6 33.9 %copy-start.5 = (f32[256]{0:T(256)S(1)}, f32[256]{0:T(256)}, u32[]{:S(2)}) copy-start(f32[256]{0:T(256)} %param.19) | copy-start | bytes 3076
  48.6 20.9 %all-to-all-start.2 = ((bf16[16,96,256]{2,1,0:T(8,128)(2,1)}), bf16[16,96,256]{2,1,0:T(8,128)(2,1)S(1)}, u32[]{:S(2)}, u32[]{:S(2)}) async-start(bf16[16,96,256]{2,1,0:T(8,128)(2,1)} %broadcast_in_dim.79), calls=%async_computation.2 | async-start | bytes 1572864 | tf_op jit(solution)/shard_map/all_to_all | solution.py:18
  55.9 1.0 copy-start.2
  70.3 11.1 %all-to-all-start.3 = ((f32[16,1,96]{2,1,0:T(1,128)}), f32[16,1,96]{2,1,0:T(1,128)S(1)}, u32[]{:S(2)}, u32[]{:S(2)}) async-start(f32[16,1,96]{2,1,0:T(1,128)} %broadcast_in_dim.82), calls=%async_computation.3 | async-start | bytes 16384 | tf_op jit(solution)/shard_map/all_to_all | solution.py:18
  82.4 14.0 %all-to-all-start.4 = ((bf16[16,1,24,256]{3,2,1,0:T(8,128)(2,1)}), bf16[16,1,24,256]{3,2,1,0:T(8,128)(2,1)}, u32[]{:S(2)}, u32[]{:S(2)}) async-start(bf16[16,1,24,256]{3,2,1,0:T(8,128)(2,1)} %bitcast.15), calls=%async_computation.4 | async-start | bytes 393216 | tf_op jit(solution)/shard_map/all_to_all | solution.py:197
  105.5 13.4 %all-to-all-start.5 = ((bf16[1,24,16,256]{3,1,0,2:T(8,128)(2,1)}), bf16[1,24,16,256]{3,1,0,2:T(8,128)(2,1)S(1)}, u32[]{:S(2)}, u32[]{:S(2)}) async-start(bf16[1,24,16,256]{3,1,0,2:T(8,128)(2,1)} %fusion.4), calls=%async_computation.5 | async-start | bytes 393216 | tf_op jit(solution)/shard_map/all_to_all | solution.py:207
where the time goes:
time: 141 us; the launch traced here: 139 us
  waiting for transfers between devices  43.7 us (31%)
  starting transfers between devices  43.2 us (31%)
  blocking collectives  19 us (13%)
  local copies, waits for them, and re-layouts  16.2 us (11%)
  other arithmetic  8.35 us (6%)
  matrix products  8.16 us (6%)
    all_to_all x4, waiting for transfers between devices, copy_for_each(): return lax.all_to_all(copies, axis, split_axis=0, concat_axis=0, tiled=True)  28.9 us
    all_to_all x4, starting transfers between devices, copy_for_each(): return lax.all_to_all(copies, axis, split_axis=0, concat_axis=0, tiled=True)  25.3 us
    all_to_all x1, blocking collectives, copy_for_each(): return lax.all_to_all(copies, axis, split_axis=0, concat_axis=0, tiled=True)  19 us
    ppermute x6, starting transfers between devices, from_partner(): lax.ppermute(shard, axis, [(i, i ^ 1 << distance) for i in range(lax.axis...  7.76 us
    all_to_all x1, waiting for transfers between devices, on_device(): lax.all_to_all(leaving.astype(jnp.bfloat16), 'batch', split_axis=2, conca...  6.06 us
    all_to_all x1, starting transfers between devices, on_device(): lax.all_to_all(outgoing, 'batch', split_axis=0, concat_axis=3, tiled=True)  5.38 us
    ppermute x6, waiting for transfers between devices, from_partner(): lax.ppermute(shard, axis, [(i, i ^ 1 << distance) for i in range(lax.axis...  4.82 us
    all_to_all x1, starting transfers between devices, on_device(): lax.all_to_all(leaving.astype(jnp.bfloat16), 'batch', split_axis=2, conca...  4.76 us
  transfers between devices with their start and end apart: 12, of which 10 were waited for; matrix products, arithmetic and copies ran while one was open for 12% of the time, Pallas kernels for 0%

commit v1 on v0

--- a/solution.py
+++ b/solution.py
@@ -87,7 +87,7 @@
     local_pages = page_cache.shape[1]
     page_len = page_cache.shape[2]
     scaling = 1.0 / math.sqrt(head_dim)
-    all_heads = gathered_copies(queries, "head", 1)
+    all_heads = lax.all_gather(queries, "head", axis=1, tiled=True)
     kv_local = kv_index % (kv_heads // sect_size)
     group_query = lax.dynamic_slice_in_dim(all_heads, kv_local * head_dim, head_dim, 2)
     heads_dev = all_heads.shape[1] // group_size
@@ -152,13 +152,13 @@
         .astype(jnp.bfloat16)
     )
     head_terms = jnp.dot(
-        gathered_copies(attention, "batch", 0), out_weight, preferred_element_type=jnp.float32
-    )
-    projected = taken_together(head_terms.astype(jnp.bfloat16), ("sect", "head")).astype(
-        jnp.float32
-    )
+        lax.all_gather(attention, "batch", axis=0, tiled=True),
+        out_weight,
+        preferred_element_type=jnp.float32,
+    )
+    projected = lax.psum(head_terms, ("sect", "head"))
     hidden_state = residual.astype(jnp.float32) + projected
-    squares = of_everyone(jnp.sum(hidden_state * hidden_state, axis=1), "batch")
+    squares = lax.psum(jnp.sum(hidden_state * hidden_state, axis=1), "batch")
     inverse = lax.rsqrt(squares / D + NORM_EPS)
     normed = (hidden_state * inverse[:, None] * norm_gain[None, :]).astype(jnp.bfloat16)
     token_count, top_count = expert_ids.shape
@@ -215,7 +215,7 @@
     )
     weights_used = weights_used.reshape(token_count, send_count)
     combined = jnp.dot(weights_used, came_back, preferred_element_type=jnp.float32)
-    expert_mix = taken_together(combined.astype(jnp.bfloat16), ("sect", "head")).astype(jnp.float32)
+    expert_mix = lax.psum(combined, ("sect", "head"))
     return (hidden_state + expert_mix).astype(jnp.bfloat16)
 
 

time: 141 us -> 343 us (2.43)
  waiting for transfers between devices: 43.7 us -> 196 us
  blocking collectives: 19 us -> 73.9 us
  starting transfers between devices: 43.2 us -> 23.4 us
  between operations: 0.35 us -> 13.7 us
  matrix products: 8.16 us -> 12 us
    psum x0 -> x2, waiting for transfers between devices: none -> 184 us  [the longest x1 94.1 us: on_device(): projected = lax.psum(head_terms, ('sect', 'head'))]
    all_gather x0 -> x2, blocking collectives: none -> 52.5 us  [the longest x1 34.3 us: on_device(): all_heads = lax.all_gather(queries, 'head', axis=1, tiled=True)]
    all_to_all x4 -> x0, waiting for transfers between devices: 28.9 us -> none  [copy_for_each(): return lax.all_to_all(copies, axis, split_axis=0, concat_axis=0, tiled=True)]
    all_to_all x4 -> x0, starting transfers between devices: 25.3 us -> none  [copy_for_each(): return lax.all_to_all(copies, axis, split_axis=0, concat_axis=0, tiled=True)]
    psum x0 -> x1, blocking collectives: none -> 21.5 us  [on_device(): squares = lax.psum(jnp.sum(hidden_state * hidden_state, axis=1), 'batch')]
    all_to_all x1 -> x0, blocking collectives: 19 us -> none  [copy_for_each(): return lax.all_to_all(copies, axis, split_axis=0, concat_axis=0, tiled=True)]
    all_to_all x1, starting transfers between devices: 5.38 us -> 9.58 us  [on_device(): lax.all_to_all(outgoing, 'batch', split_axis=0, concat_axis=3, tiled=True)]
    broadcast_in_dim x5 -> x0, local copies, waits for them, and re-layouts: 3.66 us -> none  [copy_for_each(): copies = jnp.broadcast_to(shard, (lax.axis_size(axis), *shard.shape))]
  transfers between devices with their start and end apart: 12 -> 10, of which waited for: 10 -> 6; matrix products, arithmetic and copies ran while one was open for 12% -> 4% of each run, Pallas kernels for 0% -> 0%
where the time goes in v1:
time: 343 us; the launch traced here: 342 us
  waiting for transfers between devices  196 us (57%)
  blocking collectives  73.9 us (22%)
  starting transfers between devices  23.4 us (7%)
  between operations  13.7 us (4%)
  local copies, waits for them, and re-layouts  13.3 us (4%)
  matrix products  12 us (3%)
  other arithmetic  10.2 us (3%)
    psum x1, waiting for transfers between devices, on_device(): projected = lax.psum(head_terms, ('sect', 'head'))  94.1 us
    psum x1, waiting for transfers between devices, on_device(): expert_mix = lax.psum(combined, ('sect', 'head'))  89.4 us
    all_gather x1, blocking collectives, on_device(): all_heads = lax.all_gather(queries, 'head', axis=1, tiled=True)  34.3 us
    psum x1, blocking collectives, on_device(): squares = lax.psum(jnp.sum(hidden_state * hidden_state, axis=1), 'batch')  21.5 us
    all_gather x1, blocking collectives, on_device(): lax.all_gather(attention, 'batch', axis=0, tiled=True)  18.2 us
    all_to_all x1, starting transfers between devices, on_device(): lax.all_to_all(outgoing, 'batch', split_axis=0, concat_axis=3, tiled=True)  9.58 us
    ppermute x6, starting transfers between devices, from_partner(): lax.ppermute(shard, axis, [(i, i ^ 1 << distance) for i in range(lax.axis...  9.03 us
  transfers between devices with their start and end apart: 10, of which 6 were waited for; matrix products, arithmetic and copies ran while one was open for 4% of the time, Pallas kernels for 0%

profile of v1, /device:TPU:32, one launch (start us, length us, event | category | flops | bytes accessed | tf_op | source)
XLA Modules:
  0.0 342.4 jit_solution(5951458100370429770)
XLA Ops:
  6.5 0.7 copy.66
  7.3 34.3 %all_gather.6 = bf16[6,16,256]{2,0,1:T(8,128)(2,1)S(1)} all-gather(bf16[6,2,256]{2,0,1:T(8,128)(2,1)S(1)} %copy.66), channel_id=1, replica_groups=mesh['sect'=2,'batch'=16,'head'=8] {'head'}, dimensions={1}, use_global_device_ids=true | all-gather | bytes 55296 | tf_op jit(solution)/shard_map/all_gather | solution.py:90
  41.6 0.7 constant_dynamic-slice_fusion.14
  42.9 3.2 fusion.49
  46.4 1.3 fusion.50
  47.8 1.2 fusion.8
  49.1 2.0 collective-permute-start.4
  51.1 1.4 convolution_add_fusion
  53.0 1.8 reduce-window.6
  55.4 0.8 fusion.2
  56.6 3.2 collective-permute-start.2
  60.3 3.3 collective-permute-start.3
  63.6 1.4 collective-permute-done.5
  65.7 18.2 %all-gather = bf16[16,6,512]{2,1,0:T(8,128)(2,1)S(1)} all-gather(bf16[1,6,512]{2,1,0:T(8,128)(2,1)S(1)} %reshape.182), channel_id=1, replica_groups=mesh['sect'=2,'batch'=16,'head'=8] {'batch'}, dimensions={0}, use_global_device_ids=true | all-gather | bytes 104448 | tf_op jit(solution)/shard_map/all_gather | solution.py:155
  83.9 0.8 fusion.51
  84.8 94.1 %all-reduce.3.cloned.1.call-done = f32[96,256]{1,0:T(8,128)} async-done(((f32[96,256]{1,0:T(8,128)}), f32[96,256]{1,0:T(8,128)}) %all-reduce.3.cloned.1.call-update) | async-done | bytes 98320 | tf_op jit(solution)/shard_map/psum | solution.py:159
  178.9 1.0 multiply_reduce_fusion
  180.0 21.5 %psum.22 = f32[96]{0:T(128)S(1)} all-reduce(f32[96]{0:T(128)S(1)} %multiply_reduce_fusion), channel_id=1, replica_groups=mesh['sect'=2,'batch'=16,'head'=8] {'batch'}, use_global_device_ids=true, to_apply=%region_11.12 | all-reduce | flops 96 | bytes 768 | tf_op jit(solution)/shard_map/psum | solution.py:161
  201.4 1.8 convolution_convert_fusion.1
  203.3 9.6 %all-to-all-start = ((bf16[16,1,24,256]{3,2,1,0:T(8,128)(2,1)}), bf16[16,1,24,256]{3,2,1,0:T(8,128)(2,1)}, u32[]{:S(2)}, u32[]{:S(2)}) async-start(bf16[16,1,24,256]{3,2,1,0:T(8,128)(2,1)} %bitcast.13), calls=%async_computation | async-start | bytes 393216 | tf_op jit(solution)/shard_map/all_to_all | solution.py:197
  212.9 3.4 %copy.86 = bf16[4096,384]{1,0:T(8,128)(2,1)S(1)} copy(bf16[4096,384]{0,1:T(8,128)(2,1)} %bitcast.92) | data formatting | bytes 6291456 | tf_op jit(solution)/shard_map/ecf,efd->ecd/dot_general | solution.py:202
  216.9 4.6 %all-to-all-done = bf16[16,1,24,256]{3,2,1,0:T(8,128)(2,1)} async-done(((bf16[16,1,24,256]{3,2,1,0:T(8,128)(2,1)}), bf16[16,1,24,256]{3,2,1,0:T(8,128)(2,1)}, u32[]{:S(2)}, u32[]{:S(2)}) %all-to-all-start) | async-done | bytes 196640 | tf_op jit(solution)/shard_map/all_to_all | solution.py:197
  221.5 1.6 copy.80
  223.1 1.7 reshape.187
  224.8 3.8 %fusion.5 = f32[1,24,2,384]{3,1,2,0:T(8,128)S(1)} fusion(bf16[24,4096,1]{1,0,2:T(8,128)(2,1)} %reshape.187, bf16[4096,2,384]{2,1,0:T(2,128)(2,1)} %bitcast.102), kind=kOutput, calls=%fused_computation.10 | convolution fusion | flops 150994944 | bytes 6561792 | tf_op jit(solution)/shard_map/ecd,edgf->ecgf/dot_general | solution.py:198
  228.7 1.9 fusion.4
  230.6 4.8 %all-to-all-start.1 = ((bf16[1,24,16,256]{3,1,0,2:T(8,128)(2,1)}), bf16[1,24,16,256]{3,1,0,2:T(8,128)(2,1)S(1)}, u32[]{:S(2)}, u32[]{:S(2)}) async-start(bf16[1,24,16,256]{3,1,0,2:T(8,128)(2,1)} %fusion.4), calls=%async_computation.1 | async-start | bytes 393216 | tf_op jit(solution)/shard_map/all_to_all | solution.py:207
  236.2 1.6 select_reduce_fusion
  238.0 5.8 %all-to-all-done.1 = bf16[1,24,16,256]{3,1,0,2:T(8,128)(2,1)S(1)} async-done(((bf16[1,24,16,256]{3,1,0,2:T(8,128)(2,1)}), bf16[1,24,16,256]{3,1,0,2:T(8,128)(2,1)S(1)}, u32[]{:S(2)}, u32[]{:S(2)}) %all-to-all-start.1) | async-done | bytes 196640 | tf_op jit(solution)/shard_map/all_to_all | solution.py:207
  243.8 0.8 fusion.52
  244.7 89.4 %all-reduce.5.cloned.1.call-done = f32[96,256]{1,0:T(8,128)} async-done(((f32[96,256]{1,0:T(8,128)}), f32[96,256]{1,0:T(8,128)}) %all-reduce.5.cloned.1.call-update) | async-done | bytes 98320 | tf_op jit(solution)/shard_map/psum | solution.py:218
  334.0 1.5 add_convert_fusion
  (74 shorter events, 5.3 us)
Async XLA Ops:
  6.5 77.4 %copy-start = (bf16[512,256]{1,0:T(8,128)(2,1)S(1)}, bf16[512,256]{1,0:T(8,128)(2,1)}, u32[]{:S(2)}) copy-start(bf16[512,256]{1,0:T(8,128)(2,1)} %param.17) | copy-start | bytes 786436
  6.5 172.4 %all-reduce.3.cloned.1.call-start = ((), (), s32[]{:S(2)}) async-start(), calls=%async_computation.2 | async-start | bytes 196608 | tf_op jit(solution)/shard_map/psum | solution.py:159
  42.9 3.2 copy-start.6
  42.9 3.4 %copy-start.8 = (s32[6]{0:T(128)S(1)}, s32[6]{0:T(128)}, u32[]{:S(2)}) copy-start(s32[6]{0:T(128)} %param.15) | copy-start | bytes 76
  46.2 6.5 %copy-start.5 = (s32[96,8]{0,1:T(8,128)S(1)}, s32[96,8]{0,1:T(8,128)}, u32[]{:S(2)}) copy-start(s32[96,8]{0,1:T(8,128)} %param.20) | copy-start | bytes 9220
  47.7 8.7 %collective-permute-start = (f32[6,8]{1,0:T(8,128)S(1)}, f32[6,8]{1,0:T(8,128)S(1)}, u32[]{:S(2)}, u32[]{:S(2)}) collective-permute-start(f32[6,8]{1,0:T(8,128)S(1)} %constant_dynamic-slice_fusion.10), channel_id=1, source_target_pairs={{0,2},{1,3},{2,0},{3,1},{4,6},{5,7},{6,4},{7,5},{8,10},{9,11},{10,... | collective-permute-start | bytes 584 | tf_op jit(solution)/shard_map/ppermute | solution.py:33
  49.1 7.3 %collective-permute-start.4 = (f32[6,8]{1,0:T(8,128)S(1)}, f32[6,8]{1,0:T(8,128)S(1)}, u32[]{:S(2)}, u32[]{:S(2)}) collective-permute-start(f32[6,8]{1,0:T(8,128)S(1)} %constant_dynamic-slice_fusion.4), channel_id=1, source_target_pairs={{0,2},{1,3},{2,0},{3,1},{4,6},{5,7},{6,4},{7,5},{8,10},{9,11},{10,... | collective-permute-start | bytes 584 | tf_op jit(solution)/shard_map/ppermute | solution.py:33
  51.1 127.8 %copy-start.2 = (bf16[96,256]{1,0:T(8,128)(2,1)S(1)}, bf16[96,256]{1,0:T(8,128)(2,1)}, u32[]{:S(2)}) copy-start(bf16[96,256]{1,0:T(8,128)(2,1)} %param.18) | copy-start | bytes 147460
  51.1 150.3 %copy-start.7 = (f32[256]{0:T(256)S(1)}, f32[256]{0:T(256)}, u32[]{:S(2)}) copy-start(f32[256]{0:T(256)} %param.19) | copy-start | bytes 3076
  52.5 7.7 %collective-permute-start.1 = (f32[6,8,128]{2,1,0:T(8,128)S(1)}, f32[6,8,128]{2,1,0:T(8,128)S(1)}, u32[]{:S(2)}, u32[]{:S(2)}) collective-permute-start(f32[6,8,128]{2,1,0:T(8,128)S(1)} %constant_dynamic-slice_fusion.9), channel_id=1, source_target_pairs={{0,2},{1,3},{2,0},{3,1},{4,6},{5,7},{6,4},{7,5},{8,10},{9,11},{10,... | collective-permute-start | bytes 73736 | tf_op jit(solution)/shard_map/ppermute | solution.py:33
  55.4 157.5 %copy-start.3 = (s32[96,8]{1,0:T(8,128)}, s32[96,8]{1,0:T(8,128)S(1)}, u32[]{:S(2)}) copy-start(s32[96,8]{1,0:T(8,128)S(1)} %fusion.22) | copy-start | bytes 9220
  56.6 7.0 %collective-permute-start.2 = (f32[6,4]{1,0:T(8,128)S(1)}, f32[6,4]{1,0:T(8,128)S(1)}, u32[]{:S(2)}, u32[]{:S(2)}) collective-permute-start(f32[6,4]{1,0:T(8,128)S(1)} %constant_dynamic-slice_fusion.7), channel_id=1, source_target_pairs={{0,1},{1,0},{2,3},{3,2},{4,5},{5,4},{6,7},{7,6},{8,9},{9,8},{10,11... | collective-permute-start | bytes 296 | tf_op jit(solution)/shard_map/ppermute | solution.py:33
  59.9 5.1 %collective-permute-start.5 = (f32[6,4]{1,0:T(8,128)S(1)}, f32[6,4]{1,0:T(8,128)S(1)}, u32[]{:S(2)}, u32[]{:S(2)}) collective-permute-start(f32[6,4]{1,0:T(8,128)S(1)} %constant_dynamic-slice_fusion.2), channel_id=1, source_target_pairs={{0,1},{1,0},{2,3},{3,2},{4,5},{5,4},{6,7},{7,6},{8,9},{9,8},{10,11... | collective-permute-start | bytes 296 | tf_op jit(solution)/shard_map/ppermute | solution.py:33
  60.3 5.3 %collective-permute-start.3 = (f32[6,4,128]{2,1,0:T(4,128)S(1)}, f32[6,4,128]{2,1,0:T(4,128)S(1)}, u32[]{:S(2)}, u32[]{:S(2)}) collective-permute-start(f32[6,4,128]{2,1,0:T(4,128)S(1)} %constant_dynamic-slice_fusion.6), channel_id=1, source_target_pairs={{0,1},{1,0},{2,3},{3,2},{4,5},{5,4},{6,7},{7,6},{8,9},{9,8},{10,11... | collective-permute-start | bytes 36872 | tf_op jit(solution)/shard_map/ppermute | solution.py:33
  203.3 18.2 %all-to-all-start = ((bf16[16,1,24,256]{3,2,1,0:T(8,128)(2,1)}), bf16[16,1,24,256]{3,2,1,0:T(8,128)(2,1)}, u32[]{:S(2)}, u32[]{:S(2)}) async-start(bf16[16,1,24,256]{3,2,1,0:T(8,128)(2,1)} %bitcast.13), calls=%async_computation | async-start | bytes 393216 | tf_op jit(solution)/shard_map/all_to_all | solution.py:197
  212.9 3.4 %copy-start.4 = (f32[96,8]{0,1:T(8,128)S(1)}, f32[96,8]{0,1:T(8,128)}, u32[]{:S(2)}) copy-start(f32[96,8]{0,1:T(8,128)} %param.21) | copy-start | bytes 9220
  228.7 105.4 %copy-start.1 = (f32[96,256]{1,0:T(8,128)S(1)}, f32[96,256]{1,0:T(8,128)}, u32[]{:S(2)}) copy-start(f32[96,256]{1,0:T(8,128)} %all-reduce.3.cloned.1.call-done) | copy-start | bytes 294916
  230.6 13.3 %all-to-all-start.1 = ((bf16[1,24,16,256]{3,1,0,2:T(8,128)(2,1)}), bf16[1,24,16,256]{3,1,0,2:T(8,128)(2,1)S(1)}, u32[]{:S(2)}, u32[]{:S(2)}) async-start(bf16[1,24,16,256]{3,1,0,2:T(8,128)(2,1)} %fusion.4), calls=%async_computation.1 | async-start | bytes 393216 | tf_op jit(solution)/shard_map/all_to_all | solution.py:207
  235.3 98.7 %all-reduce.5.cloned.1.call-start = ((), (), s32[]{:S(2)}) async-start(), calls=%async_computation.3 | async-start | bytes 196608 | tf_op jit(solution)/shard_map/psum | solution.py:218
Sparse Core Ops, SparseCore 0:
  84.9 94.0 all-reduce.2
  244.8 89.1 all-reduce.4

commit v2 on v0

--- a/solution.py
+++ b/solution.py
@@ -51,6 +51,22 @@
         joined,
         first_sum * first_factor + second_sum * second_factor,
         first_acc * first_factor[..., None] + second_acc * second_factor[..., None],
+    )
+
+
+def merge_packed(first, second, width):
+    first_max, first_sum = first[..., width], first[..., width + 1]
+    second_max, second_sum = second[..., width], second[..., width + 1]
+    joined = jnp.maximum(first_max, second_max)
+    first_factor = jnp.exp(first_max - joined)
+    second_factor = jnp.exp(second_max - joined)
+    return jnp.concatenate(
+        [
+            first[..., :width] * first_factor[..., None] + second[..., :width] * second_factor[..., None],
+            joined[..., None],
+            (first_sum * first_factor + second_sum * second_factor)[..., None],
+        ],
+        axis=2,
     )
 
 
@@ -87,10 +103,15 @@
     local_pages = page_cache.shape[1]
     page_len = page_cache.shape[2]
     scaling = 1.0 / math.sqrt(head_dim)
-    all_heads = gathered_copies(queries, "head", 1)
-    kv_local = kv_index % (kv_heads // sect_size)
-    group_query = lax.dynamic_slice_in_dim(all_heads, kv_local * head_dim, head_dim, 2)
-    heads_dev = all_heads.shape[1] // group_size
+    kv_per_sect = kv_heads // sect_size
+    per_target = [
+        queries[..., (target * kv_per_sect // head_size) * head_dim :][..., :head_dim]
+        for target in range(head_size)
+    ]
+    group_query = in_order(
+        lax.all_to_all(jnp.stack(per_target), "head", split_axis=0, concat_axis=0, tiled=True), 1
+    )
+    heads_dev = group_query.shape[1] // group_size
     block_cols = heads_dev * head_dim
     chosen = lax.dynamic_index_in_dim(page_ids, kv_index, 1, keepdims=False)
     leading_page = quarter * local_pages
@@ -137,30 +158,32 @@
     weighted = weighted + fresh_weight.astype(jnp.bfloat16).astype(jnp.float32)[
         ..., None
     ] * newest_entry[:, None, head_dim:].astype(jnp.float32)
-    partial_value = (running_max, running_sum, weighted)
+    packed = jnp.concatenate([weighted, running_max[..., None], running_sum[..., None]], axis=2)
     bit_count = group_size.bit_length() - 1
     for bit_index in reversed(range(bit_count)):
-        half_heads = partial_value[0].shape[1] // 2
+        half_heads = packed.shape[1] // 2
         keep_half = quarter >> bit_index & 1
-        kept = head_slice(partial_value, keep_half * half_heads, half_heads)
-        sent = head_slice(partial_value, (1 - keep_half) * half_heads, half_heads)
+        kept = lax.dynamic_slice_in_dim(packed, keep_half * half_heads, half_heads, 1)
+        sent = lax.dynamic_slice_in_dim(packed, (1 - keep_half) * half_heads, half_heads, 1)
         partner = from_partner(sent, "head", bit_index)
-        partial_value = merge_pair(kept, partner)
+        packed = merge_packed(kept, partner, head_dim)
     attention = (
-        (partial_value[2] / partial_value[1][..., None])
+        (packed[..., :head_dim] / packed[..., head_dim + 1 :])
         .reshape(seq_count, block_cols)
         .astype(jnp.bfloat16)
     )
-    head_terms = jnp.dot(
-        gathered_copies(attention, "batch", 0), out_weight, preferred_element_type=jnp.float32
-    )
+    cols_dev = residual.shape[1]
+    gain_row = jnp.zeros((1, block_cols), jnp.float32).at[0, :cols_dev].set(norm_gain)
+    carried = gathered_copies(
+        jnp.concatenate([attention.astype(jnp.float32), gain_row], axis=0), "batch", 0
+    ).reshape(lax.axis_size("batch"), seq_count + 1, block_cols)
+    all_attention = carried[:, :seq_count].reshape(-1, block_cols).astype(jnp.bfloat16)
+    full_gain = carried[:, seq_count, :cols_dev].reshape(-1)
+    head_terms = jnp.dot(all_attention, out_weight, preferred_element_type=jnp.float32)
     projected = taken_together(head_terms.astype(jnp.bfloat16), ("sect", "head")).astype(
         jnp.float32
     )
     hidden_state = residual.astype(jnp.float32) + projected
-    squares = of_everyone(jnp.sum(hidden_state * hidden_state, axis=1), "batch")
-    inverse = lax.rsqrt(squares / D + NORM_EPS)
-    normed = (hidden_state * inverse[:, None] * norm_gain[None, :]).astype(jnp.bfloat16)
     token_count, top_count = expert_ids.shape
     capacity = 2 * token_count * top_count // EXPERTS
     pair_local = gate_up_weight.shape[0]
@@ -184,17 +207,21 @@
         == jnp.arange(slot_total, dtype=jnp.int32)[:, None, None]
     )
     selector_full = (
-        jnp.any(matches, axis=2).astype(jnp.bfloat16).reshape(batch_size, 2, slot_dev, token_count)
+        jnp.any(matches, axis=2).astype(jnp.float32).reshape(batch_size, 2, slot_dev, token_count)
     )
     selector = lax.dynamic_index_in_dim(selector_full, sub_half, 1, keepdims=False).reshape(
         send_count, token_count
     )
     coefficient = route_weight / jnp.sum(route_weight, axis=1, keepdims=True)
     combine_full = jnp.sum(jnp.where(matches, coefficient[None, :, :], 0.0), axis=2).T
-    cols_dev = normed.shape[1]
-    outgoing = jnp.dot(selector, normed, preferred_element_type=jnp.float32).astype(jnp.bfloat16)
+    outgoing = jnp.dot(
+        selector, hidden_state, precision=lax.Precision.HIGHEST, preferred_element_type=jnp.float32
+    )
     outgoing = outgoing.reshape(batch_size, pair_local, capacity, cols_dev)
-    arrived = lax.all_to_all(outgoing, "batch", split_axis=0, concat_axis=3, tiled=True)[0]
+    rows = lax.all_to_all(outgoing, "batch", split_axis=0, concat_axis=3, tiled=True)[0]
+    squares = jnp.sum(rows * rows, axis=2)
+    inverse = lax.rsqrt(squares / D + NORM_EPS)
+    arrived = (rows * inverse[..., None] * full_gain[None, None, :]).astype(jnp.bfloat16)
     mixture = jnp.einsum(
         "ecd,edgf->ecgf", arrived, gate_up_weight, preferred_element_type=jnp.float32
     )

time: 141 us -> 148 us (1.050)
  local copies, waits for them, and re-layouts: 16.2 us -> 27.2 us
  starting transfers between devices: 43.2 us -> 34.6 us
  other arithmetic: 8.35 us -> 11.3 us
  waiting for transfers between devices: 43.7 us -> 45.5 us
    all_to_all x4 -> x2, starting transfers between devices: 25.3 us -> 13.7 us  [copy_for_each(): return lax.all_to_all(copies, axis, split_axis=0, concat_axis=0, tiled=True)]
    unnamed x18 -> x32, local copies, waits for them, and re-layouts: 0.14 us -> 10.1 us
    all_to_all x4 -> x2, waiting for transfers between devices: 28.9 us -> 21.6 us  [copy_for_each(): return lax.all_to_all(copies, axis, split_axis=0, concat_axis=0, tiled=True)]
    all_to_all x0 -> x1, starting transfers between devices: none -> 6.93 us  [on_device(): lax.all_to_all(jnp.stack(per_target), 'head', split_axis=0, concat_axis=0...]
    ppermute x6 -> x2, starting transfers between devices: 7.76 us -> 2.07 us  [from_partner(): lax.ppermute(shard, axis, [(i, i ^ 1 << distance) for i in range(lax.axis...]
    ppermute x6 -> x2, waiting for transfers between devices: 4.82 us -> 9.14 us  [from_partner(): lax.ppermute(shard, axis, [(i, i ^ 1 << distance) for i in range(lax.axis...]
    convert_element_type x0 -> x6, local copies, waits for them, and re-layouts: none -> 2.74 us  [the longest x2 2.4 us: on_device(): (rows * inverse[..., None] * full_gain[None, None, :]).astype(jnp.bfloat16)]
    all_to_all x0 -> x1, waiting for transfers between devices: none -> 2.19 us  [on_device(): lax.all_to_all(jnp.stack(per_target), 'head', split_axis=0, concat_axis=0...]
  transfers between devices with their start and end apart: 12 -> 7, of which waited for: 10 -> 7; matrix products, arithmetic and copies ran while one was open for 12% -> 12% of each run, Pallas kernels for 0% -> 0%
where the time goes in v2:
time: 148 us; the launch traced here: 146 us
  waiting for transfers between devices  45.5 us (31%)
  starting transfers between devices  34.6 us (23%)
  local copies, waits for them, and re-layouts  27.2 us (18%)
  blocking collectives  18.8 us (13%)
  other arithmetic  11.3 us (8%)
  matrix products  8.28 us (6%)
    all_to_all x2, waiting for transfers between devices, copy_for_each(): return lax.all_to_all(copies, axis, split_axis=0, concat_axis=0, tiled=True)  21.6 us
    all_to_all x1, blocking collectives, copy_for_each(): return lax.all_to_all(copies, axis, split_axis=0, concat_axis=0, tiled=True)  18.8 us
    all_to_all x2, starting transfers between devices, copy_for_each(): return lax.all_to_all(copies, axis, split_axis=0, concat_axis=0, tiled=True)  13.7 us
    unnamed x32, local copies, waits for them, and re-layouts  10.1 us
    ppermute x2, waiting for transfers between devices, from_partner(): lax.ppermute(shard, axis, [(i, i ^ 1 << distance) for i in range(lax.axis...  9.14 us
    all_to_all x1, waiting for transfers between devices, on_device(): lax.all_to_all(leaving.astype(jnp.bfloat16), 'batch', split_axis=2, conca...  6.93 us
    all_to_all x1, starting transfers between devices, on_device(): lax.all_to_all(jnp.stack(per_target), 'head', split_axis=0, concat_axis=0...  6.93 us
    all_to_all x1, starting transfers between devices, on_device(): lax.all_to_all(outgoing, 'batch', split_axis=0, concat_axis=3, tiled=True)  6.27 us
  transfers between devices with their start and end apart: 7, of which 7 were waited for; matrix products, arithmetic and copies ran while one was open for 12% of the time, Pallas kernels for 0%

profile of v2, /device:TPU:32, one launch (start us, length us, event | category | flops | bytes accessed | tf_op | source)
XLA Modules:
  0.0 146.0 jit_solution(6288068802513821512)
XLA Ops:
  0.0 1.3 constant_dynamic-update-slice_fusion.7
  1.3 1.3 constant_dynamic-update-slice_fusion.6
  2.6 1.3 constant_dynamic-update-slice_fusion.5
  3.8 1.3 constant_dynamic-update-slice_fusion.4
  5.1 1.3 constant_dynamic-update-slice_fusion.3
  6.4 1.3 constant_dynamic-update-slice_fusion.2
  7.6 1.3 constant_dynamic-update-slice_fusion.1
  8.9 1.3 constant_dynamic-update-slice_fusion
  10.2 6.9 %all-to-all-start = ((bf16[8,6,2,128]{3,2,1,0:T(2,128)(2,1)}), bf16[8,6,2,128]{3,2,1,0:T(2,128)(2,1)S(1)}, u32[]{:S(2)}, u32[]{:S(2)}) async-start(bf16[8,6,2,128]{3,2,1,0:T(2,128)(2,1)} %constant_dynamic-update-slice_fusion), calls=%async_computation | async-start | bytes 49152 | tf_op jit(solution)/shard_map/all_to_all | solution.py:112
  18.4 3.2 %fusion.58 = (bf16[6,16,64,128]{3,2,1,0:T(8,128)(2,1)S(1)}, bf16[6,16,64,128]{3,2,1,0:T(8,128)(2,1)S(1)}) fusion(bf16[6,16,64,256]{3,2,1,0:T(8,128)(2,1)} %param.16), kind=kLoop, calls=%fused_computation.130 | loop fusion | bytes 6291456 | tf_op jit(solution)/shard_map/slice | solution.py:130
  22.6 2.2 %all-to-all-done = bf16[8,6,2,128]{3,2,1,0:T(2,128)(2,1)S(1)} async-done(((bf16[8,6,2,128]{3,2,1,0:T(2,128)(2,1)}), bf16[8,6,2,128]{3,2,1,0:T(2,128)(2,1)S(1)}, u32[]{:S(2)}, u32[]{:S(2)}) %all-to-all-start) | async-done | bytes 24608 | tf_op jit(solution)/shard_map/all_to_all | solution.py:112
  28.5 3.3 %collective-permute-done = f32[6,8,130]{2,1,0:T(8,128)S(1)} collective-permute-done((f32[6,8,130]{2,1,0:T(8,128)S(1)}, f32[6,8,130]{2,1,0:T(8,128)S(1)}, u32[]{:S(2)}, u32[]{:S(2)}) %collective-permute-start) | collective-permute-done | bytes 24992 | tf_op jit(solution)/shard_map/ppermute | solution.py:33
  32.8 1.4 collective-permute-start.1
  34.9 5.9 %collective-permute-done.1 = f32[6,4,130]{0,1,2:T(4,128)S(1)} collective-permute-done((f32[6,4,130]{0,1,2:T(4,128)S(1)}, f32[6,4,130]{0,1,2:T(4,128)S(1)}, u32[]{:S(2)}, u32[]{:S(2)}) %collective-permute-start.1) | collective-permute-done | bytes 12512 | tf_op jit(solution)/shard_map/ppermute | solution.py:33
  41.8 8.6 %all-to-all-start.1 = ((f32[16,7,512]{2,1,0:T(8,128)}), f32[16,7,512]{2,1,0:T(8,128)S(1)}, u32[]{:S(2)}, u32[]{:S(2)}) async-start(f32[16,7,512]{2,1,0:T(8,128)} %broadcast_in_dim.81), calls=%async_computation.1 | async-start | bytes 524288 | tf_op jit(solution)/shard_map/all_to_all | solution.py:18
  50.7 9.3 %all-to-all-done.1 = f32[16,7,512]{2,1,0:T(8,128)S(1)} async-done(((f32[16,7,512]{2,1,0:T(8,128)}), f32[16,7,512]{2,1,0:T(8,128)S(1)}, u32[]{:S(2)}, u32[]{:S(2)}) %all-to-all-start.1) | async-done | bytes 229408 | tf_op jit(solution)/shard_map/all_to_all | solution.py:18
  61.2 5.1 %all-to-all-start.2 = ((bf16[16,96,256]{2,1,0:T(8,128)(2,1)}), bf16[16,96,256]{2,1,0:T(8,128)(2,1)S(1)}, u32[]{:S(2)}, u32[]{:S(2)}) async-start(bf16[16,96,256]{2,1,0:T(8,128)(2,1)} %broadcast_in_dim.82), calls=%async_computation.2 | async-start | bytes 1572864 | tf_op jit(solution)/shard_map/all_to_all | solution.py:18
  66.4 1.8 %reduce-window.6 = s32[64,6,128]{2,0,1:T(8,128)S(1)} reduce-window(s32[64,6,128]{2,0,1:T(8,128)S(1)} %fusion.24, s32[]{:T(128)} %constant.140.clone.1), window={size=1x1x128 pad=0_0x0_0x127_0}, to_apply=%region_5.6 | reduce-window | flops 6242304 | bytes 393220 | tf_op jit(solution)/shard_map/reduce-window
  69.8 12.3 %all-to-all-done.2 = bf16[16,96,256]{2,1,0:T(8,128)(2,1)S(1)} async-done(((bf16[16,96,256]{2,1,0:T(8,128)(2,1)}), bf16[16,96,256]{2,1,0:T(8,128)(2,1)S(1)}, u32[]{:S(2)}, u32[]{:S(2)}) %all-to-all-start.2) | async-done | bytes 786464 | tf_op jit(solution)/shard_map/all_to_all | solution.py:18
  82.2 1.1 convolution_bitcast_fusion
  83.2 6.3 %all-to-all-start.3 = ((f32[16,1,24,256]{3,2,1,0:T(8,128)}), f32[16,1,24,256]{3,2,1,0:T(8,128)}, u32[]{:S(2)}, u32[]{:S(2)}) async-start(f32[16,1,24,256]{3,2,1,0:T(8,128)} %convolution_bitcast_fusion), calls=%async_computation.3 | async-start | bytes 786432 | tf_op jit(solution)/shard_map/all_to_all | solution.py:221
  89.5 3.4 %copy.248 = bf16[4096,384]{1,0:T(8,128)(2,1)S(1)} copy(bf16[4096,384]{0,1:T(8,128)(2,1)} %bitcast.139) | data formatting | bytes 6291456 | tf_op jit(solution)/shard_map/ecf,efd->ecd/dot_general | solution.py:229
  93.0 1.3 reduce_sum.69
  95.8 5.6 %all-to-all-done.3 = f32[16,1,24,256]{3,2,1,0:T(8,128)} async-done(((f32[16,1,24,256]{3,2,1,0:T(8,128)}), f32[16,1,24,256]{3,2,1,0:T(8,128)}, u32[]{:S(2)}, u32[]{:S(2)}) %all-to-all-start.3) | async-done | bytes 393248 | tf_op jit(solution)/shard_map/all_to_all | solution.py:221
  101.4 1.1 fusion.8
  102.6 1.1 fusion.18
  104.4 1.7 %reshape.269 = bf16[24,4096,1]{1,0,2:T(8,128)(2,1)} reshape(bf16[1,1,24,16,256]{4,3,2,1,0:T(8,128)(2,1)} %copy.240) | data formatting | bytes 393216 | tf_op jit(solution)/shard_map/convert_element_type | solution.py:224
  106.1 3.8 %fusion.5 = f32[1,24,2,384]{3,1,2,0:T(8,128)S(1)} fusion(bf16[24,4096,1]{1,0,2:T(8,128)(2,1)} %reshape.269, bf16[4096,2,384]{2,1,0:T(2,128)(2,1)} %bitcast.156), kind=kOutput, calls=%fused_computation.12 | convolution fusion | flops 150994944 | bytes 6561792 | tf_op jit(solution)/shard_map/ecd,edgf->ecgf/dot_general | solution.py:225
  109.9 1.9 %fusion.4 = bf16[1,24,16,256]{3,1,0,2:T(8,128)(2,1)} fusion(bf16[16,256,384]{2,1,0:T(8,128)(2,1)S(1)} %bitcast.136, f32[1,24,2,384]{3,1,2,0:T(8,128)S(1)} %fusion.5), kind=kOutput, calls=%fused_computation.11 | convolution fusion | flops 75651072 | bytes 3416064 | tf_op jit(solution)/shard_map/ecf,efd->ecd/dot_general | solution.py:229
  111.8 5.6 %all-to-all-start.4 = ((bf16[1,24,16,256]{3,1,0,2:T(8,128)(2,1)}), bf16[1,24,16,256]{3,1,0,2:T(8,128)(2,1)S(1)}, u32[]{:S(2)}, u32[]{:S(2)}) async-start(bf16[1,24,16,256]{3,1,0,2:T(8,128)(2,1)} %fusion.4), calls=%async_computation.4 | async-start | bytes 393216 | tf_op jit(solution)/shard_map/all_to_all | solution.py:234
  119.2 6.9 %all-to-all-done.4 = bf16[1,24,16,256]{3,1,0,2:T(8,128)(2,1)S(1)} async-done(((bf16[1,24,16,256]{3,1,0,2:T(8,128)(2,1)}), bf16[1,24,16,256]{3,1,0,2:T(8,128)(2,1)S(1)}, u32[]{:S(2)}, u32[]{:S(2)}) %all-to-all-start.4) | async-done | bytes 196640 | tf_op jit(solution)/shard_map/all_to_all | solution.py:234
  126.5 18.8 %all_to_all.47 = bf16[16,96,256]{2,1,0:T(8,128)(2,1)S(1)} all-to-all(bf16[16,96,256]{2,1,0:T(8,128)(2,1)S(1)} %broadcast_in_dim.85), channel_id=1, replica_groups=mesh['sect'=2,'batch'=16,'head'=8] {'sect','head'}, dimensions={0} | all-to-all | bytes 1572864 | tf_op jit(solution)/shard_map/all_to_all | solution.py:18
  (95 shorter events, 16.7 us)
Async XLA Ops:
  0.0 60.1 %copy-start = (bf16[512,256]{1,0:T(8,128)(2,1)S(1)}, bf16[512,256]{1,0:T(8,128)(2,1)}, u32[]{:S(2)}) copy-start(bf16[512,256]{1,0:T(8,128)(2,1)} %param.19) | copy-start | bytes 786436
  10.2 14.6 %all-to-all-start = ((bf16[8,6,2,128]{3,2,1,0:T(2,128)(2,1)}), bf16[8,6,2,128]{3,2,1,0:T(2,128)(2,1)S(1)}, u32[]{:S(2)}, u32[]{:S(2)}) async-start(bf16[8,6,2,128]{3,2,1,0:T(2,128)(2,1)} %constant_dynamic-update-slice_fusion), calls=%async_computation | async-start | bytes 49152 | tf_op jit(solution)/shard_map/all_to_all | solution.py:112
  18.4 3.2 %copy-start.5 = (bf16[6,4,256]{2,1,0:T(4,128)(2,1)S(1)}, bf16[6,4,256]{2,1,0:T(4,128)(2,1)}, u32[]{:S(2)}) copy-start(bf16[6,4,256]{2,1,0:T(4,128)(2,1)} %param.15) | copy-start | bytes 36868
  18.4 3.3 %copy-start.7 = (s32[6]{0:T(128)S(1)}, s32[6]{0:T(128)}, u32[]{:S(2)}) copy-start(s32[6]{0:T(128)} %param.17) | copy-start | bytes 76
  27.6 4.2 %collective-permute-start = (f32[6,8,130]{2,1,0:T(8,128)S(1)}, f32[6,8,130]{2,1,0:T(8,128)S(1)}, u32[]{:S(2)}, u32[]{:S(2)}) collective-permute-start(f32[6,8,130]{2,1,0:T(8,128)S(1)} %copy.217), channel_id=1, source_target_pairs={{0,2},{1,3},{2,0},{3,1},{4,6},{5,7},{6,4},{7,5},{8,10},{9,11},{10,... | collective-permute-start | bytes 74888 | tf_op jit(solution)/shard_map/ppermute | solution.py:33
  28.3 5.9 %copy-start.6 = (f32[256]{0:T(256)S(1)}, f32[256]{0:T(256)}, u32[]{:S(2)}) copy-start(f32[256]{0:T(256)} %param.21) | copy-start | bytes 3076
  32.7 17.7 %copy-start.4 = (s32[96,8]{0,1:T(8,128)S(1)}, s32[96,8]{0,1:T(8,128)}, u32[]{:S(2)}) copy-start(s32[96,8]{0,1:T(8,128)} %param.22) | copy-start | bytes 9220
  32.8 8.0 %collective-permute-start.1 = (f32[6,4,130]{0,1,2:T(4,128)S(1)}, f32[6,4,130]{0,1,2:T(4,128)S(1)}, u32[]{:S(2)}, u32[]{:S(2)}) collective-permute-start(f32[6,4,130]{0,1,2:T(4,128)S(1)} %constant_dynamic-slice_fusion.3), channel_id=1, source_target_pairs={{0,1},{1,0},{2,3},{3,2},{4,5},{5,4},{6,7},{7,6},{8,9},{9,8},{10,11... | collective-permute-start | bytes 37448 | tf_op jit(solution)/shard_map/ppermute | solution.py:33
  41.8 18.2 %all-to-all-start.1 = ((f32[16,7,512]{2,1,0:T(8,128)}), f32[16,7,512]{2,1,0:T(8,128)S(1)}, u32[]{:S(2)}, u32[]{:S(2)}) async-start(f32[16,7,512]{2,1,0:T(8,128)} %broadcast_in_dim.81), calls=%async_computation.1 | async-start | bytes 524288 | tf_op jit(solution)/shard_map/all_to_all | solution.py:18
  60.0 1.2 copy-start.1
  61.2 20.8 %all-to-all-start.2 = ((bf16[16,96,256]{2,1,0:T(8,128)(2,1)}), bf16[16,96,256]{2,1,0:T(8,128)(2,1)S(1)}, u32[]{:S(2)}, u32[]{:S(2)}) async-start(bf16[16,96,256]{2,1,0:T(8,128)(2,1)} %broadcast_in_dim.82), calls=%async_computation.2 | async-start | bytes 1572864 | tf_op jit(solution)/shard_map/all_to_all | solution.py:18
  66.4 15.8 %copy-start.2 = (bf16[96,256]{1,0:T(8,128)(2,1)S(1)}, bf16[96,256]{1,0:T(8,128)(2,1)}, u32[]{:S(2)}) copy-start(bf16[96,256]{1,0:T(8,128)(2,1)} %param.20) | copy-start | bytes 147460
  83.2 18.2 %all-to-all-start.3 = ((f32[16,1,24,256]{3,2,1,0:T(8,128)}), f32[16,1,24,256]{3,2,1,0:T(8,128)}, u32[]{:S(2)}, u32[]{:S(2)}) async-start(f32[16,1,24,256]{3,2,1,0:T(8,128)} %convolution_bitcast_fusion), calls=%async_computation.3 | async-start | bytes 786432 | tf_op jit(solution)/shard_map/all_to_all | solution.py:221
  111.8 14.3 %all-to-all-start.4 = ((bf16[1,24,16,256]{3,1,0,2:T(8,128)(2,1)}), bf16[1,24,16,256]{3,1,0,2:T(8,128)(2,1)S(1)}, u32[]{:S(2)}, u32[]{:S(2)}) async-start(bf16[1,24,16,256]{3,1,0,2:T(8,128)(2,1)} %fusion.4), calls=%async_computation.4 | async-start | bytes 393216 | tf_op jit(solution)/shard_map/all_to_all | solution.py:234
  126.4 19.0 %copy-start.3 = (bf16[96,256]{1,0:T(8,128)(2,1)S(1)}, bf16[96,256]{1,0:T(8,128)(2,1)}, u32[]{:S(2)}) copy-start(bf16[96,256]{1,0:T(8,128)(2,1)} %param.20) | copy-start | bytes 147460

commit v3 on v2

--- a/solution.py
+++ b/solution.py
@@ -52,6 +52,19 @@
         first_sum * first_factor + second_sum * second_factor,
         first_acc * first_factor[..., None] + second_acc * second_factor[..., None],
     )
+
+
+def split_three(value):
+    high = lax.reduce_precision(value, exponent_bits=8, mantissa_bits=7)
+    rest = value - high
+    middle = lax.reduce_precision(rest, exponent_bits=8, mantissa_bits=7)
+    low = rest - middle
+    return jnp.stack([high, middle, low]).astype(jnp.bfloat16)
+
+
+def join_three(parts):
+    parts = parts.astype(jnp.float32)
+    return (parts[:, 0] + parts[:, 1] + parts[:, 2]).reshape(-1)
 
 
 def merge_packed(first, second, width):
@@ -104,12 +117,12 @@
     page_len = page_cache.shape[2]
     scaling = 1.0 / math.sqrt(head_dim)
     kv_per_sect = kv_heads // sect_size
-    per_target = [
-        queries[..., (target * kv_per_sect // head_size) * head_dim :][..., :head_dim]
-        for target in range(head_size)
-    ]
+    by_kv = jnp.moveaxis(queries.reshape(*queries.shape[:2], kv_per_sect, head_dim), 2, 0)
+    per_target = jnp.broadcast_to(
+        by_kv[:, None], (kv_per_sect, head_size // kv_per_sect, *by_kv.shape[1:])
+    ).reshape(head_size, *by_kv.shape[1:])
     group_query = in_order(
-        lax.all_to_all(jnp.stack(per_target), "head", split_axis=0, concat_axis=0, tiled=True), 1
+        lax.all_to_all(per_target, "head", split_axis=0, concat_axis=0, tiled=True), 1
     )
     heads_dev = group_query.shape[1] // group_size
     block_cols = heads_dev * head_dim
@@ -173,12 +186,15 @@
         .astype(jnp.bfloat16)
     )
     cols_dev = residual.shape[1]
-    gain_row = jnp.zeros((1, block_cols), jnp.float32).at[0, :cols_dev].set(norm_gain)
+    gain_parts = split_three(norm_gain)
+    gain_rows = -(-gain_parts.size // block_cols)
+    gain_block = jnp.pad(gain_parts.reshape(-1), (0, gain_rows * block_cols - gain_parts.size))
     carried = gathered_copies(
-        jnp.concatenate([attention.astype(jnp.float32), gain_row], axis=0), "batch", 0
-    ).reshape(lax.axis_size("batch"), seq_count + 1, block_cols)
-    all_attention = carried[:, :seq_count].reshape(-1, block_cols).astype(jnp.bfloat16)
-    full_gain = carried[:, seq_count, :cols_dev].reshape(-1)
+        jnp.concatenate([attention, gain_block.reshape(gain_rows, block_cols)], axis=0), "batch", 0
+    ).reshape(lax.axis_size("batch"), seq_count + gain_rows, block_cols)
+    all_attention = carried[:, :seq_count].reshape(-1, block_cols)
+    got_parts = carried[:, seq_count:].reshape(lax.axis_size("batch"), -1)[:, : gain_parts.size]
+    full_gain = join_three(got_parts.reshape(-1, 3, cols_dev))
     head_terms = jnp.dot(all_attention, out_weight, preferred_element_type=jnp.float32)
     projected = taken_together(head_terms.astype(jnp.bfloat16), ("sect", "head")).astype(
         jnp.float32
@@ -207,7 +223,7 @@
         == jnp.arange(slot_total, dtype=jnp.int32)[:, None, None]
     )
     selector_full = (
-        jnp.any(matches, axis=2).astype(jnp.float32).reshape(batch_size, 2, slot_dev, token_count)
+        jnp.any(matches, axis=2).astype(jnp.bfloat16).reshape(batch_size, 2, slot_dev, token_count)
     )
     selector = lax.dynamic_index_in_dim(selector_full, sub_half, 1, keepdims=False).reshape(
         send_count, token_count
@@ -215,10 +231,11 @@
     coefficient = route_weight / jnp.sum(route_weight, axis=1, keepdims=True)
     combine_full = jnp.sum(jnp.where(matches, coefficient[None, :, :], 0.0), axis=2).T
     outgoing = jnp.dot(
-        selector, hidden_state, precision=lax.Precision.HIGHEST, preferred_element_type=jnp.float32
-    )
+        selector, hidden_state.astype(jnp.bfloat16), preferred_element_type=jnp.float32
+    ).astype(jnp.bfloat16)
     outgoing = outgoing.reshape(batch_size, pair_local, capacity, cols_dev)
     rows = lax.all_to_all(outgoing, "batch", split_axis=0, concat_axis=3, tiled=True)[0]
+    rows = rows.astype(jnp.float32)
     squares = jnp.sum(rows * rows, axis=2)
     inverse = lax.rsqrt(squares / D + NORM_EPS)
     arrived = (rows * inverse[..., None] * full_gain[None, None, :]).astype(jnp.bfloat16)

time: 148 us -> 134 us (0.905)
  waiting for transfers between devices: 45.5 us -> 36.6 us
  local copies, waits for them, and re-layouts: 27.2 us -> 21.8 us
  starting transfers between devices: 34.6 us -> 31.7 us
  other arithmetic: 11.3 us -> 13.2 us
    all_to_all x2, waiting for transfers between devices: 21.6 us -> 12.1 us  [copy_for_each(): return lax.all_to_all(copies, axis, split_axis=0, concat_axis=0, tiled=True)]
    unnamed x32 -> x26, local copies, waits for them, and re-layouts: 10.1 us -> 1.79 us
    another operation x2 -> x3, local copies, waits for them, and re-layouts: 1.54 us -> 0.01 us  [split_three(): return jnp.stack([high, middle, low]).astype(jnp.bfloat16)]
  transfers between devices with their start and end apart: 7 -> 7, of which waited for: 7 -> 7; matrix products, arithmetic and copies ran while one was open for 12% -> 17% of each run, Pallas kernels for 0% -> 0%
where the time goes in v3:
time: 134 us; the launch traced here: 132 us
  waiting for transfers between devices  36.6 us (27%)
  starting transfers between devices  31.7 us (24%)
  local copies, waits for them, and re-layouts  21.8 us (16%)
  blocking collectives  19 us (14%)
  other arithmetic  13.2 us (10%)
  matrix products  8.91 us (7%)
    all_to_all x1, blocking collectives, copy_for_each(): return lax.all_to_all(copies, axis, split_axis=0, concat_axis=0, tiled=True)  19 us
    all_to_all x2, starting transfers between devices, copy_for_each(): return lax.all_to_all(copies, axis, split_axis=0, concat_axis=0, tiled=True)  13.1 us
    all_to_all x2, waiting for transfers between devices, copy_for_each(): return lax.all_to_all(copies, axis, split_axis=0, concat_axis=0, tiled=True)  12.1 us
    ppermute x2, waiting for transfers between devices, from_partner(): lax.ppermute(shard, axis, [(i, i ^ 1 << distance) for i in range(lax.axis...  10.4 us
    all_to_all x1, starting transfers between devices, on_device(): lax.all_to_all(per_target, 'head', split_axis=0, concat_axis=0, tiled=True)  6.93 us
    all_to_all x1, waiting for transfers between devices, on_device(): lax.all_to_all(leaving.astype(jnp.bfloat16), 'batch', split_axis=2, conca...  6.87 us
    all_to_all x1, starting transfers between devices, on_device(): lax.all_to_all(outgoing, 'batch', split_axis=0, concat_axis=3, tiled=True)  5.48 us
    all_to_all x1, starting transfers between devices, on_device(): lax.all_to_all(leaving.astype(jnp.bfloat16), 'batch', split_axis=2, conca...  4.76 us
  transfers between devices with their start and end apart: 7, of which 7 were waited for; matrix products, arithmetic and copies ran while one was open for 17% of the time, Pallas kernels for 0%

profile of v3, /device:TPU:32, one launch (start us, length us, event | category | flops | bytes accessed | tf_op | source)
XLA Modules:
  0.0 131.6 jit_solution(11538781338931602056)
XLA Ops:
  1.4 6.9 %all-to-all-start = ((bf16[8,6,2,128]{3,2,1,0:T(2,128)(2,1)}), bf16[8,6,2,128]{3,2,1,0:T(2,128)(2,1)S(1)}, u32[]{:S(2)}, u32[]{:S(2)}) async-start(bf16[8,6,2,128]{3,2,1,0:T(2,128)(2,1)} %bitcast.2), calls=%async_computation | async-start | bytes 49152 | tf_op jit(solution)/shard_map/all_to_all | solution.py:125
  9.6 3.2 %fusion.56 = (bf16[6,16,64,128]{3,2,1,0:T(8,128)(2,1)S(1)}, bf16[6,16,64,128]{3,2,1,0:T(8,128)(2,1)S(1)}) fusion(bf16[6,16,64,256]{3,2,1,0:T(8,128)(2,1)} %param.14), kind=kLoop, calls=%fused_computation.124 | loop fusion | bytes 6291456 | tf_op jit(solution)/shard_map/slice | solution.py:143
  13.2 2.8 %all-to-all-done = bf16[8,6,2,128]{3,2,1,0:T(2,128)(2,1)S(1)} async-done(((bf16[8,6,2,128]{3,2,1,0:T(2,128)(2,1)}), bf16[8,6,2,128]{3,2,1,0:T(2,128)(2,1)S(1)}, u32[]{:S(2)}, u32[]{:S(2)}) %all-to-all-start) | async-done | bytes 24608 | tf_op jit(solution)/shard_map/all_to_all | solution.py:125
  19.7 3.3 %collective-permute-done = f32[6,8,130]{2,1,0:T(8,128)S(1)} collective-permute-done((f32[6,8,130]{2,1,0:T(8,128)S(1)}, f32[6,8,130]{2,1,0:T(8,128)S(1)}, u32[]{:S(2)}, u32[]{:S(2)}) %collective-permute-start) | collective-permute-done | bytes 24992 | tf_op jit(solution)/shard_map/ppermute | solution.py:33
  24.0 0.8 collective-permute-start.1
  24.8 7.2 %collective-permute-done.1 = f32[6,4,130]{0,1,2:T(4,128)S(1)} collective-permute-done((f32[6,4,130]{0,1,2:T(4,128)S(1)}, f32[6,4,130]{0,1,2:T(4,128)S(1)}, u32[]{:S(2)}, u32[]{:S(2)}) %collective-permute-start.1) | collective-permute-done | bytes 12512 | tf_op jit(solution)/shard_map/ppermute | solution.py:33
  33.0 8.6 %all-to-all-start.1 = ((bf16[16,8,512]{2,1,0:T(8,128)(2,1)}), bf16[16,8,512]{2,1,0:T(8,128)(2,1)S(1)}, u32[]{:S(2)}, u32[]{:S(2)}) async-start(bf16[16,8,512]{2,1,0:T(8,128)(2,1)} %broadcast_in_dim.87), calls=%async_computation.1 | async-start | bytes 262144 | tf_op jit(solution)/shard_map/all_to_all | solution.py:18
  41.7 7.2 %all-to-all-done.1 = bf16[16,8,512]{2,1,0:T(8,128)(2,1)S(1)} async-done(((bf16[16,8,512]{2,1,0:T(8,128)(2,1)}), bf16[16,8,512]{2,1,0:T(8,128)(2,1)S(1)}, u32[]{:S(2)}, u32[]{:S(2)}) %all-to-all-start.1) | async-done | bytes 131104 | tf_op jit(solution)/shard_map/all_to_all | solution.py:18
  49.2 1.0 broadcast_in_dim.88
  50.1 4.5 %all-to-all-start.2 = ((bf16[16,96,256]{2,1,0:T(8,128)(2,1)}), bf16[16,96,256]{2,1,0:T(8,128)(2,1)}, u32[]{:S(2)}, u32[]{:S(2)}) async-start(bf16[16,96,256]{2,1,0:T(8,128)(2,1)} %broadcast_in_dim.88), calls=%async_computation.2 | async-start | bytes 1572864 | tf_op jit(solution)/shard_map/all_to_all | solution.py:18
  54.8 1.8 %reduce-window.6 = s32[64,6,128]{2,0,1:T(8,128)S(1)} reduce-window(s32[64,6,128]{2,0,1:T(8,128)S(1)} %fusion.24, s32[]{:T(128)} %constant.114.clone.1), window={size=1x1x128 pad=0_0x0_0x127_0}, to_apply=%region_4.5 | reduce-window | flops 6242304 | bytes 393220 | tf_op jit(solution)/shard_map/reduce-window
  58.0 0.8 copy.269
  58.8 3.5 %copy.279 = bf16[4096,384]{1,0:T(8,128)(2,1)S(1)} copy(bf16[4096,384]{0,1:T(8,128)(2,1)} %bitcast.121) | data formatting | bytes 6291456 | tf_op jit(solution)/shard_map/ecf,efd->ecd/dot_general | solution.py:246
  62.3 1.3 reduce_sum.69
  64.2 0.9 slice.114
  65.8 5.0 %all-to-all-done.2 = bf16[16,96,256]{2,1,0:T(8,128)(2,1)} async-done(((bf16[16,96,256]{2,1,0:T(8,128)(2,1)}), bf16[16,96,256]{2,1,0:T(8,128)(2,1)}, u32[]{:S(2)}, u32[]{:S(2)}) %all-to-all-start.2) | async-done | bytes 786464 | tf_op jit(solution)/shard_map/all_to_all | solution.py:18
  70.7 1.2 convert_reduce_fusion.1
  72.0 1.7 %convolution_convert_fusion.1 = bf16[384,256]{1,0:T(8,128)(2,1)} fusion(pred[384,96]{1,0:T(8,128)(4,1)} %bitcast.129, f32[96,256]{1,0:T(8,128)S(1)} %convert_reduce_fusion.1, bf16[96,256]{1,0:T(8,128)(2,1)} %param.18), kind=kOutput, calls=%fused_computation.10 | convolution fusion | flops 19046400 | bytes 380928 | tf_op jit(solution)/shard_map/dot_general | solution.py:233
  73.7 5.5 %all-to-all-start.3 = ((bf16[16,1,24,256]{3,2,1,0:T(8,128)(2,1)}), bf16[16,1,24,256]{3,2,1,0:T(8,128)(2,1)}, u32[]{:S(2)}, u32[]{:S(2)}) async-start(bf16[16,1,24,256]{3,2,1,0:T(8,128)(2,1)} %bitcast.122), calls=%async_computation.3 | async-start | bytes 393216 | tf_op jit(solution)/shard_map/all_to_all | solution.py:237
  79.2 1.4 %slice_convert_fusion = f32[16,768]{1,0:T(8,128)} fusion(bf16[16,1024]{1,0:T(8,128)(2,1)} %bitcast.132), kind=kLoop, calls=%fused_computation.64 | loop fusion | flops 12288 | bytes 73728 | tf_op jit(solution)/shard_map/convert_element_type | solution.py:66
  80.5 1.4 %reshape.276 = f32[16,3,256]{2,1,0:T(4,128)} reshape(f32[16,768]{1,0:T(8,128)} %slice_convert_fusion) | data formatting | bytes 98304 | tf_op jit(solution)/shard_map/convert_element_type | solution.py:66
  82.0 1.0 slice_add_fusion
  83.6 4.3 %all-to-all-done.3 = bf16[16,1,24,256]{3,2,1,0:T(8,128)(2,1)} async-done(((bf16[16,1,24,256]{3,2,1,0:T(8,128)(2,1)}), bf16[16,1,24,256]{3,2,1,0:T(8,128)(2,1)}, u32[]{:S(2)}, u32[]{:S(2)}) %all-to-all-start.3) | async-done | bytes 196640 | tf_op jit(solution)/shard_map/all_to_all | solution.py:237
  87.8 1.1 fusion.8
  88.9 1.1 fusion.18
  90.7 1.7 %reshape.279 = bf16[24,4096,1]{1,0,2:T(8,128)(2,1)} reshape(bf16[1,1,24,16,256]{4,3,2,1,0:T(8,128)(2,1)} %copy.271) | data formatting | bytes 393216 | tf_op jit(solution)/shard_map/convert_element_type | solution.py:241
  92.4 3.8 %fusion.5 = f32[1,24,2,384]{3,1,2,0:T(8,128)S(1)} fusion(bf16[24,4096,1]{1,0,2:T(8,128)(2,1)} %reshape.279, bf16[4096,2,384]{2,1,0:T(2,128)(2,1)} %bitcast.143), kind=kOutput, calls=%fused_computation.12 | convolution fusion | flops 150994944 | bytes 6561792 | tf_op jit(solution)/shard_map/ecd,edgf->ecgf/dot_general | solution.py:242
  96.2 1.9 %fusion.4 = bf16[1,24,16,256]{3,1,0,2:T(8,128)(2,1)} fusion(bf16[16,256,384]{2,1,0:T(8,128)(2,1)S(1)} %bitcast.118, f32[1,24,2,384]{3,1,2,0:T(8,128)S(1)} %fusion.5), kind=kOutput, calls=%fused_computation.11 | convolution fusion | flops 75651072 | bytes 3416064 | tf_op jit(solution)/shard_map/ecf,efd->ecd/dot_general | solution.py:246
  98.1 4.8 %all-to-all-start.4 = ((bf16[1,24,16,256]{3,1,0,2:T(8,128)(2,1)}), bf16[1,24,16,256]{3,1,0,2:T(8,128)(2,1)S(1)}, u32[]{:S(2)}, u32[]{:S(2)}) async-start(bf16[1,24,16,256]{3,1,0,2:T(8,128)(2,1)} %fusion.4), calls=%async_computation.4 | async-start | bytes 393216 | tf_op jit(solution)/shard_map/all_to_all | solution.py:251
  103.7 0.8 select_reduce_fusion
  104.7 6.9 %all-to-all-done.4 = bf16[1,24,16,256]{3,1,0,2:T(8,128)(2,1)S(1)} async-done(((bf16[1,24,16,256]{3,1,0,2:T(8,128)(2,1)}), bf16[1,24,16,256]{3,1,0,2:T(8,128)(2,1)S(1)}, u32[]{:S(2)}, u32[]{:S(2)}) %all-to-all-start.4) | async-done | bytes 196640 | tf_op jit(solution)/shard_map/all_to_all | solution.py:251
  111.8 19.0 %all_to_all.44 = bf16[16,96,256]{2,1,0:T(8,128)(2,1)S(1)} all-to-all(bf16[16,96,256]{2,1,0:T(8,128)(2,1)S(1)} %broadcast_in_dim.91), channel_id=1, replica_groups=mesh['sect'=2,'batch'=16,'head'=8] {'sect','head'}, dimensions={0} | all-to-all | bytes 1572864 | tf_op jit(solution)/shard_map/all_to_all | solution.py:18
  (100 shorter events, 14.9 us)
Async XLA Ops:
  0.0 49.0 %copy-start = (bf16[512,256]{1,0:T(8,128)(2,1)S(1)}, bf16[512,256]{1,0:T(8,128)(2,1)}, u32[]{:S(2)}) copy-start(bf16[512,256]{1,0:T(8,128)(2,1)} %param.17) | copy-start | bytes 786436
  1.4 14.6 %all-to-all-start = ((bf16[8,6,2,128]{3,2,1,0:T(2,128)(2,1)}), bf16[8,6,2,128]{3,2,1,0:T(2,128)(2,1)S(1)}, u32[]{:S(2)}, u32[]{:S(2)}) async-start(bf16[8,6,2,128]{3,2,1,0:T(2,128)(2,1)} %bitcast.2), calls=%async_computation | async-start | bytes 49152 | tf_op jit(solution)/shard_map/all_to_all | solution.py:125
  9.6 3.2 %copy-start.5 = (bf16[6,4,256]{2,1,0:T(4,128)(2,1)S(1)}, bf16[6,4,256]{2,1,0:T(4,128)(2,1)}, u32[]{:S(2)}) copy-start(bf16[6,4,256]{2,1,0:T(4,128)(2,1)} %param.13) | copy-start | bytes 36868
  9.6 3.3 %copy-start.7 = (s32[6]{0:T(128)S(1)}, s32[6]{0:T(128)}, u32[]{:S(2)}) copy-start(s32[6]{0:T(128)} %param.15) | copy-start | bytes 76
  9.6 3.4 %copy-start.6 = (f32[256]{0:T(256)S(1)}, f32[256]{0:T(256)}, u32[]{:S(2)}) copy-start(f32[256]{0:T(256)} %param.19) | copy-start | bytes 3076
  18.8 4.2 %collective-permute-start = (f32[6,8,130]{2,1,0:T(8,128)S(1)}, f32[6,8,130]{2,1,0:T(8,128)S(1)}, u32[]{:S(2)}, u32[]{:S(2)}) collective-permute-start(f32[6,8,130]{2,1,0:T(8,128)S(1)} %copy.248), channel_id=1, source_target_pairs={{0,2},{1,3},{2,0},{3,1},{4,6},{5,7},{6,4},{7,5},{8,10},{9,11},{10,... | collective-permute-start | bytes 74888 | tf_op jit(solution)/shard_map/ppermute | solution.py:33
  23.9 17.7 %copy-start.4 = (s32[96,8]{0,1:T(8,128)S(1)}, s32[96,8]{0,1:T(8,128)}, u32[]{:S(2)}) copy-start(s32[96,8]{0,1:T(8,128)} %param.20) | copy-start | bytes 9220
  24.0 8.0 %collective-permute-start.1 = (f32[6,4,130]{0,1,2:T(4,128)S(1)}, f32[6,4,130]{0,1,2:T(4,128)S(1)}, u32[]{:S(2)}, u32[]{:S(2)}) collective-permute-start(f32[6,4,130]{0,1,2:T(4,128)S(1)} %constant_dynamic-slice_fusion.4), channel_id=1, source_target_pairs={{0,1},{1,0},{2,3},{3,2},{4,5},{5,4},{6,7},{7,6},{8,9},{9,8},{10,11... | collective-permute-start | bytes 37448 | tf_op jit(solution)/shard_map/ppermute | solution.py:33
  33.0 16.0 %all-to-all-start.1 = ((bf16[16,8,512]{2,1,0:T(8,128)(2,1)}), bf16[16,8,512]{2,1,0:T(8,128)(2,1)S(1)}, u32[]{:S(2)}, u32[]{:S(2)}) async-start(bf16[16,8,512]{2,1,0:T(8,128)(2,1)} %broadcast_in_dim.87), calls=%async_computation.1 | async-start | bytes 262144 | tf_op jit(solution)/shard_map/all_to_all | solution.py:18
  48.9 1.2 copy-start.1
  50.1 20.6 %all-to-all-start.2 = ((bf16[16,96,256]{2,1,0:T(8,128)(2,1)}), bf16[16,96,256]{2,1,0:T(8,128)(2,1)}, u32[]{:S(2)}, u32[]{:S(2)}) async-start(bf16[16,96,256]{2,1,0:T(8,128)(2,1)} %broadcast_in_dim.88), calls=%async_computation.2 | async-start | bytes 1572864 | tf_op jit(solution)/shard_map/all_to_all | solution.py:18
  58.8 4.8 %copy-start.2 = (pred[768,96]{1,0:T(8,128)(4,1)S(1)}, pred[768,96]{1,0:T(8,128)(4,1)}, u32[]{:S(2)}) copy-start(pred[768,96]{1,0:T(8,128)(4,1)} %copy.269) | copy-start | bytes 221188
  73.7 14.1 %all-to-all-start.3 = ((bf16[16,1,24,256]{3,2,1,0:T(8,128)(2,1)}), bf16[16,1,24,256]{3,2,1,0:T(8,128)(2,1)}, u32[]{:S(2)}, u32[]{:S(2)}) async-start(bf16[16,1,24,256]{3,2,1,0:T(8,128)(2,1)} %bitcast.122), calls=%async_computation.3 | async-start | bytes 393216 | tf_op jit(solution)/shard_map/all_to_all | solution.py:237
  98.1 13.4 %all-to-all-start.4 = ((bf16[1,24,16,256]{3,1,0,2:T(8,128)(2,1)}), bf16[1,24,16,256]{3,1,0,2:T(8,128)(2,1)S(1)}, u32[]{:S(2)}, u32[]{:S(2)}) async-start(bf16[1,24,16,256]{3,1,0,2:T(8,128)(2,1)} %fusion.4), calls=%async_computation.4 | async-start | bytes 393216 | tf_op jit(solution)/shard_map/all_to_all | solution.py:251
  111.7 19.2 %copy-start.3 = (bf16[96,256]{1,0:T(8,128)(2,1)S(1)}, bf16[96,256]{1,0:T(8,128)(2,1)}, u32[]{:S(2)}) copy-start(bf16[96,256]{1,0:T(8,128)(2,1)} %param.18) | copy-start | bytes 147460

commit v4 on v3

--- a/solution.py
+++ b/solution.py
@@ -60,11 +60,6 @@
     middle = lax.reduce_precision(rest, exponent_bits=8, mantissa_bits=7)
     low = rest - middle
     return jnp.stack([high, middle, low]).astype(jnp.bfloat16)
-
-
-def join_three(parts):
-    parts = parts.astype(jnp.float32)
-    return (parts[:, 0] + parts[:, 1] + parts[:, 2]).reshape(-1)
 
 
 def merge_packed(first, second, width):
@@ -186,15 +181,7 @@
         .astype(jnp.bfloat16)
     )
     cols_dev = residual.shape[1]
-    gain_parts = split_three(norm_gain)
-    gain_rows = -(-gain_parts.size // block_cols)
-    gain_block = jnp.pad(gain_parts.reshape(-1), (0, gain_rows * block_cols - gain_parts.size))
-    carried = gathered_copies(
-        jnp.concatenate([attention, gain_block.reshape(gain_rows, block_cols)], axis=0), "batch", 0
-    ).reshape(lax.axis_size("batch"), seq_count + gain_rows, block_cols)
-    all_attention = carried[:, :seq_count].reshape(-1, block_cols)
-    got_parts = carried[:, seq_count:].reshape(lax.axis_size("batch"), -1)[:, : gain_parts.size]
-    full_gain = join_three(got_parts.reshape(-1, 3, cols_dev))
+    all_attention = gathered_copies(attention, "batch", 0)
     head_terms = jnp.dot(all_attention, out_weight, preferred_element_type=jnp.float32)
     projected = taken_together(head_terms.astype(jnp.bfloat16), ("sect", "head")).astype(
         jnp.float32
@@ -230,18 +217,33 @@
     )
     coefficient = route_weight / jnp.sum(route_weight, axis=1, keepdims=True)
     combine_full = jnp.sum(jnp.where(matches, coefficient[None, :, :], 0.0), axis=2).T
-    outgoing = jnp.dot(
-        selector, hidden_state.astype(jnp.bfloat16), preferred_element_type=jnp.float32
-    ).astype(jnp.bfloat16)
-    outgoing = outgoing.reshape(batch_size, pair_local, capacity, cols_dev)
-    rows = lax.all_to_all(outgoing, "batch", split_axis=0, concat_axis=3, tiled=True)[0]
-    rows = rows.astype(jnp.float32)
-    squares = jnp.sum(rows * rows, axis=2)
-    inverse = lax.rsqrt(squares / D + NORM_EPS)
-    arrived = (rows * inverse[..., None] * full_gain[None, None, :]).astype(jnp.bfloat16)
+    scaled = (hidden_state * norm_gain[None, :]).astype(jnp.bfloat16)
+    square_parts = split_three(jnp.sum(hidden_state * hidden_state, axis=1))
+    outgoing = jnp.dot(selector, scaled, preferred_element_type=jnp.float32).astype(jnp.bfloat16)
+    slot_squares = jnp.dot(selector, square_parts.T, preferred_element_type=jnp.float32)
+    square_width = 3 * slot_dev
+    square_rows = -(-square_width // cols_dev)
+    square_block = jnp.pad(
+        slot_squares.astype(jnp.bfloat16).reshape(batch_size, square_width),
+        ((0, 0), (0, square_rows * cols_dev - square_width)),
+    ).reshape(batch_size, square_rows, cols_dev)
+    outgoing = jnp.concatenate(
+        [outgoing.reshape(batch_size, slot_dev, cols_dev), square_block], axis=1
+    )
+    arrived = lax.all_to_all(outgoing, "batch", split_axis=0, concat_axis=0, tiled=True)
+    rows = arrived[:, :slot_dev].reshape(batch_size, pair_local, capacity, cols_dev)
+    got_squares = arrived[:, slot_dev:].reshape(batch_size, -1)[:, :square_width]
+    squares = jnp.sum(
+        got_squares.reshape(batch_size, slot_dev, 3).astype(jnp.float32), axis=(0, 2)
+    )
+    inverse = lax.rsqrt(squares / D + NORM_EPS).reshape(pair_local, capacity)
     mixture = jnp.einsum(
-        "ecd,edgf->ecgf", arrived, gate_up_weight, preferred_element_type=jnp.float32
-    )
+        "becd,ebdgf->ecgf",
+        rows,
+        gate_up_weight.reshape(pair_local, batch_size, cols_dev, *gate_up_weight.shape[2:]),
+        preferred_element_type=jnp.float32,
+    )
+    mixture = mixture * inverse[:, :, None, None]
     activated = (jax.nn.silu(mixture[:, :, 0]) * mixture[:, :, 1]).astype(jnp.bfloat16)
     expert_part = jnp.einsum(
         "ecf,efd->ecd", activated, down_weight, preferred_element_type=jnp.float32

time: 134 us -> 133 us (level)
  waiting for transfers between devices: 36.6 us -> 44.6 us
  local copies, waits for them, and re-layouts: 21.8 us -> 16.4 us
  other arithmetic: 13.2 us -> 11.8 us
    all_to_all x2, waiting for transfers between devices: 12.1 us -> 19.5 us  [copy_for_each(): return lax.all_to_all(copies, axis, split_axis=0, concat_axis=0, tiled=True)]
    convert_element_type x4 -> x1, local copies, waits for them, and re-layouts: 3.86 us -> 0.19 us  [on_device(): slot_squares.astype(jnp.bfloat16).reshape(batch_size, square_width)]
    convert_element_type x2 -> x0, other arithmetic: 2.41 us -> none  [the longest x1 1.36 us: join_three(): parts = parts.astype(jnp.float32)]
    dot_general x2 -> x3, matrix products: 5.53 us -> 4.19 us  [the longest x1 3.84 us: on_device(): jnp.einsum('becd,ebdgf->ecgf', rows, gate_up_weight.reshape(pair_local, b...]
  transfers between devices with their start and end apart: 7 -> 7, of which waited for: 7 -> 7; matrix products, arithmetic and copies ran while one was open for 17% -> 12% of each run, Pallas kernels for 0% -> 0%
where the time goes in v4:
time: 133 us; the launch traced here: 131 us
  waiting for transfers between devices  44.6 us (34%)
  starting transfers between devices  31.2 us (23%)
  blocking collectives  18.9 us (14%)
  local copies, waits for them, and re-layouts  16.4 us (12%)
  other arithmetic  11.8 us (9%)
  matrix products  7.57 us (6%)
    all_to_all x2, waiting for transfers between devices, copy_for_each(): return lax.all_to_all(copies, axis, split_axis=0, concat_axis=0, tiled=True)  19.5 us
    all_to_all x1, blocking collectives, copy_for_each(): return lax.all_to_all(copies, axis, split_axis=0, concat_axis=0, tiled=True)  18.9 us
    all_to_all x2, starting transfers between devices, copy_for_each(): return lax.all_to_all(copies, axis, split_axis=0, concat_axis=0, tiled=True)  12.5 us
    ppermute x2, waiting for transfers between devices, from_partner(): lax.ppermute(shard, axis, [(i, i ^ 1 << distance) for i in range(lax.axis...  10.5 us
    all_to_all x1, starting transfers between devices, on_device(): lax.all_to_all(per_target, 'head', split_axis=0, concat_axis=0, tiled=True)  6.93 us
    all_to_all x1, waiting for transfers between devices, on_device(): lax.all_to_all(leaving.astype(jnp.bfloat16), 'batch', split_axis=2, conca...  6.09 us
    all_to_all x1, starting transfers between devices, on_device(): lax.all_to_all(outgoing, 'batch', split_axis=0, concat_axis=0, tiled=True)  5.48 us
    all_to_all x1, waiting for transfers between devices, on_device(): lax.all_to_all(outgoing, 'batch', split_axis=0, concat_axis=0, tiled=True)  5.03 us
  transfers between devices with their start and end apart: 7, of which 7 were waited for; matrix products, arithmetic and copies ran while one was open for 12% of the time, Pallas kernels for 0%

profile of v4, /device:TPU:32, one launch (start us, length us, event | category | flops | bytes accessed | tf_op | source)
XLA Modules:
  0.0 131.0 jit_solution(8241312321739689526)
XLA Ops:
  0.0 0.7 reshape.220
  1.4 6.9 %all-to-all-start = ((bf16[8,6,2,128]{3,2,1,0:T(2,128)(2,1)}), bf16[8,6,2,128]{3,2,1,0:T(2,128)(2,1)S(1)}, u32[]{:S(2)}, u32[]{:S(2)}) async-start(bf16[8,6,2,128]{3,2,1,0:T(2,128)(2,1)} %bitcast.2), calls=%async_computation | async-start | bytes 49152 | tf_op jit(solution)/shard_map/all_to_all | solution.py:120
  8.3 0.7 constant_dynamic-slice_fusion.8
  9.6 2.7 %fusion.63 = (bf16[6,16,64,128]{3,2,1,0:T(8,128)(2,1)S(1)}, bf16[6,16,64,128]{3,2,1,0:T(8,128)(2,1)S(1)}) fusion(bf16[6,16,64,256]{3,2,1,0:T(8,128)(2,1)} %param.14), kind=kLoop, calls=%fused_computation.128 | loop fusion | bytes 6291456 | tf_op jit(solution)/shard_map/slice | solution.py:138
  12.6 3.4 %all-to-all-done = bf16[8,6,2,128]{3,2,1,0:T(2,128)(2,1)S(1)} async-done(((bf16[8,6,2,128]{3,2,1,0:T(2,128)(2,1)}), bf16[8,6,2,128]{3,2,1,0:T(2,128)(2,1)S(1)}, u32[]{:S(2)}, u32[]{:S(2)}) %all-to-all-start) | async-done | bytes 24608 | tf_op jit(solution)/shard_map/all_to_all | solution.py:120
  18.8 0.6 collective-permute-start
  19.7 3.3 %collective-permute-done = f32[6,8,130]{2,1,0:T(8,128)S(1)} collective-permute-done((f32[6,8,130]{2,1,0:T(8,128)S(1)}, f32[6,8,130]{2,1,0:T(8,128)S(1)}, u32[]{:S(2)}, u32[]{:S(2)}) %collective-permute-start) | collective-permute-done | bytes 24992 | tf_op jit(solution)/shard_map/ppermute | solution.py:33
  24.0 0.7 collective-permute-start.1
  24.8 7.3 %collective-permute-done.1 = f32[6,4,130]{0,1,2:T(4,128)S(1)} collective-permute-done((f32[6,4,130]{0,1,2:T(4,128)S(1)}, f32[6,4,130]{0,1,2:T(4,128)S(1)}, u32[]{:S(2)}, u32[]{:S(2)}) %collective-permute-start.1) | collective-permute-done | bytes 12512 | tf_op jit(solution)/shard_map/ppermute | solution.py:33
  32.3 0.7 broadcast_in_dim.87
  33.0 8.6 %all-to-all-start.1 = ((bf16[16,6,512]{2,1,0:T(8,128)(2,1)}), bf16[16,6,512]{2,1,0:T(8,128)(2,1)S(1)}, u32[]{:S(2)}, u32[]{:S(2)}) async-start(bf16[16,6,512]{2,1,0:T(8,128)(2,1)} %broadcast_in_dim.87), calls=%async_computation.1 | async-start | bytes 262144 | tf_op jit(solution)/shard_map/all_to_all | solution.py:18
  41.7 7.2 %all-to-all-done.1 = bf16[16,6,512]{2,1,0:T(8,128)(2,1)S(1)} async-done(((bf16[16,6,512]{2,1,0:T(8,128)(2,1)}), bf16[16,6,512]{2,1,0:T(8,128)(2,1)S(1)}, u32[]{:S(2)}, u32[]{:S(2)}) %all-to-all-start.1) | async-done | bytes 98336 | tf_op jit(solution)/shard_map/all_to_all | solution.py:18
  49.2 1.0 broadcast_in_dim.88
  50.1 3.9 %all-to-all-start.2 = ((bf16[16,96,256]{2,1,0:T(8,128)(2,1)}), bf16[16,96,256]{2,1,0:T(8,128)(2,1)S(1)}, u32[]{:S(2)}, u32[]{:S(2)}) async-start(bf16[16,96,256]{2,1,0:T(8,128)(2,1)} %broadcast_in_dim.88), calls=%async_computation.2 | async-start | bytes 1572864 | tf_op jit(solution)/shard_map/all_to_all | solution.py:18
  54.2 1.8 %reduce-window.6 = s32[64,6,128]{2,0,1:T(8,128)S(1)} reduce-window(s32[64,6,128]{2,0,1:T(8,128)S(1)} %fusion.26, s32[]{:T(128)} %constant.114.clone.1), window={size=1x1x128 pad=0_0x0_0x127_0}, to_apply=%region_4.5 | reduce-window | flops 6242304 | bytes 393220 | tf_op jit(solution)/shard_map/reduce-window
  56.6 0.8 fusion.2
  57.7 12.4 %all-to-all-done.2 = bf16[16,96,256]{2,1,0:T(8,128)(2,1)S(1)} async-done(((bf16[16,96,256]{2,1,0:T(8,128)(2,1)}), bf16[16,96,256]{2,1,0:T(8,128)(2,1)S(1)}, u32[]{:S(2)}, u32[]{:S(2)}) %all-to-all-start.2) | async-done | bytes 786464 | tf_op jit(solution)/shard_map/all_to_all | solution.py:18
  71.0 0.7 pad_maximum_fusion.2
  71.7 5.5 %all-to-all-start.3 = ((bf16[16,25,256]{2,1,0:T(8,128)(2,1)}), bf16[16,25,256]{2,1,0:T(8,128)(2,1)}, u32[]{:S(2)}, u32[]{:S(2)}) async-start(bf16[16,25,256]{2,1,0:T(8,128)(2,1)} %pad_maximum_fusion.2), calls=%async_computation.3 | async-start | bytes 524288 | tf_op jit(solution)/shard_map/all_to_all | solution.py:233
  77.2 3.4 %copy.256 = bf16[4096,384]{1,0:T(8,128)(2,1)S(1)} copy(bf16[4096,384]{0,1:T(8,128)(2,1)} %bitcast.127) | data formatting | bytes 6291456 | tf_op jit(solution)/shard_map/ecf,efd->ecd/dot_general | solution.py:248
  80.6 1.3 reduce_sum.87
  81.9 5.0 %all-to-all-done.3 = bf16[16,25,256]{2,1,0:T(8,128)(2,1)} async-done(((bf16[16,25,256]{2,1,0:T(8,128)(2,1)}), bf16[16,25,256]{2,1,0:T(8,128)(2,1)}, u32[]{:S(2)}, u32[]{:S(2)}) %all-to-all-start.3) | async-done | bytes 204832 | tf_op jit(solution)/shard_map/all_to_all | solution.py:233
  86.9 0.9 slice.102
  88.4 1.3 %reduce_sum.92 = f32[24,3]{1,0:T(8,128)} reshape(f32[72]{0:T(128)} %convert_reduce_fusion.2) | data formatting | bytes 576 | tf_op jit(solution)/shard_map/reduce_sum | solution.py:236
  89.7 1.4 %reduce_sum.93 = f32[24]{0:T(128)} reduce(f32[24,3]{1,0:T(8,128)} %reduce_sum.92, f32[]{:T(128)} %constant.129.clone.1), dimensions={1}, to_apply=%region_12.13 | reduce | flops 48 | bytes 388 | tf_op jit(solution)/shard_map/reduce_sum | solution.py:236
  91.7 3.8 %fusion.11 = f32[1,24,2,384]{3,1,2,0:T(8,128)S(1)} fusion(bf16[16,256,2,384]{3,2,1,0:T(2,128)(2,1)} %bitcast.147, bf16[16,25,256]{2,1,0:T(8,128)(2,1)} %all-to-all-done.3, f32[24]{0:T(128)S(1)} %add_rsqrt_fusion), kind=kOutput, calls=%fused_computation.16 | convolution fusion | flops 151013376 | bytes 6561888 | tf_op jit(solution)/shard_map/becd,ebdgf->ecgf/dot_general | solution.py:240
  95.5 1.9 %fusion.4 = bf16[1,24,16,256]{3,1,0,2:T(8,128)(2,1)} fusion(bf16[16,256,384]{2,1,0:T(8,128)(2,1)S(1)} %bitcast.124, f32[1,24,2,384]{3,1,2,0:T(8,128)S(1)} %fusion.11), kind=kOutput, calls=%fused_computation.11 | convolution fusion | flops 75651072 | bytes 3416064 | tf_op jit(solution)/shard_map/ecf,efd->ecd/dot_general | solution.py:248
  97.4 5.0 %all-to-all-start.4 = ((bf16[1,24,16,256]{3,1,0,2:T(8,128)(2,1)}), bf16[1,24,16,256]{3,1,0,2:T(8,128)(2,1)S(1)}, u32[]{:S(2)}, u32[]{:S(2)}) async-start(bf16[1,24,16,256]{3,1,0,2:T(8,128)(2,1)} %fusion.4), calls=%async_computation.4 | async-start | bytes 393216 | tf_op jit(solution)/shard_map/all_to_all | solution.py:253
  102.3 0.7 broadcast_divide_fusion
  103.1 1.6 %select_reduce_fusion = bf16[768,96]{0,1:T(8,128)(2,1)S(1)} fusion(f32[96,8]{1,0:T(8,128)S(1)} %copy.243, s32[96,8]{1,0:T(8,128)} %copy-done.2), kind=kLoop, calls=%fused_computation.2 | loop fusion | flops 1695744 | bytes 153600 | tf_op jit(solution)/shard_map/reduce_sum | solution.py:219
  104.9 6.1 %all-to-all-done.4 = bf16[1,24,16,256]{3,1,0,2:T(8,128)(2,1)S(1)} async-done(((bf16[1,24,16,256]{3,1,0,2:T(8,128)(2,1)}), bf16[1,24,16,256]{3,1,0,2:T(8,128)(2,1)S(1)}, u32[]{:S(2)}, u32[]{:S(2)}) %all-to-all-start.4) | async-done | bytes 196640 | tf_op jit(solution)/shard_map/all_to_all | solution.py:253
  111.3 18.9 %all_to_all.40 = bf16[16,96,256]{2,1,0:T(8,128)(2,1)S(1)} all-to-all(bf16[16,96,256]{2,1,0:T(8,128)(2,1)S(1)} %broadcast_in_dim.91), channel_id=1, replica_groups=mesh['sect'=2,'batch'=16,'head'=8] {'sect','head'}, dimensions={0} | all-to-all | bytes 1572864 | tf_op jit(solution)/shard_map/all_to_all | solution.py:18
  (92 shorter events, 10.4 us)
Async XLA Ops:
  0.0 49.0 %copy-start = (bf16[512,256]{1,0:T(8,128)(2,1)S(1)}, bf16[512,256]{1,0:T(8,128)(2,1)}, u32[]{:S(2)}) copy-start(bf16[512,256]{1,0:T(8,128)(2,1)} %param.17) | copy-start | bytes 786436
  1.4 14.6 %all-to-all-start = ((bf16[8,6,2,128]{3,2,1,0:T(2,128)(2,1)}), bf16[8,6,2,128]{3,2,1,0:T(2,128)(2,1)S(1)}, u32[]{:S(2)}, u32[]{:S(2)}) async-start(bf16[8,6,2,128]{3,2,1,0:T(2,128)(2,1)} %bitcast.2), calls=%async_computation | async-start | bytes 49152 | tf_op jit(solution)/shard_map/all_to_all | solution.py:120
  9.6 2.7 %copy-start.4 = (bf16[6,4,256]{2,1,0:T(4,128)(2,1)S(1)}, bf16[6,4,256]{2,1,0:T(4,128)(2,1)}, u32[]{:S(2)}) copy-start(bf16[6,4,256]{2,1,0:T(4,128)(2,1)} %param.13) | copy-start | bytes 36868
  9.6 2.8 %copy-start.6 = (s32[6]{0:T(128)S(1)}, s32[6]{0:T(128)}, u32[]{:S(2)}) copy-start(s32[6]{0:T(128)} %param.15) | copy-start | bytes 76
  18.8 4.2 %collective-permute-start = (f32[6,8,130]{2,1,0:T(8,128)S(1)}, f32[6,8,130]{2,1,0:T(8,128)S(1)}, u32[]{:S(2)}, u32[]{:S(2)}) collective-permute-start(f32[6,8,130]{2,1,0:T(8,128)S(1)} %copy.224), channel_id=1, source_target_pairs={{0,2},{1,3},{2,0},{3,1},{4,6},{5,7},{6,4},{7,5},{8,10},{9,11},{10,... | collective-permute-start | bytes 74888 | tf_op jit(solution)/shard_map/ppermute | solution.py:33
  23.6 17.9 %copy-start.3 = (s32[96,8]{0,1:T(8,128)S(1)}, s32[96,8]{0,1:T(8,128)}, u32[]{:S(2)}) copy-start(s32[96,8]{0,1:T(8,128)} %param.20) | copy-start | bytes 9220
  24.0 8.0 %collective-permute-start.1 = (f32[6,4,130]{0,1,2:T(4,128)S(1)}, f32[6,4,130]{0,1,2:T(4,128)S(1)}, u32[]{:S(2)}, u32[]{:S(2)}) collective-permute-start(f32[6,4,130]{0,1,2:T(4,128)S(1)} %constant_dynamic-slice_fusion.4), channel_id=1, source_target_pairs={{0,1},{1,0},{2,3},{3,2},{4,5},{5,4},{6,7},{7,6},{8,9},{9,8},{10,11... | collective-permute-start | bytes 37448 | tf_op jit(solution)/shard_map/ppermute | solution.py:33
  33.0 16.0 %all-to-all-start.1 = ((bf16[16,6,512]{2,1,0:T(8,128)(2,1)}), bf16[16,6,512]{2,1,0:T(8,128)(2,1)S(1)}, u32[]{:S(2)}, u32[]{:S(2)}) async-start(bf16[16,6,512]{2,1,0:T(8,128)(2,1)} %broadcast_in_dim.87), calls=%async_computation.1 | async-start | bytes 262144 | tf_op jit(solution)/shard_map/all_to_all | solution.py:18
  50.1 19.9 %all-to-all-start.2 = ((bf16[16,96,256]{2,1,0:T(8,128)(2,1)}), bf16[16,96,256]{2,1,0:T(8,128)(2,1)S(1)}, u32[]{:S(2)}, u32[]{:S(2)}) async-start(bf16[16,96,256]{2,1,0:T(8,128)(2,1)} %broadcast_in_dim.88), calls=%async_computation.2 | async-start | bytes 1572864 | tf_op jit(solution)/shard_map/all_to_all | solution.py:18
  54.0 16.1 %copy-start.1 = (bf16[96,256]{1,0:T(8,128)(2,1)S(1)}, bf16[96,256]{1,0:T(8,128)(2,1)}, u32[]{:S(2)}) copy-start(bf16[96,256]{1,0:T(8,128)(2,1)} %param.18) | copy-start | bytes 147460
  54.0 16.2 %copy-start.5 = (f32[256]{0:T(256)S(1)}, f32[256]{0:T(256)}, u32[]{:S(2)}) copy-start(f32[256]{0:T(256)} %param.19) | copy-start | bytes 3076
  56.6 1.1 copy-start.2
  71.7 15.2 %all-to-all-start.3 = ((bf16[16,25,256]{2,1,0:T(8,128)(2,1)}), bf16[16,25,256]{2,1,0:T(8,128)(2,1)}, u32[]{:S(2)}, u32[]{:S(2)}) async-start(bf16[16,25,256]{2,1,0:T(8,128)(2,1)} %pad_maximum_fusion.2), calls=%async_computation.3 | async-start | bytes 524288 | tf_op jit(solution)/shard_map/all_to_all | solution.py:233
  97.4 13.7 %all-to-all-start.4 = ((bf16[1,24,16,256]{3,1,0,2:T(8,128)(2,1)}), bf16[1,24,16,256]{3,1,0,2:T(8,128)(2,1)S(1)}, u32[]{:S(2)}, u32[]{:S(2)}) async-start(bf16[1,24,16,256]{3,1,0,2:T(8,128)(2,1)} %fusion.4), calls=%async_computation.4 | async-start | bytes 393216 | tf_op jit(solution)/shard_map/all_to_all | solution.py:253

commit v5 on v4

--- a/solution.py
+++ b/solution.py
@@ -220,11 +220,12 @@
     scaled = (hidden_state * norm_gain[None, :]).astype(jnp.bfloat16)
     square_parts = split_three(jnp.sum(hidden_state * hidden_state, axis=1))
     outgoing = jnp.dot(selector, scaled, preferred_element_type=jnp.float32).astype(jnp.bfloat16)
-    slot_squares = jnp.dot(selector, square_parts.T, preferred_element_type=jnp.float32)
+    slot_squares = jnp.dot(square_parts, selector.T, preferred_element_type=jnp.float32)
     square_width = 3 * slot_dev
     square_rows = -(-square_width // cols_dev)
     square_block = jnp.pad(
-        slot_squares.astype(jnp.bfloat16).reshape(batch_size, square_width),
+        jnp.moveaxis(slot_squares.astype(jnp.bfloat16).reshape(3, batch_size, slot_dev), 0, 1)
+        .reshape(batch_size, square_width),
         ((0, 0), (0, square_rows * cols_dev - square_width)),
     ).reshape(batch_size, square_rows, cols_dev)
     outgoing = jnp.concatenate(
@@ -234,7 +235,7 @@
     rows = arrived[:, :slot_dev].reshape(batch_size, pair_local, capacity, cols_dev)
     got_squares = arrived[:, slot_dev:].reshape(batch_size, -1)[:, :square_width]
     squares = jnp.sum(
-        got_squares.reshape(batch_size, slot_dev, 3).astype(jnp.float32), axis=(0, 2)
+        got_squares.reshape(batch_size * 3, slot_dev).astype(jnp.float32), axis=0
     )
     inverse = lax.rsqrt(squares / D + NORM_EPS).reshape(pair_local, capacity)
     mixture = jnp.einsum(

time: 133 us -> 133 us (level)
  no operation moved by 1% of the time
where the time goes in v5:
time: 133 us; the launch traced here: 131 us
  waiting for transfers between devices  44.6 us (34%)
  starting transfers between devices  31.2 us (23%)
  blocking collectives  18.9 us (14%)
  local copies, waits for them, and re-layouts  16.3 us (12%)
  other arithmetic  11.7 us (9%)
  matrix products  7.57 us (6%)
    all_to_all x2, waiting for transfers between devices, copy_for_each(): return lax.all_to_all(copies, axis, split_axis=0, concat_axis=0, tiled=True)  19.5 us
    all_to_all x1, blocking collectives, copy_for_each(): return lax.all_to_all(copies, axis, split_axis=0, concat_axis=0, tiled=True)  18.9 us
    all_to_all x2, starting transfers between devices, copy_for_each(): return lax.all_to_all(copies, axis, split_axis=0, concat_axis=0, tiled=True)  12.5 us
    ppermute x2, waiting for transfers between devices, from_partner(): lax.ppermute(shard, axis, [(i, i ^ 1 << distance) for i in range(lax.axis...  10.5 us
    all_to_all x1, starting transfers between devices, on_device(): lax.all_to_all(per_target, 'head', split_axis=0, concat_axis=0, tiled=True)  6.93 us
    all_to_all x1, waiting for transfers between devices, on_device(): lax.all_to_all(leaving.astype(jnp.bfloat16), 'batch', split_axis=2, conca...  6.09 us
    all_to_all x1, starting transfers between devices, on_device(): lax.all_to_all(outgoing, 'batch', split_axis=0, concat_axis=0, tiled=True)  5.48 us
    all_to_all x1, waiting for transfers between devices, on_device(): lax.all_to_all(outgoing, 'batch', split_axis=0, concat_axis=0, tiled=True)  5.03 us
  transfers between devices with their start and end apart: 7, of which 7 were waited for; matrix products, arithmetic and copies ran while one was open for 12% of the time, Pallas kernels for 0%

profile of v5, /device:TPU:32, one launch (start us, length us, event | category | flops | bytes accessed | tf_op | source)
XLA Modules:
  0.0 130.8 jit_solution(1071675755458819457)
XLA Ops:
  0.0 0.7 reshape.224
  1.4 6.9 %all-to-all-start = ((bf16[8,6,2,128]{3,2,1,0:T(2,128)(2,1)}), bf16[8,6,2,128]{3,2,1,0:T(2,128)(2,1)S(1)}, u32[]{:S(2)}, u32[]{:S(2)}) async-start(bf16[8,6,2,128]{3,2,1,0:T(2,128)(2,1)} %bitcast.2), calls=%async_computation | async-start | bytes 49152 | tf_op jit(solution)/shard_map/all_to_all | solution.py:120
  8.3 0.7 constant_dynamic-slice_fusion.8
  9.6 2.7 %fusion.63 = (bf16[6,16,64,128]{3,2,1,0:T(8,128)(2,1)S(1)}, bf16[6,16,64,128]{3,2,1,0:T(8,128)(2,1)S(1)}) fusion(bf16[6,16,64,256]{3,2,1,0:T(8,128)(2,1)} %param.14), kind=kLoop, calls=%fused_computation.129 | loop fusion | bytes 6291456 | tf_op jit(solution)/shard_map/slice | solution.py:138
  12.6 3.4 %all-to-all-done = bf16[8,6,2,128]{3,2,1,0:T(2,128)(2,1)S(1)} async-done(((bf16[8,6,2,128]{3,2,1,0:T(2,128)(2,1)}), bf16[8,6,2,128]{3,2,1,0:T(2,128)(2,1)S(1)}, u32[]{:S(2)}, u32[]{:S(2)}) %all-to-all-start) | async-done | bytes 24608 | tf_op jit(solution)/shard_map/all_to_all | solution.py:120
  18.8 0.6 collective-permute-start
  19.7 3.3 %collective-permute-done = f32[6,8,130]{2,1,0:T(8,128)S(1)} collective-permute-done((f32[6,8,130]{2,1,0:T(8,128)S(1)}, f32[6,8,130]{2,1,0:T(8,128)S(1)}, u32[]{:S(2)}, u32[]{:S(2)}) %collective-permute-start) | collective-permute-done | bytes 24992 | tf_op jit(solution)/shard_map/ppermute | solution.py:33
  24.0 0.7 collective-permute-start.1
  24.8 7.3 %collective-permute-done.1 = f32[6,4,130]{0,1,2:T(4,128)S(1)} collective-permute-done((f32[6,4,130]{0,1,2:T(4,128)S(1)}, f32[6,4,130]{0,1,2:T(4,128)S(1)}, u32[]{:S(2)}, u32[]{:S(2)}) %collective-permute-start.1) | collective-permute-done | bytes 12512 | tf_op jit(solution)/shard_map/ppermute | solution.py:33
  32.3 0.7 broadcast_in_dim.87
  33.0 8.6 %all-to-all-start.1 = ((bf16[16,6,512]{2,1,0:T(8,128)(2,1)}), bf16[16,6,512]{2,1,0:T(8,128)(2,1)S(1)}, u32[]{:S(2)}, u32[]{:S(2)}) async-start(bf16[16,6,512]{2,1,0:T(8,128)(2,1)} %broadcast_in_dim.87), calls=%async_computation.1 | async-start | bytes 262144 | tf_op jit(solution)/shard_map/all_to_all | solution.py:18
  41.7 7.2 %all-to-all-done.1 = bf16[16,6,512]{2,1,0:T(8,128)(2,1)S(1)} async-done(((bf16[16,6,512]{2,1,0:T(8,128)(2,1)}), bf16[16,6,512]{2,1,0:T(8,128)(2,1)S(1)}, u32[]{:S(2)}, u32[]{:S(2)}) %all-to-all-start.1) | async-done | bytes 98336 | tf_op jit(solution)/shard_map/all_to_all | solution.py:18
  49.2 1.0 broadcast_in_dim.88
  50.1 3.9 %all-to-all-start.2 = ((bf16[16,96,256]{2,1,0:T(8,128)(2,1)}), bf16[16,96,256]{2,1,0:T(8,128)(2,1)S(1)}, u32[]{:S(2)}, u32[]{:S(2)}) async-start(bf16[16,96,256]{2,1,0:T(8,128)(2,1)} %broadcast_in_dim.88), calls=%async_computation.2 | async-start | bytes 1572864 | tf_op jit(solution)/shard_map/all_to_all | solution.py:18
  54.2 1.8 %reduce-window.6 = s32[64,6,128]{2,0,1:T(8,128)S(1)} reduce-window(s32[64,6,128]{2,0,1:T(8,128)S(1)} %fusion.26, s32[]{:T(128)} %constant.114.clone.1), window={size=1x1x128 pad=0_0x0_0x127_0}, to_apply=%region_4.5 | reduce-window | flops 6242304 | bytes 393220 | tf_op jit(solution)/shard_map/reduce-window
  56.6 0.8 fusion.2
  57.7 12.4 %all-to-all-done.2 = bf16[16,96,256]{2,1,0:T(8,128)(2,1)S(1)} async-done(((bf16[16,96,256]{2,1,0:T(8,128)(2,1)}), bf16[16,96,256]{2,1,0:T(8,128)(2,1)S(1)}, u32[]{:S(2)}, u32[]{:S(2)}) %all-to-all-start.2) | async-done | bytes 786464 | tf_op jit(solution)/shard_map/all_to_all | solution.py:18
  70.9 0.7 pad_maximum_fusion.2
  71.6 5.5 %all-to-all-start.3 = ((bf16[16,25,256]{2,1,0:T(8,128)(2,1)}), bf16[16,25,256]{2,1,0:T(8,128)(2,1)}, u32[]{:S(2)}, u32[]{:S(2)}) async-start(bf16[16,25,256]{2,1,0:T(8,128)(2,1)} %pad_maximum_fusion.2), calls=%async_computation.3 | async-start | bytes 524288 | tf_op jit(solution)/shard_map/all_to_all | solution.py:234
  77.1 3.4 %copy.257 = bf16[4096,384]{1,0:T(8,128)(2,1)S(1)} copy(bf16[4096,384]{0,1:T(8,128)(2,1)} %bitcast.130) | data formatting | bytes 6291456 | tf_op jit(solution)/shard_map/ecf,efd->ecd/dot_general | solution.py:249
  80.5 1.3 reduce_sum.80
  81.8 5.0 %all-to-all-done.3 = bf16[16,25,256]{2,1,0:T(8,128)(2,1)} async-done(((bf16[16,25,256]{2,1,0:T(8,128)(2,1)}), bf16[16,25,256]{2,1,0:T(8,128)(2,1)}, u32[]{:S(2)}, u32[]{:S(2)}) %all-to-all-start.3) | async-done | bytes 204832 | tf_op jit(solution)/shard_map/all_to_all | solution.py:234
  86.8 0.9 slice.102
  88.3 1.4 %reshape.243 = f32[48,24]{1,0:T(8,128)} reshape(f32[16,72]{1,0:T(8,128)} %slice_convert_fusion) | data formatting | bytes 9216 | tf_op jit(solution)/shard_map/convert_element_type | solution.py:238
  89.7 1.2 reduce_sum.84
  91.5 3.8 %fusion.11 = f32[1,24,2,384]{3,1,2,0:T(8,128)S(1)} fusion(bf16[16,256,2,384]{3,2,1,0:T(2,128)(2,1)} %bitcast.151, bf16[16,25,256]{2,1,0:T(8,128)(2,1)} %all-to-all-done.3, f32[24]{0:T(128)S(1)} %add_rsqrt_fusion), kind=kOutput, calls=%fused_computation.16 | convolution fusion | flops 151013376 | bytes 6561888 | tf_op jit(solution)/shard_map/becd,ebdgf->ecgf/dot_general | solution.py:241
  95.3 1.9 %fusion.4 = bf16[1,24,16,256]{3,1,0,2:T(8,128)(2,1)} fusion(bf16[16,256,384]{2,1,0:T(8,128)(2,1)S(1)} %bitcast.127, f32[1,24,2,384]{3,1,2,0:T(8,128)S(1)} %fusion.11), kind=kOutput, calls=%fused_computation.11 | convolution fusion | flops 75651072 | bytes 3416064 | tf_op jit(solution)/shard_map/ecf,efd->ecd/dot_general | solution.py:249
  97.2 5.0 %all-to-all-start.4 = ((bf16[1,24,16,256]{3,1,0,2:T(8,128)(2,1)}), bf16[1,24,16,256]{3,1,0,2:T(8,128)(2,1)S(1)}, u32[]{:S(2)}, u32[]{:S(2)}) async-start(bf16[1,24,16,256]{3,1,0,2:T(8,128)(2,1)} %fusion.4), calls=%async_computation.4 | async-start | bytes 393216 | tf_op jit(solution)/shard_map/all_to_all | solution.py:254
  102.2 0.7 broadcast_divide_fusion
  103.0 1.6 %select_reduce_fusion = bf16[768,96]{0,1:T(8,128)(2,1)S(1)} fusion(f32[96,8]{1,0:T(8,128)S(1)} %copy.244, s32[96,8]{1,0:T(8,128)} %copy-done.2), kind=kLoop, calls=%fused_computation.2 | loop fusion | flops 1695744 | bytes 153600 | tf_op jit(solution)/shard_map/reduce_sum | solution.py:219
  104.8 6.1 %all-to-all-done.4 = bf16[1,24,16,256]{3,1,0,2:T(8,128)(2,1)S(1)} async-done(((bf16[1,24,16,256]{3,1,0,2:T(8,128)(2,1)}), bf16[1,24,16,256]{3,1,0,2:T(8,128)(2,1)S(1)}, u32[]{:S(2)}, u32[]{:S(2)}) %all-to-all-start.4) | async-done | bytes 196640 | tf_op jit(solution)/shard_map/all_to_all | solution.py:254
  111.2 18.9 %all_to_all.40 = bf16[16,96,256]{2,1,0:T(8,128)(2,1)S(1)} all-to-all(bf16[16,96,256]{2,1,0:T(8,128)(2,1)S(1)} %broadcast_in_dim.91), channel_id=1, replica_groups=mesh['sect'=2,'batch'=16,'head'=8] {'sect','head'}, dimensions={0} | all-to-all | bytes 1572864 | tf_op jit(solution)/shard_map/all_to_all | solution.py:18
  (93 shorter events, 10.3 us)
Async XLA Ops:
  0.0 49.0 %copy-start = (bf16[512,256]{1,0:T(8,128)(2,1)S(1)}, bf16[512,256]{1,0:T(8,128)(2,1)}, u32[]{:S(2)}) copy-start(bf16[512,256]{1,0:T(8,128)(2,1)} %param.17) | copy-start | bytes 786436
  1.4 14.6 %all-to-all-start = ((bf16[8,6,2,128]{3,2,1,0:T(2,128)(2,1)}), bf16[8,6,2,128]{3,2,1,0:T(2,128)(2,1)S(1)}, u32[]{:S(2)}, u32[]{:S(2)}) async-start(bf16[8,6,2,128]{3,2,1,0:T(2,128)(2,1)} %bitcast.2), calls=%async_computation | async-start | bytes 49152 | tf_op jit(solution)/shard_map/all_to_all | solution.py:120
  9.6 2.7 %copy-start.4 = (bf16[6,4,256]{2,1,0:T(4,128)(2,1)S(1)}, bf16[6,4,256]{2,1,0:T(4,128)(2,1)}, u32[]{:S(2)}) copy-start(bf16[6,4,256]{2,1,0:T(4,128)(2,1)} %param.13) | copy-start | bytes 36868
  9.6 2.8 %copy-start.6 = (s32[6]{0:T(128)S(1)}, s32[6]{0:T(128)}, u32[]{:S(2)}) copy-start(s32[6]{0:T(128)} %param.15) | copy-start | bytes 76
  18.8 4.2 %collective-permute-start = (f32[6,8,130]{2,1,0:T(8,128)S(1)}, f32[6,8,130]{2,1,0:T(8,128)S(1)}, u32[]{:S(2)}, u32[]{:S(2)}) collective-permute-start(f32[6,8,130]{2,1,0:T(8,128)S(1)} %copy.225), channel_id=1, source_target_pairs={{0,2},{1,3},{2,0},{3,1},{4,6},{5,7},{6,4},{7,5},{8,10},{9,11},{10,... | collective-permute-start | bytes 74888 | tf_op jit(solution)/shard_map/ppermute | solution.py:33
  23.6 17.9 %copy-start.3 = (s32[96,8]{0,1:T(8,128)S(1)}, s32[96,8]{0,1:T(8,128)}, u32[]{:S(2)}) copy-start(s32[96,8]{0,1:T(8,128)} %param.20) | copy-start | bytes 9220
  24.0 8.0 %collective-permute-start.1 = (f32[6,4,130]{0,1,2:T(4,128)S(1)}, f32[6,4,130]{0,1,2:T(4,128)S(1)}, u32[]{:S(2)}, u32[]{:S(2)}) collective-permute-start(f32[6,4,130]{0,1,2:T(4,128)S(1)} %constant_dynamic-slice_fusion.4), channel_id=1, source_target_pairs={{0,1},{1,0},{2,3},{3,2},{4,5},{5,4},{6,7},{7,6},{8,9},{9,8},{10,11... | collective-permute-start | bytes 37448 | tf_op jit(solution)/shard_map/ppermute | solution.py:33
  33.0 16.0 %all-to-all-start.1 = ((bf16[16,6,512]{2,1,0:T(8,128)(2,1)}), bf16[16,6,512]{2,1,0:T(8,128)(2,1)S(1)}, u32[]{:S(2)}, u32[]{:S(2)}) async-start(bf16[16,6,512]{2,1,0:T(8,128)(2,1)} %broadcast_in_dim.87), calls=%async_computation.1 | async-start | bytes 262144 | tf_op jit(solution)/shard_map/all_to_all | solution.py:18
  50.1 19.9 %all-to-all-start.2 = ((bf16[16,96,256]{2,1,0:T(8,128)(2,1)}), bf16[16,96,256]{2,1,0:T(8,128)(2,1)S(1)}, u32[]{:S(2)}, u32[]{:S(2)}) async-start(bf16[16,96,256]{2,1,0:T(8,128)(2,1)} %broadcast_in_dim.88), calls=%async_computation.2 | async-start | bytes 1572864 | tf_op jit(solution)/shard_map/all_to_all | solution.py:18
  54.0 16.1 %copy-start.1 = (bf16[96,256]{1,0:T(8,128)(2,1)S(1)}, bf16[96,256]{1,0:T(8,128)(2,1)}, u32[]{:S(2)}) copy-start(bf16[96,256]{1,0:T(8,128)(2,1)} %param.18) | copy-start | bytes 147460
  54.0 16.2 %copy-start.5 = (f32[256]{0:T(256)S(1)}, f32[256]{0:T(256)}, u32[]{:S(2)}) copy-start(f32[256]{0:T(256)} %param.19) | copy-start | bytes 3076
  56.6 1.1 copy-start.2
  71.6 15.2 %all-to-all-start.3 = ((bf16[16,25,256]{2,1,0:T(8,128)(2,1)}), bf16[16,25,256]{2,1,0:T(8,128)(2,1)}, u32[]{:S(2)}, u32[]{:S(2)}) async-start(bf16[16,25,256]{2,1,0:T(8,128)(2,1)} %pad_maximum_fusion.2), calls=%async_computation.3 | async-start | bytes 524288 | tf_op jit(solution)/shard_map/all_to_all | solution.py:234
  97.2 13.7 %all-to-all-start.4 = ((bf16[1,24,16,256]{3,1,0,2:T(8,128)(2,1)}), bf16[1,24,16,256]{3,1,0,2:T(8,128)(2,1)S(1)}, u32[]{:S(2)}, u32[]{:S(2)}) async-start(bf16[1,24,16,256]{3,1,0,2:T(8,128)(2,1)} %fusion.4), calls=%async_computation.4 | async-start | bytes 393216 | tf_op jit(solution)/shard_map/all_to_all | solution.py:254

commit v6 on v5

--- a/solution.py
+++ b/solution.py
@@ -7,6 +7,8 @@
 
 D = 4096
 EXPERTS = 64
+KEY_VALUE_HEADS = 4
+HEAD = ("htop", "hq")
 
 
 NEG_FILL = -1e30
@@ -102,10 +104,10 @@
     head_dim = newest_key_value.shape[2] // 2
     kv_heads = newest_key_value.shape[1]
     sect_size = lax.axis_size("sect")
-    head_size = lax.axis_size("head")
+    head_size = lax.axis_size(HEAD)
     batch_size = lax.axis_size("batch")
     group_size = sect_size * head_size // kv_heads
-    position = lax.axis_index("sect") * head_size + lax.axis_index("head")
+    position = lax.axis_index("sect") * head_size + lax.axis_index(HEAD)
     kv_index = position // group_size
     quarter = position % group_size
     local_pages = page_cache.shape[1]
@@ -117,7 +119,7 @@
         by_kv[:, None], (kv_per_sect, head_size // kv_per_sect, *by_kv.shape[1:])
     ).reshape(head_size, *by_kv.shape[1:])
     group_query = in_order(
-        lax.all_to_all(per_target, "head", split_axis=0, concat_axis=0, tiled=True), 1
+        lax.all_to_all(per_target, HEAD, split_axis=0, concat_axis=0, tiled=True), 1
     )
     heads_dev = group_query.shape[1] // group_size
     block_cols = heads_dev * head_dim
@@ -166,24 +168,38 @@
     weighted = weighted + fresh_weight.astype(jnp.bfloat16).astype(jnp.float32)[
         ..., None
     ] * newest_entry[:, None, head_dim:].astype(jnp.float32)
-    packed = jnp.concatenate([weighted, running_max[..., None], running_sum[..., None]], axis=2)
-    bit_count = group_size.bit_length() - 1
-    for bit_index in reversed(range(bit_count)):
-        half_heads = packed.shape[1] // 2
-        keep_half = quarter >> bit_index & 1
-        kept = lax.dynamic_slice_in_dim(packed, keep_half * half_heads, half_heads, 1)
-        sent = lax.dynamic_slice_in_dim(packed, (1 - keep_half) * half_heads, half_heads, 1)
-        partner = from_partner(sent, "head", bit_index)
-        packed = merge_packed(kept, partner, head_dim)
-    attention = (
-        (packed[..., :head_dim] / packed[..., head_dim + 1 :])
-        .reshape(seq_count, block_cols)
+    batch_count = lax.axis_size("batch")
+    chunk_rows = seq_count * heads_dev
+    stats = jnp.stack([running_max, running_sum])
+    stats = stats.reshape(2, seq_count, group_size, heads_dev)
+    stats = jnp.moveaxis(stats, 2, 0).reshape(group_size, 2, chunk_rows)
+    lane_pad = -(-chunk_rows // head_dim) * head_dim
+    stats = jnp.pad(stats, ((0, 0), (0, 0), (0, lane_pad - chunk_rows)))
+    stat_rows = lane_pad // head_dim
+    stats = stats.reshape(group_size, 2 * stat_rows, head_dim)
+    parts = weighted.reshape(seq_count, group_size, heads_dev, head_dim)
+    parts = jnp.moveaxis(parts, 1, 0).reshape(group_size, chunk_rows, head_dim)
+    chunk = jnp.concatenate([parts, stats], axis=1)
+    outgoing_parts = jnp.broadcast_to(chunk[None], (batch_count, *chunk.shape)).reshape(
+        batch_count * group_size, *chunk.shape[1:]
+    )
+    got = lax.all_to_all(outgoing_parts, ("batch", "hq"), split_axis=0, concat_axis=0, tiled=True)
+    got = got.reshape(batch_count, group_size, *chunk.shape[1:])
+    got_acc = got[:, :, :chunk_rows]
+    got_stats = got[:, :, chunk_rows:].reshape(batch_count, group_size, 2, lane_pad)[..., :chunk_rows]
+    got_max, got_sum = got_stats[:, :, 0], got_stats[:, :, 1]
+    joined = jnp.max(got_max, axis=1, keepdims=True)
+    factor = jnp.exp(got_max - joined)
+    total = jnp.sum(got_sum * factor, axis=1)
+    merged = jnp.sum(got_acc * factor[..., None], axis=1)
+    all_attention = (
+        (merged / total[..., None])
+        .reshape(batch_count * seq_count, block_cols)
         .astype(jnp.bfloat16)
     )
     cols_dev = residual.shape[1]
-    all_attention = gathered_copies(attention, "batch", 0)
     head_terms = jnp.dot(all_attention, out_weight, preferred_element_type=jnp.float32)
-    projected = taken_together(head_terms.astype(jnp.bfloat16), ("sect", "head")).astype(
+    projected = taken_together(head_terms.astype(jnp.bfloat16), ("sect", *HEAD)).astype(
         jnp.float32
     )
     hidden_state = residual.astype(jnp.float32) + projected
@@ -194,7 +210,7 @@
     one_hot = (flat_ids[:, None] == jnp.arange(EXPERTS, dtype=jnp.int32)[None, :]).astype(jnp.int32)
     earlier = jnp.cumsum(one_hot, axis=0) - one_hot
     rank_in = jnp.sum(earlier * one_hot, axis=1)
-    sub_half = lax.axis_index("head") // (head_size // 2)
+    sub_half = lax.axis_index(HEAD) // (head_size // 2)
     pair_first = lax.axis_index("sect") * (batch_size * pair_local)
     local_pair = flat_ids // 2 - pair_first
     in_sect = (local_pair >= 0) & (local_pair < batch_size * pair_local)
@@ -262,25 +278,32 @@
     )
     weights_used = weights_used.reshape(token_count, send_count)
     combined = jnp.dot(weights_used, came_back, preferred_element_type=jnp.float32)
-    expert_mix = taken_together(combined.astype(jnp.bfloat16), ("sect", "head")).astype(jnp.float32)
+    expert_mix = taken_together(combined.astype(jnp.bfloat16), ("sect", *HEAD)).astype(jnp.float32)
     return (hidden_state + expert_mix).astype(jnp.bfloat16)
 
 
 def solution(mesh):
+    group = mesh.shape["sect"] * mesh.shape["head"] // KEY_VALUE_HEADS
+    fine = jax.sharding.Mesh(
+        mesh.devices.reshape(
+            mesh.shape["sect"], mesh.shape["batch"], mesh.shape["head"] // group, group
+        ),
+        ("sect", "batch", *HEAD),
+    )
     placed = (
-        P("batch", "head", "sect"),
+        P("batch", HEAD, "sect"),
         P("batch", None, None),
-        P("batch", ("sect", "head"), None, None),
+        P("batch", ("sect", *HEAD), None, None),
         P("batch"),
         P("batch", None, None),
-        P(("sect", "head"), "batch"),
+        P(("sect", *HEAD), "batch"),
         P(None, "batch"),
         P("batch"),
         P(),
         P(),
-        P(("sect", "batch"), None, None, "head"),
-        P(("sect", "batch"), "head", None),
+        P(("sect", "batch"), None, None, HEAD),
+        P(("sect", "batch"), HEAD, None),
     )
     return jax.shard_map(
-        on_device, mesh=mesh, in_specs=placed, out_specs=P(None, "batch"), check_vma=False
-    )
+        on_device, mesh=fine, in_specs=placed, out_specs=P(None, "batch"), check_vma=False
+    )

time: 133 us -> 146 us (1.098)
  waiting for transfers between devices: 44.6 us -> 54 us
  matrix products: 7.57 us -> 9.24 us
    all_to_all x1 -> x2, waiting for transfers between devices: 3.43 us -> 32 us  [the longest x1 29 us: on_device(): lax.all_to_all(outgoing_parts, ('batch', 'hq'), split_axis=0, concat_axis...]
    ppermute x2 -> x0, waiting for transfers between devices: 10.5 us -> none  [from_partner(): lax.ppermute(shard, axis, [(i, i ^ 1 << distance) for i in range(lax.axis...]
    all_to_all x1 -> x2, starting transfers between devices: 6.93 us -> 16.9 us  [the longest x1 9.98 us: on_device(): lax.all_to_all(outgoing_parts, ('batch', 'hq'), split_axis=0, concat_axis...]
    all_to_all x2 -> x1, waiting for transfers between devices: 19.5 us -> 11 us  [copy_for_each(): return lax.all_to_all(copies, axis, split_axis=0, concat_axis=0, tiled=True)]
    all_to_all x2 -> x1, starting transfers between devices: 12.5 us -> 5.36 us  [copy_for_each(): return lax.all_to_all(copies, axis, split_axis=0, concat_axis=0, tiled=True)]
  transfers between devices with their start and end apart: 7 -> 5, of which waited for: 7 -> 5; matrix products, arithmetic and copies ran while one was open for 12% -> 11% of each run, Pallas kernels for 0% -> 0%
where the time goes in v6:
time: 146 us; the launch traced here: 144 us
  waiting for transfers between devices  54 us (37%)
  starting transfers between devices  32.2 us (22%)
  blocking collectives  18.8 us (13%)
  local copies, waits for them, and re-layouts  15.9 us (11%)
  other arithmetic  12.9 us (9%)
  matrix products  9.24 us (6%)
    all_to_all x1, waiting for transfers between devices, on_device(): lax.all_to_all(outgoing_parts, ('batch', 'hq'), split_axis=0, concat_axis...  29 us
    all_to_all x1, blocking collectives, copy_for_each(): return lax.all_to_all(copies, axis, split_axis=0, concat_axis=0, tiled=True)  18.8 us
    all_to_all x1, waiting for transfers between devices, copy_for_each(): return lax.all_to_all(copies, axis, split_axis=0, concat_axis=0, tiled=True)  11 us
    all_to_all x1, starting transfers between devices, on_device(): lax.all_to_all(outgoing_parts, ('batch', 'hq'), split_axis=0, concat_axis...  9.98 us
    all_to_all x1, starting transfers between devices, on_device(): lax.all_to_all(per_target, HEAD, split_axis=0, concat_axis=0, tiled=True)  6.93 us
    all_to_all x1, waiting for transfers between devices, on_device(): lax.all_to_all(leaving.astype(jnp.bfloat16), 'batch', split_axis=2, conca...  6.08 us
    all_to_all x1, starting transfers between devices, copy_for_each(): return lax.all_to_all(copies, axis, split_axis=0, concat_axis=0, tiled=True)  5.36 us
    all_to_all x1, starting transfers between devices, on_device(): lax.all_to_all(leaving.astype(jnp.bfloat16), 'batch', split_axis=2, conca...  4.97 us
  transfers between devices with their start and end apart: 5, of which 5 were waited for; matrix products, arithmetic and copies ran while one was open for 11% of the time, Pallas kernels for 0%

profile of v6, /device:TPU:32, one launch (start us, length us, event | category | flops | bytes accessed | tf_op | source)
XLA Modules:
  0.0 143.5 jit_solution(18414346354531608546)
XLA Ops:
  0.0 0.7 reshape.253
  1.4 6.9 %all-to-all-start = ((bf16[8,6,2,128]{3,2,1,0:T(2,128)(2,1)}), bf16[8,6,2,128]{3,2,1,0:T(2,128)(2,1)S(1)}, u32[]{:S(2)}, u32[]{:S(2)}) async-start(bf16[8,6,2,128]{3,2,1,0:T(2,128)(2,1)} %bitcast.2), calls=%async_computation | async-start | bytes 49152 | tf_op jit(solution)/shard_map/all_to_all | solution.py:122
  8.3 0.7 constant_dynamic-slice_fusion.3
  9.6 3.2 %fusion.54 = (bf16[6,16,64,128]{3,2,1,0:T(8,128)(2,1)S(1)}, bf16[6,16,64,128]{3,2,1,0:T(8,128)(2,1)S(1)}) fusion(bf16[6,16,64,256]{3,2,1,0:T(8,128)(2,1)} %param.14), kind=kLoop, calls=%fused_computation.109 | loop fusion | bytes 6291456 | tf_op jit(solution)/shard_map/slice | solution.py:140
  13.0 3.0 %all-to-all-done = bf16[8,6,2,128]{3,2,1,0:T(2,128)(2,1)S(1)} async-done(((bf16[8,6,2,128]{3,2,1,0:T(2,128)(2,1)}), bf16[8,6,2,128]{3,2,1,0:T(2,128)(2,1)S(1)}, u32[]{:S(2)}, u32[]{:S(2)}) %all-to-all-start) | async-done | bytes 24608 | tf_op jit(solution)/shard_map/all_to_all | solution.py:122
  16.2 1.3 fusion.55
  17.5 1.2 fusion.15
  18.8 1.4 convolution_add_fusion
  20.5 1.1 broadcast_in_dim.78
  21.6 10.0 %all-to-all-start.1 = ((f32[64,26,128]{2,1,0:T(8,128)}), f32[64,26,128]{2,1,0:T(8,128)S(1)}, u32[]{:S(2)}, u32[]{:S(2)}) async-start(f32[64,26,128]{2,1,0:T(8,128)} %bitcast.16), calls=%async_computation.1 | async-start | bytes 2097152 | tf_op jit(solution)/shard_map/all_to_all | solution.py:186
  31.8 29.0 %all-to-all-done.1 = f32[64,26,128]{2,1,0:T(8,128)S(1)} async-done(((f32[64,26,128]{2,1,0:T(8,128)}), f32[64,26,128]{2,1,0:T(8,128)S(1)}, u32[]{:S(2)}, u32[]{:S(2)}) %all-to-all-start.1) | async-done | bytes 852000 | tf_op jit(solution)/shard_map/all_to_all | solution.py:186
  62.5 1.0 broadcast_in_dim.79
  63.5 5.4 %all-to-all-start.2 = ((bf16[16,96,256]{2,1,0:T(8,128)(2,1)}), bf16[16,96,256]{2,1,0:T(8,128)(2,1)S(1)}, u32[]{:S(2)}, u32[]{:S(2)}) async-start(bf16[16,96,256]{2,1,0:T(8,128)(2,1)} %broadcast_in_dim.79), calls=%async_computation.2 | async-start | bytes 1572864 | tf_op jit(solution)/shard_map/all_to_all | solution.py:20
  69.0 1.8 %reduce-window.6 = s32[64,6,128]{2,0,1:T(8,128)S(1)} reduce-window(s32[64,6,128]{2,0,1:T(8,128)S(1)} %fusion.24, s32[]{:T(128)} %constant.117.clone.1), window={size=1x1x128 pad=0_0x0_0x127_0}, to_apply=%region_7.8 | reduce-window | flops 6242304 | bytes 393220 | tf_op jit(solution)/shard_map/reduce-window
  71.4 0.8 fusion.2
  72.5 11.0 %all-to-all-done.2 = bf16[16,96,256]{2,1,0:T(8,128)(2,1)S(1)} async-done(((bf16[16,96,256]{2,1,0:T(8,128)(2,1)}), bf16[16,96,256]{2,1,0:T(8,128)(2,1)S(1)}, u32[]{:S(2)}, u32[]{:S(2)}) %all-to-all-start.2) | async-done | bytes 786464 | tf_op jit(solution)/shard_map/all_to_all | solution.py:20
  84.3 0.7 pad_maximum_fusion
  85.0 4.9 %all-to-all-start.3 = ((bf16[16,25,256]{2,1,0:T(8,128)(2,1)}), bf16[16,25,256]{2,1,0:T(8,128)(2,1)}, u32[]{:S(2)}, u32[]{:S(2)}) async-start(bf16[16,25,256]{2,1,0:T(8,128)(2,1)} %pad_maximum_fusion), calls=%async_computation.3 | async-start | bytes 524288 | tf_op jit(solution)/shard_map/all_to_all | solution.py:250
  90.0 3.4 %copy.147 = bf16[4096,384]{1,0:T(8,128)(2,1)S(1)} copy(bf16[4096,384]{0,1:T(8,128)(2,1)} %bitcast.140) | data formatting | bytes 6291456 | tf_op jit(solution)/shard_map/ecf,efd->ecd/dot_general | solution.py:265
  93.4 1.3 reduce_sum.100
  94.7 5.0 %all-to-all-done.3 = bf16[16,25,256]{2,1,0:T(8,128)(2,1)} async-done(((bf16[16,25,256]{2,1,0:T(8,128)(2,1)}), bf16[16,25,256]{2,1,0:T(8,128)(2,1)}, u32[]{:S(2)}, u32[]{:S(2)}) %all-to-all-start.3) | async-done | bytes 204832 | tf_op jit(solution)/shard_map/all_to_all | solution.py:250
  99.7 0.9 slice.68
  101.1 1.4 reshape.276
  102.5 1.2 reduce_sum.104
  104.3 3.8 %fusion.11 = f32[1,24,2,384]{3,1,2,0:T(8,128)S(1)} fusion(bf16[16,256,2,384]{3,2,1,0:T(2,128)(2,1)} %bitcast.162, bf16[16,25,256]{2,1,0:T(8,128)(2,1)} %all-to-all-done.3, f32[24]{0:T(128)S(1)} %add_rsqrt_fusion), kind=kOutput, calls=%fused_computation.16 | convolution fusion | flops 151013376 | bytes 6561888 | tf_op jit(solution)/shard_map/becd,ebdgf->ecgf/dot_general | solution.py:257
  108.2 1.9 %fusion.4 = bf16[1,24,16,256]{3,1,0,2:T(8,128)(2,1)} fusion(bf16[16,256,384]{2,1,0:T(8,128)(2,1)S(1)} %bitcast.134, f32[1,24,2,384]{3,1,2,0:T(8,128)S(1)} %fusion.11), kind=kOutput, calls=%fused_computation.11 | convolution fusion | flops 75651072 | bytes 3416064 | tf_op jit(solution)/shard_map/ecf,efd->ecd/dot_general | solution.py:265
  110.0 5.0 %all-to-all-start.4 = ((bf16[1,24,16,256]{3,1,0,2:T(8,128)(2,1)}), bf16[1,24,16,256]{3,1,0,2:T(8,128)(2,1)S(1)}, u32[]{:S(2)}, u32[]{:S(2)}) async-start(bf16[1,24,16,256]{3,1,0,2:T(8,128)(2,1)} %fusion.4), calls=%async_computation.4 | async-start | bytes 393216 | tf_op jit(solution)/shard_map/all_to_all | solution.py:270
  115.0 0.7 broadcast_divide_fusion
  115.8 1.6 %select_reduce_fusion = bf16[768,96]{0,1:T(8,128)(2,1)S(1)} fusion(f32[96,8]{1,0:T(8,128)S(1)} %copy.136, s32[96,8]{1,0:T(8,128)} %copy-done.2), kind=kLoop, calls=%fused_computation.2 | loop fusion | flops 1695744 | bytes 153600 | tf_op jit(solution)/shard_map/reduce_sum | solution.py:235
  117.6 6.1 %all-to-all-done.4 = bf16[1,24,16,256]{3,1,0,2:T(8,128)(2,1)S(1)} async-done(((bf16[1,24,16,256]{3,1,0,2:T(8,128)(2,1)}), bf16[1,24,16,256]{3,1,0,2:T(8,128)(2,1)S(1)}, u32[]{:S(2)}, u32[]{:S(2)}) %all-to-all-start.4) | async-done | bytes 196640 | tf_op jit(solution)/shard_map/all_to_all | solution.py:270
  124.0 18.8 %all_to_all.40 = bf16[16,96,256]{2,1,0:T(8,128)(2,1)S(1)} all-to-all(bf16[16,96,256]{2,1,0:T(8,128)(2,1)S(1)} %broadcast_in_dim.82), channel_id=1, replica_groups=mesh['sect'=2,'batch'=16,'htop'=2,'hq'=4] {'sect','htop','hq'}, dimensions={0} | all-to-all | bytes 1572864 | tf_op jit(solution)/shard_map/all_to_all | solution.py:20
  142.9 0.6 add_convert_fusion
  (76 shorter events, 7.4 us)
Async XLA Ops:
  0.0 62.3 %copy-start = (bf16[512,256]{1,0:T(8,128)(2,1)S(1)}, bf16[512,256]{1,0:T(8,128)(2,1)}, u32[]{:S(2)}) copy-start(bf16[512,256]{1,0:T(8,128)(2,1)} %param.17) | copy-start | bytes 786436
  1.4 14.6 %all-to-all-start = ((bf16[8,6,2,128]{3,2,1,0:T(2,128)(2,1)}), bf16[8,6,2,128]{3,2,1,0:T(2,128)(2,1)S(1)}, u32[]{:S(2)}, u32[]{:S(2)}) async-start(bf16[8,6,2,128]{3,2,1,0:T(2,128)(2,1)} %bitcast.2), calls=%async_computation | async-start | bytes 49152 | tf_op jit(solution)/shard_map/all_to_all | solution.py:122
  9.6 3.2 %copy-start.4 = (bf16[6,4,256]{2,1,0:T(4,128)(2,1)S(1)}, bf16[6,4,256]{2,1,0:T(4,128)(2,1)}, u32[]{:S(2)}) copy-start(bf16[6,4,256]{2,1,0:T(4,128)(2,1)} %param.13) | copy-start | bytes 36868
  9.6 3.3 %copy-start.6 = (s32[6]{0:T(128)S(1)}, s32[6]{0:T(128)}, u32[]{:S(2)}) copy-start(s32[6]{0:T(128)} %param.15) | copy-start | bytes 76
  18.8 12.9 %copy-start.3 = (s32[96,8]{0,1:T(8,128)S(1)}, s32[96,8]{0,1:T(8,128)}, u32[]{:S(2)}) copy-start(s32[96,8]{0,1:T(8,128)} %param.20) | copy-start | bytes 9220
  21.6 39.2 %all-to-all-start.1 = ((f32[64,26,128]{2,1,0:T(8,128)}), f32[64,26,128]{2,1,0:T(8,128)S(1)}, u32[]{:S(2)}, u32[]{:S(2)}) async-start(f32[64,26,128]{2,1,0:T(8,128)} %bitcast.16), calls=%async_computation.1 | async-start | bytes 2097152 | tf_op jit(solution)/shard_map/all_to_all | solution.py:186
  62.5 21.0 %copy-start.1 = (bf16[96,256]{1,0:T(8,128)(2,1)S(1)}, bf16[96,256]{1,0:T(8,128)(2,1)}, u32[]{:S(2)}) copy-start(bf16[96,256]{1,0:T(8,128)(2,1)} %param.18) | copy-start | bytes 147460
  63.5 20.2 %copy-start.5 = (f32[256]{0:T(256)S(1)}, f32[256]{0:T(256)}, u32[]{:S(2)}) copy-start(f32[256]{0:T(256)} %param.19) | copy-start | bytes 3076
  63.5 19.9 %all-to-all-start.2 = ((bf16[16,96,256]{2,1,0:T(8,128)(2,1)}), bf16[16,96,256]{2,1,0:T(8,128)(2,1)S(1)}, u32[]{:S(2)}, u32[]{:S(2)}) async-start(bf16[16,96,256]{2,1,0:T(8,128)(2,1)} %broadcast_in_dim.79), calls=%async_computation.2 | async-start | bytes 1572864 | tf_op jit(solution)/shard_map/all_to_all | solution.py:20
  71.4 18.6 %copy-start.2 = (s32[96,8]{1,0:T(8,128)}, s32[96,8]{1,0:T(8,128)S(1)}, u32[]{:S(2)}) copy-start(s32[96,8]{1,0:T(8,128)S(1)} %fusion.30) | copy-start | bytes 9220
  85.0 14.6 %all-to-all-start.3 = ((bf16[16,25,256]{2,1,0:T(8,128)(2,1)}), bf16[16,25,256]{2,1,0:T(8,128)(2,1)}, u32[]{:S(2)}, u32[]{:S(2)}) async-start(bf16[16,25,256]{2,1,0:T(8,128)(2,1)} %pad_maximum_fusion), calls=%async_computation.3 | async-start | bytes 524288 | tf_op jit(solution)/shard_map/all_to_all | solution.py:250
  110.0 13.7 %all-to-all-start.4 = ((bf16[1,24,16,256]{3,1,0,2:T(8,128)(2,1)}), bf16[1,24,16,256]{3,1,0,2:T(8,128)(2,1)S(1)}, u32[]{:S(2)}, u32[]{:S(2)}) async-start(bf16[1,24,16,256]{3,1,0,2:T(8,128)(2,1)} %fusion.4), calls=%async_computation.4 | async-start | bytes 393216 | tf_op jit(solution)/shard_map/all_to_all | solution.py:270

commit v7 on v5

--- a/solution.py
+++ b/solution.py
@@ -221,22 +221,17 @@
     square_parts = split_three(jnp.sum(hidden_state * hidden_state, axis=1))
     outgoing = jnp.dot(selector, scaled, preferred_element_type=jnp.float32).astype(jnp.bfloat16)
     slot_squares = jnp.dot(square_parts, selector.T, preferred_element_type=jnp.float32)
-    square_width = 3 * slot_dev
-    square_rows = -(-square_width // cols_dev)
     square_block = jnp.pad(
-        jnp.moveaxis(slot_squares.astype(jnp.bfloat16).reshape(3, batch_size, slot_dev), 0, 1)
-        .reshape(batch_size, square_width),
-        ((0, 0), (0, square_rows * cols_dev - square_width)),
-    ).reshape(batch_size, square_rows, cols_dev)
+        jnp.moveaxis(slot_squares.astype(jnp.bfloat16).reshape(3, batch_size, slot_dev), 0, 1),
+        ((0, 0), (0, 0), (0, cols_dev - slot_dev)),
+    )
     outgoing = jnp.concatenate(
         [outgoing.reshape(batch_size, slot_dev, cols_dev), square_block], axis=1
     )
     arrived = lax.all_to_all(outgoing, "batch", split_axis=0, concat_axis=0, tiled=True)
     rows = arrived[:, :slot_dev].reshape(batch_size, pair_local, capacity, cols_dev)
-    got_squares = arrived[:, slot_dev:].reshape(batch_size, -1)[:, :square_width]
-    squares = jnp.sum(
-        got_squares.reshape(batch_size * 3, slot_dev).astype(jnp.float32), axis=0
-    )
+    got_squares = arrived[:, slot_dev:, :slot_dev].astype(jnp.float32)
+    squares = jnp.sum(got_squares, axis=(0, 1))
     inverse = lax.rsqrt(squares / D + NORM_EPS).reshape(pair_local, capacity)
     mixture = jnp.einsum(
         "becd,ebdgf->ecgf",

time: 133 us -> 129 us (0.970)
  local copies, waits for them, and re-layouts: 16.3 us -> 14 us
  other arithmetic: 11.7 us -> 10.1 us
    convert_element_type x1 -> x0, local copies, waits for them, and re-layouts: 1.37 us -> none  [on_device(): got_squares.reshape(batch_size * 3, slot_dev).astype(jnp.float32)]
where the time goes in v7:
time: 129 us; the launch traced here: 127 us
  waiting for transfers between devices  44.6 us (35%)
  starting transfers between devices  31.2 us (24%)
  blocking collectives  18.9 us (15%)
  local copies, waits for them, and re-layouts  14 us (11%)
  other arithmetic  10.1 us (8%)
  matrix products  7.57 us (6%)
    all_to_all x2, waiting for transfers between devices, copy_for_each(): return lax.all_to_all(copies, axis, split_axis=0, concat_axis=0, tiled=True)  19.5 us
    all_to_all x1, blocking collectives, copy_for_each(): return lax.all_to_all(copies, axis, split_axis=0, concat_axis=0, tiled=True)  18.9 us
    all_to_all x2, starting transfers between devices, copy_for_each(): return lax.all_to_all(copies, axis, split_axis=0, concat_axis=0, tiled=True)  12.5 us
    ppermute x2, waiting for transfers between devices, from_partner(): lax.ppermute(shard, axis, [(i, i ^ 1 << distance) for i in range(lax.axis...  10.5 us
    all_to_all x1, starting transfers between devices, on_device(): lax.all_to_all(per_target, 'head', split_axis=0, concat_axis=0, tiled=True)  6.93 us
    all_to_all x1, waiting for transfers between devices, on_device(): lax.all_to_all(leaving.astype(jnp.bfloat16), 'batch', split_axis=2, conca...  6.09 us
    all_to_all x1, starting transfers between devices, on_device(): lax.all_to_all(outgoing, 'batch', split_axis=0, concat_axis=0, tiled=True)  5.48 us
    all_to_all x1, waiting for transfers between devices, on_device(): lax.all_to_all(outgoing, 'batch', split_axis=0, concat_axis=0, tiled=True)  5.03 us
  transfers between devices with their start and end apart: 7, of which 7 were waited for; matrix products, arithmetic and copies ran while one was open for 12% of the time, Pallas kernels for 0%

profile of v7, /device:TPU:32, one launch (start us, length us, event | category | flops | bytes accessed | tf_op | source)
XLA Modules:
  0.0 126.8 jit_solution(13013270757990722810)
XLA Ops:
  0.0 0.7 reshape.212
  0.8 0.6 broadcast_in_dim.80
  1.4 6.9 %all-to-all-start = ((bf16[8,6,2,128]{3,2,1,0:T(2,128)(2,1)}), bf16[8,6,2,128]{3,2,1,0:T(2,128)(2,1)S(1)}, u32[]{:S(2)}, u32[]{:S(2)}) async-start(bf16[8,6,2,128]{3,2,1,0:T(2,128)(2,1)} %bitcast.2), calls=%async_computation | async-start | bytes 49152 | tf_op jit(solution)/shard_map/all_to_all | solution.py:120
  8.3 0.7 constant_dynamic-slice_fusion.8
  9.6 2.7 %fusion.65 = (bf16[6,16,64,128]{3,2,1,0:T(8,128)(2,1)S(1)}, bf16[6,16,64,128]{3,2,1,0:T(8,128)(2,1)S(1)}) fusion(bf16[6,16,64,256]{3,2,1,0:T(8,128)(2,1)} %param.14), kind=kLoop, calls=%fused_computation.129 | loop fusion | bytes 6291456 | tf_op jit(solution)/shard_map/slice | solution.py:138
  12.6 3.4 %all-to-all-done = bf16[8,6,2,128]{3,2,1,0:T(2,128)(2,1)S(1)} async-done(((bf16[8,6,2,128]{3,2,1,0:T(2,128)(2,1)}), bf16[8,6,2,128]{3,2,1,0:T(2,128)(2,1)S(1)}, u32[]{:S(2)}, u32[]{:S(2)}) %all-to-all-start) | async-done | bytes 24608 | tf_op jit(solution)/shard_map/all_to_all | solution.py:120
  18.8 0.6 collective-permute-start
  19.7 3.3 %collective-permute-done = f32[6,8,130]{2,1,0:T(8,128)S(1)} collective-permute-done((f32[6,8,130]{2,1,0:T(8,128)S(1)}, f32[6,8,130]{2,1,0:T(8,128)S(1)}, u32[]{:S(2)}, u32[]{:S(2)}) %collective-permute-start) | collective-permute-done | bytes 24992 | tf_op jit(solution)/shard_map/ppermute | solution.py:33
  24.0 0.7 collective-permute-start.1
  24.8 7.3 %collective-permute-done.1 = f32[6,4,130]{0,1,2:T(4,128)S(1)} collective-permute-done((f32[6,4,130]{0,1,2:T(4,128)S(1)}, f32[6,4,130]{0,1,2:T(4,128)S(1)}, u32[]{:S(2)}, u32[]{:S(2)}) %collective-permute-start.1) | collective-permute-done | bytes 12512 | tf_op jit(solution)/shard_map/ppermute | solution.py:33
  32.3 0.7 broadcast_in_dim.87
  33.0 8.6 %all-to-all-start.1 = ((bf16[16,6,512]{2,1,0:T(8,128)(2,1)}), bf16[16,6,512]{2,1,0:T(8,128)(2,1)S(1)}, u32[]{:S(2)}, u32[]{:S(2)}) async-start(bf16[16,6,512]{2,1,0:T(8,128)(2,1)} %broadcast_in_dim.87), calls=%async_computation.1 | async-start | bytes 262144 | tf_op jit(solution)/shard_map/all_to_all | solution.py:18
  41.7 7.2 %all-to-all-done.1 = bf16[16,6,512]{2,1,0:T(8,128)(2,1)S(1)} async-done(((bf16[16,6,512]{2,1,0:T(8,128)(2,1)}), bf16[16,6,512]{2,1,0:T(8,128)(2,1)S(1)}, u32[]{:S(2)}, u32[]{:S(2)}) %all-to-all-start.1) | async-done | bytes 98336 | tf_op jit(solution)/shard_map/all_to_all | solution.py:18
  49.2 1.0 broadcast_in_dim.88
  50.1 3.9 %all-to-all-start.2 = ((bf16[16,96,256]{2,1,0:T(8,128)(2,1)}), bf16[16,96,256]{2,1,0:T(8,128)(2,1)S(1)}, u32[]{:S(2)}, u32[]{:S(2)}) async-start(bf16[16,96,256]{2,1,0:T(8,128)(2,1)} %broadcast_in_dim.88), calls=%async_computation.2 | async-start | bytes 1572864 | tf_op jit(solution)/shard_map/all_to_all | solution.py:18
  54.2 1.8 %reduce-window.6 = s32[64,6,128]{2,0,1:T(8,128)S(1)} reduce-window(s32[64,6,128]{2,0,1:T(8,128)S(1)} %fusion.28, s32[]{:T(128)} %constant.114.clone.1), window={size=1x1x128 pad=0_0x0_0x127_0}, to_apply=%region_4.5 | reduce-window | flops 6242304 | bytes 393220 | tf_op jit(solution)/shard_map/reduce-window
  56.6 0.8 fusion.2
  57.7 12.4 %all-to-all-done.2 = bf16[16,96,256]{2,1,0:T(8,128)(2,1)S(1)} async-done(((bf16[16,96,256]{2,1,0:T(8,128)(2,1)}), bf16[16,96,256]{2,1,0:T(8,128)(2,1)S(1)}, u32[]{:S(2)}, u32[]{:S(2)}) %all-to-all-start.2) | async-done | bytes 786464 | tf_op jit(solution)/shard_map/all_to_all | solution.py:18
  70.7 0.7 fusion.17
  71.5 5.5 %all-to-all-start.3 = ((bf16[16,27,256]{2,1,0:T(8,128)(2,1)}), bf16[16,27,256]{2,1,0:T(8,128)(2,1)}, u32[]{:S(2)}, u32[]{:S(2)}) async-start(bf16[16,27,256]{2,1,0:T(8,128)(2,1)} %fusion.17), calls=%async_computation.3 | async-start | bytes 524288 | tf_op jit(solution)/shard_map/all_to_all | solution.py:231
  77.0 3.4 %copy.249 = bf16[4096,384]{1,0:T(8,128)(2,1)S(1)} copy(bf16[4096,384]{0,1:T(8,128)(2,1)} %bitcast.125) | data formatting | bytes 6291456 | tf_op jit(solution)/shard_map/ecf,efd->ecd/dot_general | solution.py:244
  80.4 1.3 %reduce_sum.80 = f32[96]{0:T(128)} reduce(f32[96,8]{0,1:T(8,128)} %param.21, f32[]{:T(128)} %constant.129.clone.1), dimensions={1}, to_apply=%region_7.8 | reduce | flops 672 | bytes 3460 | tf_op jit(solution)/shard_map/reduce_sum | solution.py:218
  81.7 5.0 %all-to-all-done.3 = bf16[16,27,256]{2,1,0:T(8,128)(2,1)} async-done(((bf16[16,27,256]{2,1,0:T(8,128)(2,1)}), bf16[16,27,256]{2,1,0:T(8,128)(2,1)}, u32[]{:S(2)}, u32[]{:S(2)}) %all-to-all-start.3) | async-done | bytes 221216 | tf_op jit(solution)/shard_map/all_to_all | solution.py:231
  86.7 0.8 convert_reduce_fusion.2
  87.5 3.8 %fusion.11 = f32[1,24,2,384]{3,1,2,0:T(8,128)S(1)} fusion(bf16[16,256,2,384]{3,2,1,0:T(2,128)(2,1)} %bitcast.145, bf16[16,27,256]{2,1,0:T(8,128)(2,1)} %all-to-all-done.3, f32[24]{0:T(128)S(1)} %add_rsqrt_fusion), kind=kOutput, calls=%fused_computation.16 | convolution fusion | flops 151013376 | bytes 6561888 | tf_op jit(solution)/shard_map/becd,ebdgf->ecgf/dot_general | solution.py:236
  91.4 1.9 %fusion.4 = bf16[1,24,16,256]{3,1,0,2:T(8,128)(2,1)} fusion(bf16[16,256,384]{2,1,0:T(8,128)(2,1)S(1)} %bitcast.122, f32[1,24,2,384]{3,1,2,0:T(8,128)S(1)} %fusion.11), kind=kOutput, calls=%fused_computation.11 | convolution fusion | flops 75651072 | bytes 3416064 | tf_op jit(solution)/shard_map/ecf,efd->ecd/dot_general | solution.py:244
  93.2 5.0 %all-to-all-start.4 = ((bf16[1,24,16,256]{3,1,0,2:T(8,128)(2,1)}), bf16[1,24,16,256]{3,1,0,2:T(8,128)(2,1)S(1)}, u32[]{:S(2)}, u32[]{:S(2)}) async-start(bf16[1,24,16,256]{3,1,0,2:T(8,128)(2,1)} %fusion.4), calls=%async_computation.4 | async-start | bytes 393216 | tf_op jit(solution)/shard_map/all_to_all | solution.py:249
  98.2 0.7 broadcast_divide_fusion
  99.0 1.6 %select_reduce_fusion = bf16[768,96]{0,1:T(8,128)(2,1)S(1)} fusion(f32[96,8]{1,0:T(8,128)S(1)} %copy.237, s32[96,8]{1,0:T(8,128)} %copy-done.2), kind=kLoop, calls=%fused_computation.2 | loop fusion | flops 1695744 | bytes 153600 | tf_op jit(solution)/shard_map/reduce_sum | solution.py:219
  100.8 6.1 %all-to-all-done.4 = bf16[1,24,16,256]{3,1,0,2:T(8,128)(2,1)S(1)} async-done(((bf16[1,24,16,256]{3,1,0,2:T(8,128)(2,1)}), bf16[1,24,16,256]{3,1,0,2:T(8,128)(2,1)S(1)}, u32[]{:S(2)}, u32[]{:S(2)}) %all-to-all-start.4) | async-done | bytes 196640 | tf_op jit(solution)/shard_map/all_to_all | solution.py:249
  107.2 18.9 %all_to_all.40 = bf16[16,96,256]{2,1,0:T(8,128)(2,1)S(1)} all-to-all(bf16[16,96,256]{2,1,0:T(8,128)(2,1)S(1)} %broadcast_in_dim.91), channel_id=1, replica_groups=mesh['sect'=2,'batch'=16,'head'=8] {'sect','head'}, dimensions={0} | all-to-all | bytes 1572864 | tf_op jit(solution)/shard_map/all_to_all | solution.py:18
  126.2 0.6 add_convert_fusion
  (86 shorter events, 7.8 us)
Async XLA Ops:
  0.0 49.0 %copy-start = (bf16[512,256]{1,0:T(8,128)(2,1)S(1)}, bf16[512,256]{1,0:T(8,128)(2,1)}, u32[]{:S(2)}) copy-start(bf16[512,256]{1,0:T(8,128)(2,1)} %param.17) | copy-start | bytes 786436
  1.4 14.6 %all-to-all-start = ((bf16[8,6,2,128]{3,2,1,0:T(2,128)(2,1)}), bf16[8,6,2,128]{3,2,1,0:T(2,128)(2,1)S(1)}, u32[]{:S(2)}, u32[]{:S(2)}) async-start(bf16[8,6,2,128]{3,2,1,0:T(2,128)(2,1)} %bitcast.2), calls=%async_computation | async-start | bytes 49152 | tf_op jit(solution)/shard_map/all_to_all | solution.py:120
  9.6 2.7 %copy-start.4 = (bf16[6,4,256]{2,1,0:T(4,128)(2,1)S(1)}, bf16[6,4,256]{2,1,0:T(4,128)(2,1)}, u32[]{:S(2)}) copy-start(bf16[6,4,256]{2,1,0:T(4,128)(2,1)} %param.13) | copy-start | bytes 36868
  9.6 2.8 %copy-start.6 = (s32[6]{0:T(128)S(1)}, s32[6]{0:T(128)}, u32[]{:S(2)}) copy-start(s32[6]{0:T(128)} %param.15) | copy-start | bytes 76
  18.8 4.2 %collective-permute-start = (f32[6,8,130]{2,1,0:T(8,128)S(1)}, f32[6,8,130]{2,1,0:T(8,128)S(1)}, u32[]{:S(2)}, u32[]{:S(2)}) collective-permute-start(f32[6,8,130]{2,1,0:T(8,128)S(1)} %copy.218), channel_id=1, source_target_pairs={{0,2},{1,3},{2,0},{3,1},{4,6},{5,7},{6,4},{7,5},{8,10},{9,11},{10,... | collective-permute-start | bytes 74888 | tf_op jit(solution)/shard_map/ppermute | solution.py:33
  23.6 17.9 %copy-start.3 = (s32[96,8]{0,1:T(8,128)S(1)}, s32[96,8]{0,1:T(8,128)}, u32[]{:S(2)}) copy-start(s32[96,8]{0,1:T(8,128)} %param.20) | copy-start | bytes 9220
  24.0 8.0 %collective-permute-start.1 = (f32[6,4,130]{0,1,2:T(4,128)S(1)}, f32[6,4,130]{0,1,2:T(4,128)S(1)}, u32[]{:S(2)}, u32[]{:S(2)}) collective-permute-start(f32[6,4,130]{0,1,2:T(4,128)S(1)} %constant_dynamic-slice_fusion.4), channel_id=1, source_target_pairs={{0,1},{1,0},{2,3},{3,2},{4,5},{5,4},{6,7},{7,6},{8,9},{9,8},{10,11... | collective-permute-start | bytes 37448 | tf_op jit(solution)/shard_map/ppermute | solution.py:33
  33.0 16.0 %all-to-all-start.1 = ((bf16[16,6,512]{2,1,0:T(8,128)(2,1)}), bf16[16,6,512]{2,1,0:T(8,128)(2,1)S(1)}, u32[]{:S(2)}, u32[]{:S(2)}) async-start(bf16[16,6,512]{2,1,0:T(8,128)(2,1)} %broadcast_in_dim.87), calls=%async_computation.1 | async-start | bytes 262144 | tf_op jit(solution)/shard_map/all_to_all | solution.py:18
  50.1 19.9 %all-to-all-start.2 = ((bf16[16,96,256]{2,1,0:T(8,128)(2,1)}), bf16[16,96,256]{2,1,0:T(8,128)(2,1)S(1)}, u32[]{:S(2)}, u32[]{:S(2)}) async-start(bf16[16,96,256]{2,1,0:T(8,128)(2,1)} %broadcast_in_dim.88), calls=%async_computation.2 | async-start | bytes 1572864 | tf_op jit(solution)/shard_map/all_to_all | solution.py:18
  54.0 16.1 %copy-start.1 = (bf16[96,256]{1,0:T(8,128)(2,1)S(1)}, bf16[96,256]{1,0:T(8,128)(2,1)}, u32[]{:S(2)}) copy-start(bf16[96,256]{1,0:T(8,128)(2,1)} %param.18) | copy-start | bytes 147460
  54.0 16.2 %copy-start.5 = (f32[256]{0:T(256)S(1)}, f32[256]{0:T(256)}, u32[]{:S(2)}) copy-start(f32[256]{0:T(256)} %param.19) | copy-start | bytes 3076
  56.6 1.1 copy-start.2
  71.5 15.2 %all-to-all-start.3 = ((bf16[16,27,256]{2,1,0:T(8,128)(2,1)}), bf16[16,27,256]{2,1,0:T(8,128)(2,1)}, u32[]{:S(2)}, u32[]{:S(2)}) async-start(bf16[16,27,256]{2,1,0:T(8,128)(2,1)} %fusion.17), calls=%async_computation.3 | async-start | bytes 524288 | tf_op jit(solution)/shard_map/all_to_all | solution.py:231
  93.2 13.7 %all-to-all-start.4 = ((bf16[1,24,16,256]{3,1,0,2:T(8,128)(2,1)}), bf16[1,24,16,256]{3,1,0,2:T(8,128)(2,1)S(1)}, u32[]{:S(2)}, u32[]{:S(2)}) async-start(bf16[1,24,16,256]{3,1,0,2:T(8,128)(2,1)} %fusion.4), calls=%async_computation.4 | async-start | bytes 393216 | tf_op jit(solution)/shard_map/all_to_all | solution.py:249

commit v8 on v7

--- a/solution.py
+++ b/solution.py
@@ -74,7 +74,7 @@
             joined[..., None],
             (first_sum * first_factor + second_sum * second_factor)[..., None],
         ],
-        axis=2,
+        axis=-1,
     )
 
 
@@ -168,11 +168,12 @@
     ] * newest_entry[:, None, head_dim:].astype(jnp.float32)
     packed = jnp.concatenate([weighted, running_max[..., None], running_sum[..., None]], axis=2)
     bit_count = group_size.bit_length() - 1
-    for bit_index in reversed(range(bit_count)):
-        half_heads = packed.shape[1] // 2
+    packed = packed.reshape(seq_count, *([2] * bit_count), heads_dev, head_dim + 2)
+    for bit_index in range(bit_count):
+        bit_axis = bit_count - bit_index
         keep_half = quarter >> bit_index & 1
-        kept = lax.dynamic_slice_in_dim(packed, keep_half * half_heads, half_heads, 1)
-        sent = lax.dynamic_slice_in_dim(packed, (1 - keep_half) * half_heads, half_heads, 1)
+        kept = lax.dynamic_index_in_dim(packed, keep_half, bit_axis, keepdims=False)
+        sent = lax.dynamic_index_in_dim(packed, 1 - keep_half, bit_axis, keepdims=False)
         partner = from_partner(sent, "head", bit_index)
         packed = merge_packed(kept, partner, head_dim)
     attention = (

time: 129 us -> 132 us (1.023)
  matrix products: 7.57 us -> 9.24 us
  transfers between devices with their start and end apart: 7 -> 7, of which waited for: 7 -> 7; matrix products, arithmetic and copies ran while one was open for 12% -> 13% of each run, Pallas kernels for 0% -> 0%
where the time goes in v8:
time: 132 us; the launch traced here: 130 us
  waiting for transfers between devices  43.8 us (33%)
  starting transfers between devices  31.8 us (24%)
  blocking collectives  18.9 us (14%)
  local copies, waits for them, and re-layouts  14.6 us (11%)
  other arithmetic  11 us (8%)
  matrix products  9.24 us (7%)
    all_to_all x2, waiting for transfers between devices, copy_for_each(): return lax.all_to_all(copies, axis, split_axis=0, concat_axis=0, tiled=True)  19.6 us
    all_to_all x1, blocking collectives, copy_for_each(): return lax.all_to_all(copies, axis, split_axis=0, concat_axis=0, tiled=True)  18.9 us
    all_to_all x2, starting transfers between devices, copy_for_each(): return lax.all_to_all(copies, axis, split_axis=0, concat_axis=0, tiled=True)  13 us
    ppermute x2, waiting for transfers between devices, from_partner(): lax.ppermute(shard, axis, [(i, i ^ 1 << distance) for i in range(lax.axis...  10.1 us
    all_to_all x1, starting transfers between devices, on_device(): lax.all_to_all(per_target, 'head', split_axis=0, concat_axis=0, tiled=True)  6.93 us
    all_to_all x1, waiting for transfers between devices, on_device(): lax.all_to_all(leaving.astype(jnp.bfloat16), 'batch', split_axis=2, conca...  6.09 us
    all_to_all x1, starting transfers between devices, on_device(): lax.all_to_all(outgoing, 'batch', split_axis=0, concat_axis=0, tiled=True)  5.48 us
    all_to_all x1, waiting for transfers between devices, on_device(): lax.all_to_all(outgoing, 'batch', split_axis=0, concat_axis=0, tiled=True)  5.03 us
  transfers between devices with their start and end apart: 7, of which 7 were waited for; matrix products, arithmetic and copies ran while one was open for 13% of the time, Pallas kernels for 0%

profile of v8, /device:TPU:32, one launch (start us, length us, event | category | flops | bytes accessed | tf_op | source)
XLA Modules:
  0.0 129.8 jit_solution(2350427617278809410)
XLA Ops:
  0.0 0.7 reshape.218
  1.4 6.9 %all-to-all-start = ((bf16[8,6,2,128]{3,2,1,0:T(2,128)(2,1)}), bf16[8,6,2,128]{3,2,1,0:T(2,128)(2,1)S(1)}, u32[]{:S(2)}, u32[]{:S(2)}) async-start(bf16[8,6,2,128]{3,2,1,0:T(2,128)(2,1)} %bitcast.2), calls=%async_computation | async-start | bytes 49152 | tf_op jit(solution)/shard_map/all_to_all | solution.py:120
  8.3 0.7 constant_dynamic-slice_fusion.6
  9.6 3.2 %fusion.63 = (bf16[6,16,64,128]{3,2,1,0:T(8,128)(2,1)S(1)}, bf16[6,16,64,128]{3,2,1,0:T(8,128)(2,1)S(1)}) fusion(bf16[6,16,64,256]{3,2,1,0:T(8,128)(2,1)} %param.14), kind=kLoop, calls=%fused_computation.128 | loop fusion | bytes 6291456 | tf_op jit(solution)/shard_map/slice | solution.py:138
  13.0 3.0 %all-to-all-done = bf16[8,6,2,128]{3,2,1,0:T(2,128)(2,1)S(1)} async-done(((bf16[8,6,2,128]{3,2,1,0:T(2,128)(2,1)}), bf16[8,6,2,128]{3,2,1,0:T(2,128)(2,1)S(1)}, u32[]{:S(2)}, u32[]{:S(2)}) %all-to-all-start) | async-done | bytes 24608 | tf_op jit(solution)/shard_map/all_to_all | solution.py:120
  16.2 1.3 fusion.65
  17.5 1.2 fusion.15
  19.3 1.4 %convolution_add_fusion = f32[6,16,128]{2,1,0:T(8,128)S(1)} fusion(bf16[6,1024,128]{2,1,0:T(8,128)(2,1)S(1)} %bitcast.131, f32[6,16,1024]{2,1,0:T(8,128)} %get-tuple-element.28, f32[6,16]{1,0:T(8,128)S(1)} %fusion.42, pred[6,1024]{1,0:T(8,128)(4,1)S(1)} %compare_and_fusion, f32[6,128]{1,0:T(8,128)S(1)} %get-tuple-element.22, f32[6,16]{1,0:T(8,128)S(1)} %get-tuple-element.20), kind=kOutput, calls=%fused_computation.17 | convolution fusion | flops 25485312 | bytes 2025216 | tf_op jit(solution)/shard_map/shk,skd->shd/dot_general | solution.py:160
  20.8 0.7 collective-permute-start
  22.0 4.5 %collective-permute-done = f32[6,2,4,130]{3,2,1,0:T(4,128)S(1)} collective-permute-done((f32[6,2,4,130]{3,2,1,0:T(4,128)S(1)}, f32[6,2,4,130]{3,2,1,0:T(4,128)S(1)}, u32[]{:S(2)}, u32[]{:S(2)}) %collective-permute-start) | collective-permute-done | bytes 24992 | tf_op jit(solution)/shard_map/ppermute | solution.py:33
  28.9 5.6 %collective-permute-done.1 = f32[6,4,130]{0,1,2:T(4,128)S(1)} collective-permute-done((f32[6,4,130]{0,1,2:T(4,128)S(1)}, f32[6,4,130]{0,1,2:T(4,128)S(1)}, u32[]{:S(2)}, u32[]{:S(2)}) %collective-permute-start.1) | collective-permute-done | bytes 12512 | tf_op jit(solution)/shard_map/ppermute | solution.py:33
  34.7 0.7 broadcast_in_dim.81
  35.4 8.6 %all-to-all-start.1 = ((bf16[16,6,512]{2,1,0:T(8,128)(2,1)}), bf16[16,6,512]{2,1,0:T(8,128)(2,1)S(1)}, u32[]{:S(2)}, u32[]{:S(2)}) async-start(bf16[16,6,512]{2,1,0:T(8,128)(2,1)} %broadcast_in_dim.81), calls=%async_computation.1 | async-start | bytes 262144 | tf_op jit(solution)/shard_map/all_to_all | solution.py:18
  44.2 7.2 %all-to-all-done.1 = bf16[16,6,512]{2,1,0:T(8,128)(2,1)S(1)} async-done(((bf16[16,6,512]{2,1,0:T(8,128)(2,1)}), bf16[16,6,512]{2,1,0:T(8,128)(2,1)S(1)}, u32[]{:S(2)}, u32[]{:S(2)}) %all-to-all-start.1) | async-done | bytes 98336 | tf_op jit(solution)/shard_map/all_to_all | solution.py:18
  51.6 1.0 broadcast_in_dim.82
  52.6 4.4 %all-to-all-start.2 = ((bf16[16,96,256]{2,1,0:T(8,128)(2,1)}), bf16[16,96,256]{2,1,0:T(8,128)(2,1)S(1)}, u32[]{:S(2)}, u32[]{:S(2)}) async-start(bf16[16,96,256]{2,1,0:T(8,128)(2,1)} %broadcast_in_dim.82), calls=%async_computation.2 | async-start | bytes 1572864 | tf_op jit(solution)/shard_map/all_to_all | solution.py:18
  57.2 1.8 %reduce-window.6 = s32[64,6,128]{2,0,1:T(8,128)S(1)} reduce-window(s32[64,6,128]{2,0,1:T(8,128)S(1)} %fusion.27, s32[]{:T(128)} %constant.128.clone.1), window={size=1x1x128 pad=0_0x0_0x127_0}, to_apply=%region_4.5 | reduce-window | flops 6242304 | bytes 393220 | tf_op jit(solution)/shard_map/reduce-window
  59.6 0.8 fusion.2
  60.6 12.4 %all-to-all-done.2 = bf16[16,96,256]{2,1,0:T(8,128)(2,1)S(1)} async-done(((bf16[16,96,256]{2,1,0:T(8,128)(2,1)}), bf16[16,96,256]{2,1,0:T(8,128)(2,1)S(1)}, u32[]{:S(2)}, u32[]{:S(2)}) %all-to-all-start.2) | async-done | bytes 786464 | tf_op jit(solution)/shard_map/all_to_all | solution.py:18
  73.7 0.7 fusion.17
  74.5 5.5 %all-to-all-start.3 = ((bf16[16,27,256]{2,1,0:T(8,128)(2,1)}), bf16[16,27,256]{2,1,0:T(8,128)(2,1)}, u32[]{:S(2)}, u32[]{:S(2)}) async-start(bf16[16,27,256]{2,1,0:T(8,128)(2,1)} %fusion.17), calls=%async_computation.3 | async-start | bytes 524288 | tf_op jit(solution)/shard_map/all_to_all | solution.py:232
  80.0 3.4 %copy.213 = bf16[4096,384]{1,0:T(8,128)(2,1)S(1)} copy(bf16[4096,384]{0,1:T(8,128)(2,1)} %bitcast.133) | data formatting | bytes 6291456 | tf_op jit(solution)/shard_map/ecf,efd->ecd/dot_general | solution.py:245
  83.4 1.3 reduce_sum.80
  84.7 5.0 %all-to-all-done.3 = bf16[16,27,256]{2,1,0:T(8,128)(2,1)} async-done(((bf16[16,27,256]{2,1,0:T(8,128)(2,1)}), bf16[16,27,256]{2,1,0:T(8,128)(2,1)}, u32[]{:S(2)}, u32[]{:S(2)}) %all-to-all-start.3) | async-done | bytes 221216 | tf_op jit(solution)/shard_map/all_to_all | solution.py:232
  89.7 0.8 convert_reduce_fusion.2
  90.5 3.8 %fusion.11 = f32[1,24,2,384]{3,1,2,0:T(8,128)S(1)} fusion(bf16[16,256,2,384]{3,2,1,0:T(2,128)(2,1)} %bitcast.161, bf16[16,27,256]{2,1,0:T(8,128)(2,1)} %all-to-all-done.3, f32[24]{0:T(128)S(1)} %add_rsqrt_fusion), kind=kOutput, calls=%fused_computation.16 | convolution fusion | flops 151013376 | bytes 6561888 | tf_op jit(solution)/shard_map/becd,ebdgf->ecgf/dot_general | solution.py:237
  94.3 1.9 %fusion.4 = bf16[1,24,16,256]{3,1,0,2:T(8,128)(2,1)} fusion(bf16[16,256,384]{2,1,0:T(8,128)(2,1)S(1)} %bitcast.130, f32[1,24,2,384]{3,1,2,0:T(8,128)S(1)} %fusion.11), kind=kOutput, calls=%fused_computation.11 | convolution fusion | flops 75651072 | bytes 3416064 | tf_op jit(solution)/shard_map/ecf,efd->ecd/dot_general | solution.py:245
  96.2 5.0 %all-to-all-start.4 = ((bf16[1,24,16,256]{3,1,0,2:T(8,128)(2,1)}), bf16[1,24,16,256]{3,1,0,2:T(8,128)(2,1)S(1)}, u32[]{:S(2)}, u32[]{:S(2)}) async-start(bf16[1,24,16,256]{3,1,0,2:T(8,128)(2,1)} %fusion.4), calls=%async_computation.4 | async-start | bytes 393216 | tf_op jit(solution)/shard_map/all_to_all | solution.py:250
  101.2 0.7 broadcast_divide_fusion
  102.0 1.6 %select_reduce_fusion = bf16[768,96]{0,1:T(8,128)(2,1)S(1)} fusion(f32[96,8]{1,0:T(8,128)S(1)} %copy.203, s32[96,8]{1,0:T(8,128)} %copy-done.2), kind=kLoop, calls=%fused_computation.2 | loop fusion | flops 1695744 | bytes 153600 | tf_op jit(solution)/shard_map/reduce_sum | solution.py:220
  103.8 6.1 %all-to-all-done.4 = bf16[1,24,16,256]{3,1,0,2:T(8,128)(2,1)S(1)} async-done(((bf16[1,24,16,256]{3,1,0,2:T(8,128)(2,1)}), bf16[1,24,16,256]{3,1,0,2:T(8,128)(2,1)S(1)}, u32[]{:S(2)}, u32[]{:S(2)}) %all-to-all-start.4) | async-done | bytes 196640 | tf_op jit(solution)/shard_map/all_to_all | solution.py:250
  110.2 18.9 %all_to_all.40 = bf16[16,96,256]{2,1,0:T(8,128)(2,1)S(1)} all-to-all(bf16[16,96,256]{2,1,0:T(8,128)(2,1)S(1)} %broadcast_in_dim.85), channel_id=1, replica_groups=mesh['sect'=2,'batch'=16,'head'=8] {'sect','head'}, dimensions={0} | all-to-all | bytes 1572864 | tf_op jit(solution)/shard_map/all_to_all | solution.py:18
  (86 shorter events, 8.5 us)
Async XLA Ops:
  0.0 51.4 %copy-start = (bf16[512,256]{1,0:T(8,128)(2,1)S(1)}, bf16[512,256]{1,0:T(8,128)(2,1)}, u32[]{:S(2)}) copy-start(bf16[512,256]{1,0:T(8,128)(2,1)} %param.17) | copy-start | bytes 786436
  1.4 14.6 %all-to-all-start = ((bf16[8,6,2,128]{3,2,1,0:T(2,128)(2,1)}), bf16[8,6,2,128]{3,2,1,0:T(2,128)(2,1)S(1)}, u32[]{:S(2)}, u32[]{:S(2)}) async-start(bf16[8,6,2,128]{3,2,1,0:T(2,128)(2,1)} %bitcast.2), calls=%async_computation | async-start | bytes 49152 | tf_op jit(solution)/shard_map/all_to_all | solution.py:120
  9.6 3.2 %copy-start.4 = (bf16[6,4,256]{2,1,0:T(4,128)(2,1)S(1)}, bf16[6,4,256]{2,1,0:T(4,128)(2,1)}, u32[]{:S(2)}) copy-start(bf16[6,4,256]{2,1,0:T(4,128)(2,1)} %param.13) | copy-start | bytes 36868
  9.6 3.3 %copy-start.6 = (s32[6]{0:T(128)S(1)}, s32[6]{0:T(128)}, u32[]{:S(2)}) copy-start(s32[6]{0:T(128)} %param.15) | copy-start | bytes 76
  20.8 23.2 %copy-start.3 = (s32[96,8]{0,1:T(8,128)S(1)}, s32[96,8]{0,1:T(8,128)}, u32[]{:S(2)}) copy-start(s32[96,8]{0,1:T(8,128)} %param.20) | copy-start | bytes 9220
  20.8 5.7 %collective-permute-start = (f32[6,2,4,130]{3,2,1,0:T(4,128)S(1)}, f32[6,2,4,130]{3,2,1,0:T(4,128)S(1)}, u32[]{:S(2)}, u32[]{:S(2)}) collective-permute-start(f32[6,2,4,130]{3,2,1,0:T(4,128)S(1)} %get-tuple-element.14), channel_id=1, source_target_pairs={{0,1},{1,0},{2,3},{3,2},{4,5},{5,4},{6,7},{7,6},{8,9},{9,8},{10,11... | collective-permute-start | bytes 74888 | tf_op jit(solution)/shard_map/ppermute | solution.py:33
  28.0 6.5 %collective-permute-start.1 = (f32[6,4,130]{0,1,2:T(4,128)S(1)}, f32[6,4,130]{0,1,2:T(4,128)S(1)}, u32[]{:S(2)}, u32[]{:S(2)}) collective-permute-start(f32[6,4,130]{0,1,2:T(4,128)S(1)} %bitcast.144), channel_id=1, source_target_pairs={{0,2},{1,3},{2,0},{3,1},{4,6},{5,7},{6,4},{7,5},{8,10},{9,11},{10,... | collective-permute-start | bytes 37448 | tf_op jit(solution)/shard_map/ppermute | solution.py:33
  35.4 16.0 %all-to-all-start.1 = ((bf16[16,6,512]{2,1,0:T(8,128)(2,1)}), bf16[16,6,512]{2,1,0:T(8,128)(2,1)S(1)}, u32[]{:S(2)}, u32[]{:S(2)}) async-start(bf16[16,6,512]{2,1,0:T(8,128)(2,1)} %broadcast_in_dim.81), calls=%async_computation.1 | async-start | bytes 262144 | tf_op jit(solution)/shard_map/all_to_all | solution.py:18
  51.6 21.5 %copy-start.1 = (bf16[96,256]{1,0:T(8,128)(2,1)S(1)}, bf16[96,256]{1,0:T(8,128)(2,1)}, u32[]{:S(2)}) copy-start(bf16[96,256]{1,0:T(8,128)(2,1)} %param.18) | copy-start | bytes 147460
  52.6 20.7 %copy-start.5 = (f32[256]{0:T(256)S(1)}, f32[256]{0:T(256)}, u32[]{:S(2)}) copy-start(f32[256]{0:T(256)} %param.19) | copy-start | bytes 3076
  52.6 20.4 %all-to-all-start.2 = ((bf16[16,96,256]{2,1,0:T(8,128)(2,1)}), bf16[16,96,256]{2,1,0:T(8,128)(2,1)S(1)}, u32[]{:S(2)}, u32[]{:S(2)}) async-start(bf16[16,96,256]{2,1,0:T(8,128)(2,1)} %broadcast_in_dim.82), calls=%async_computation.2 | async-start | bytes 1572864 | tf_op jit(solution)/shard_map/all_to_all | solution.py:18
  59.6 1.1 copy-start.2
  74.5 15.2 %all-to-all-start.3 = ((bf16[16,27,256]{2,1,0:T(8,128)(2,1)}), bf16[16,27,256]{2,1,0:T(8,128)(2,1)}, u32[]{:S(2)}, u32[]{:S(2)}) async-start(bf16[16,27,256]{2,1,0:T(8,128)(2,1)} %fusion.17), calls=%async_computation.3 | async-start | bytes 524288 | tf_op jit(solution)/shard_map/all_to_all | solution.py:232
  96.2 13.7 %all-to-all-start.4 = ((bf16[1,24,16,256]{3,1,0,2:T(8,128)(2,1)}), bf16[1,24,16,256]{3,1,0,2:T(8,128)(2,1)S(1)}, u32[]{:S(2)}, u32[]{:S(2)}) async-start(bf16[1,24,16,256]{3,1,0,2:T(8,128)(2,1)} %fusion.4), calls=%async_computation.4 | async-start | bytes 393216 | tf_op jit(solution)/shard_map/all_to_all | solution.py:250

commit v9 on v7

--- a/solution.py
+++ b/solution.py
@@ -35,6 +35,16 @@
 
 def taken_together(shard, axis):
     return copy_for_each(shard, axis).astype(jnp.float32).sum(axis=0)
+
+
+def doubled_sum(shard, axis):
+    count = lax.axis_size(axis)
+    step = 1
+    while step < count:
+        partner = lax.ppermute(shard, axis, [(i, i ^ step) for i in range(count)])
+        shard = lax.reduce_precision(shard + partner, exponent_bits=8, mantissa_bits=7)
+        step *= 2
+    return shard
 
 
 def of_everyone(shard, axis):
@@ -183,7 +193,7 @@
     cols_dev = residual.shape[1]
     all_attention = gathered_copies(attention, "batch", 0)
     head_terms = jnp.dot(all_attention, out_weight, preferred_element_type=jnp.float32)
-    projected = taken_together(head_terms.astype(jnp.bfloat16), ("sect", "head")).astype(
+    projected = doubled_sum(head_terms.astype(jnp.bfloat16), ("sect", "head")).astype(
         jnp.float32
     )
     hidden_state = residual.astype(jnp.float32) + projected
@@ -257,7 +267,7 @@
     )
     weights_used = weights_used.reshape(token_count, send_count)
     combined = jnp.dot(weights_used, came_back, preferred_element_type=jnp.float32)
-    expert_mix = taken_together(combined.astype(jnp.bfloat16), ("sect", "head")).astype(jnp.float32)
+    expert_mix = doubled_sum(combined.astype(jnp.bfloat16), ("sect", "head")).astype(jnp.float32)
     return (hidden_state + expert_mix).astype(jnp.bfloat16)
 
 

time: 129 us -> 127 us (0.984); the launches traced: 127 us -> 126 us
  blocking collectives: 18.9 us -> 0 us
  waiting for transfers between devices: 44.6 us -> 61.2 us
  starting transfers between devices: 31.2 us -> 34.2 us
    ppermute x0 -> x8, waiting for transfers between devices: none -> 31.4 us  [doubled_sum(): partner = lax.ppermute(shard, axis, [(i, i ^ step) for i in range(count)])]
    all_to_all x1 -> x0, blocking collectives: 18.9 us -> none  [copy_for_each(): return lax.all_to_all(copies, axis, split_axis=0, concat_axis=0, tiled=True)]
    all_to_all x2 -> x1, waiting for transfers between devices: 19.5 us -> 5.15 us  [copy_for_each(): return lax.all_to_all(copies, axis, split_axis=0, concat_axis=0, tiled=True)]
    ppermute x0 -> x8, starting transfers between devices: none -> 6.97 us  [doubled_sum(): partner = lax.ppermute(shard, axis, [(i, i ^ step) for i in range(count)])]
    all_to_all x2 -> x1, starting transfers between devices: 12.5 us -> 8.59 us  [copy_for_each(): return lax.all_to_all(copies, axis, split_axis=0, concat_axis=0, tiled=True)]
  transfers between devices with their start and end apart: 7 -> 14, of which waited for: 7 -> 14; matrix products, arithmetic and copies ran while one was open for 12% -> 12% of each run, Pallas kernels for 0% -> 0%
where the time goes in v9:
time: 127 us; the launch traced here: 126 us
  waiting for transfers between devices  61.2 us (48%)
  starting transfers between devices  34.2 us (27%)
  local copies, waits for them, and re-layouts  13 us (10%)
  other arithmetic  9.99 us (8%)
  matrix products  7.59 us (6%)
    ppermute x8, waiting for transfers between devices, doubled_sum(): partner = lax.ppermute(shard, axis, [(i, i ^ step) for i in range(count)])  31.4 us
    ppermute x2, waiting for transfers between devices, from_partner(): lax.ppermute(shard, axis, [(i, i ^ 1 << distance) for i in range(lax.axis...  10.3 us
    all_to_all x1, starting transfers between devices, copy_for_each(): return lax.all_to_all(copies, axis, split_axis=0, concat_axis=0, tiled=True)  8.59 us
    ppermute x8, starting transfers between devices, doubled_sum(): partner = lax.ppermute(shard, axis, [(i, i ^ step) for i in range(count)])  6.97 us
    all_to_all x1, starting transfers between devices, on_device(): lax.all_to_all(per_target, 'head', split_axis=0, concat_axis=0, tiled=True)  6.93 us
    all_to_all x1, waiting for transfers between devices, on_device(): lax.all_to_all(leaving.astype(jnp.bfloat16), 'batch', split_axis=2, conca...  5.87 us
    all_to_all x1, starting transfers between devices, on_device(): lax.all_to_all(outgoing, 'batch', split_axis=0, concat_axis=0, tiled=True)  5.39 us
    all_to_all x1, waiting for transfers between devices, copy_for_each(): return lax.all_to_all(copies, axis, split_axis=0, concat_axis=0, tiled=True)  5.15 us
  transfers between devices with their start and end apart: 14, of which 14 were waited for; matrix products, arithmetic and copies ran while one was open for 12% of the time, Pallas kernels for 0%

profile of v9, /device:TPU:32, one launch (start us, length us, event | category | flops | bytes accessed | tf_op | source)
XLA Modules:
  0.0 126.3 jit_solution(6358787966154927663)
XLA Ops:
  1.4 6.9 %all-to-all-start = ((bf16[8,6,2,128]{3,2,1,0:T(2,128)(2,1)}), bf16[8,6,2,128]{3,2,1,0:T(2,128)(2,1)S(1)}, u32[]{:S(2)}, u32[]{:S(2)}) async-start(bf16[8,6,2,128]{3,2,1,0:T(2,128)(2,1)} %bitcast.2), calls=%async_computation | async-start | bytes 49152 | tf_op jit(solution)/shard_map/all_to_all | solution.py:130
  9.6 2.7 %fusion.65 = (bf16[6,16,64,128]{3,2,1,0:T(8,128)(2,1)S(1)}, bf16[6,16,64,128]{3,2,1,0:T(8,128)(2,1)S(1)}) fusion(bf16[6,16,64,256]{3,2,1,0:T(8,128)(2,1)} %param.14), kind=kLoop, calls=%fused_computation.134 | loop fusion | bytes 6291456 | tf_op jit(solution)/shard_map/slice | solution.py:148
  12.6 3.4 %all-to-all-done = bf16[8,6,2,128]{3,2,1,0:T(2,128)(2,1)S(1)} async-done(((bf16[8,6,2,128]{3,2,1,0:T(2,128)(2,1)}), bf16[8,6,2,128]{3,2,1,0:T(2,128)(2,1)S(1)}, u32[]{:S(2)}, u32[]{:S(2)}) %all-to-all-start) | async-done | bytes 24608 | tf_op jit(solution)/shard_map/all_to_all | solution.py:130
  19.7 3.3 %collective-permute-done = f32[6,8,130]{2,1,0:T(8,128)S(1)} collective-permute-done((f32[6,8,130]{2,1,0:T(8,128)S(1)}, f32[6,8,130]{2,1,0:T(8,128)S(1)}, u32[]{:S(2)}, u32[]{:S(2)}) %collective-permute-start) | collective-permute-done | bytes 24992 | tf_op jit(solution)/shard_map/ppermute | solution.py:33
  24.0 0.7 collective-permute-start.1
  25.0 7.1 %collective-permute-done.1 = f32[6,4,130]{0,1,2:T(4,128)S(1)} collective-permute-done((f32[6,4,130]{0,1,2:T(4,128)S(1)}, f32[6,4,130]{0,1,2:T(4,128)S(1)}, u32[]{:S(2)}, u32[]{:S(2)}) %collective-permute-start.1) | collective-permute-done | bytes 12512 | tf_op jit(solution)/shard_map/ppermute | solution.py:33
  33.0 8.6 %all-to-all-start.1 = ((bf16[16,6,512]{2,1,0:T(8,128)(2,1)}), bf16[16,6,512]{2,1,0:T(8,128)(2,1)S(1)}, u32[]{:S(2)}, u32[]{:S(2)}) async-start(bf16[16,6,512]{2,1,0:T(8,128)(2,1)} %broadcast_in_dim.81), calls=%async_computation.1 | async-start | bytes 262144 | tf_op jit(solution)/shard_map/all_to_all | solution.py:18
  41.7 1.8 %reduce-window.6 = s32[64,6,128]{2,0,1:T(8,128)S(1)} reduce-window(s32[64,6,128]{2,0,1:T(8,128)S(1)} %fusion.28, s32[]{:T(128)} %constant.114.clone.1), window={size=1x1x128 pad=0_0x0_0x127_0}, to_apply=%region_3.4 | reduce-window | flops 6242304 | bytes 393220 | tf_op jit(solution)/shard_map/reduce-window
  43.8 5.2 %all-to-all-done.1 = bf16[16,6,512]{2,1,0:T(8,128)(2,1)S(1)} async-done(((bf16[16,6,512]{2,1,0:T(8,128)(2,1)}), bf16[16,6,512]{2,1,0:T(8,128)(2,1)S(1)}, u32[]{:S(2)}, u32[]{:S(2)}) %all-to-all-start.1) | async-done | bytes 98336 | tf_op jit(solution)/shard_map/all_to_all | solution.py:18
  50.1 4.8 %collective-permute-done.2 = bf16[96,256]{1,0:T(8,128)(2,1)S(1)} collective-permute-done((bf16[96,256]{1,0:T(8,128)(2,1)S(1)}, bf16[96,256]{1,0:T(8,128)(2,1)S(1)}, u32[]{:S(2)}, u32[]{:S(2)}) %collective-permute-start.2) | collective-permute-done | bytes 49184 | tf_op jit(solution)/shard_map/ppermute | solution.py:44
  55.7 3.4 %collective-permute-done.3 = bf16[96,256]{1,0:T(8,128)(2,1)S(1)} collective-permute-done((bf16[96,256]{1,0:T(8,128)(2,1)S(1)}, bf16[96,256]{1,0:T(8,128)(2,1)S(1)}, u32[]{:S(2)}, u32[]{:S(2)}) %collective-permute-start.3) | collective-permute-done | bytes 49184 | tf_op jit(solution)/shard_map/ppermute | solution.py:44
  59.2 1.3 %collective-permute-start.4 = (bf16[96,256]{1,0:T(8,128)(2,1)S(1)}, bf16[96,256]{1,0:T(8,128)(2,1)S(1)}, u32[]{:S(2)}, u32[]{:S(2)}) collective-permute-start(bf16[96,256]{1,0:T(8,128)(2,1)S(1)} %add_reduce-precision_fusion.5), channel_id=1, source_target_pairs={{0,4},{1,5},{2,6},{3,7},{4,0},{5,1},{6,2},{7,3},{128,132},{129,133... | collective-permute-start | bytes 147464 | tf_op jit(solution)/shard_map/ppermute | solution.py:44
  60.5 0.8 fusion.2
  61.5 3.3 %collective-permute-done.4 = bf16[96,256]{1,0:T(8,128)(2,1)S(1)} collective-permute-done((bf16[96,256]{1,0:T(8,128)(2,1)S(1)}, bf16[96,256]{1,0:T(8,128)(2,1)S(1)}, u32[]{:S(2)}, u32[]{:S(2)}) %collective-permute-start.4) | collective-permute-done | bytes 49184 | tf_op jit(solution)/shard_map/ppermute | solution.py:44
  64.9 0.8 collective-permute-start.5
  65.6 3.4 %collective-permute-done.5 = bf16[96,256]{1,0:T(8,128)(2,1)S(1)} collective-permute-done((bf16[96,256]{1,0:T(8,128)(2,1)S(1)}, bf16[96,256]{1,0:T(8,128)(2,1)S(1)}, u32[]{:S(2)}, u32[]{:S(2)}) %collective-permute-start.5) | collective-permute-done | bytes 49184 | tf_op jit(solution)/shard_map/ppermute | solution.py:44
  70.4 5.4 %all-to-all-start.2 = ((bf16[16,27,256]{2,1,0:T(8,128)(2,1)}), bf16[16,27,256]{2,1,0:T(8,128)(2,1)}, u32[]{:S(2)}, u32[]{:S(2)}) async-start(bf16[16,27,256]{2,1,0:T(8,128)(2,1)} %fusion.17), calls=%async_computation.2 | async-start | bytes 524288 | tf_op jit(solution)/shard_map/all_to_all | solution.py:241
  75.8 3.4 %copy.249 = bf16[4096,384]{1,0:T(8,128)(2,1)S(1)} copy(bf16[4096,384]{0,1:T(8,128)(2,1)} %bitcast.125) | data formatting | bytes 6291456 | tf_op jit(solution)/shard_map/ecf,efd->ecd/dot_general | solution.py:254
  79.2 1.3 %reduce_sum.61 = f32[96]{0:T(128)} reduce(f32[96,8]{0,1:T(8,128)} %param.21, f32[]{:T(128)} %constant.129.clone.1), dimensions={1}, to_apply=%region_6.7 | reduce | flops 672 | bytes 3460 | tf_op jit(solution)/shard_map/reduce_sum | solution.py:228
  80.5 5.0 %all-to-all-done.2 = bf16[16,27,256]{2,1,0:T(8,128)(2,1)} async-done(((bf16[16,27,256]{2,1,0:T(8,128)(2,1)}), bf16[16,27,256]{2,1,0:T(8,128)(2,1)}, u32[]{:S(2)}, u32[]{:S(2)}) %all-to-all-start.2) | async-done | bytes 221216 | tf_op jit(solution)/shard_map/all_to_all | solution.py:241
  85.6 0.8 convert_reduce_fusion
  86.4 3.8 %fusion.11 = f32[1,24,2,384]{3,1,2,0:T(8,128)S(1)} fusion(bf16[16,256,2,384]{3,2,1,0:T(2,128)(2,1)} %bitcast.145, bf16[16,27,256]{2,1,0:T(8,128)(2,1)} %all-to-all-done.2, f32[24]{0:T(128)S(1)} %add_rsqrt_fusion), kind=kOutput, calls=%fused_computation.14 | convolution fusion | flops 151013376 | bytes 6561888 | tf_op jit(solution)/shard_map/becd,ebdgf->ecgf/dot_general | solution.py:246
  90.2 1.9 %fusion.4 = bf16[1,24,16,256]{3,1,0,2:T(8,128)(2,1)} fusion(bf16[16,256,384]{2,1,0:T(8,128)(2,1)S(1)} %bitcast.122, f32[1,24,2,384]{3,1,2,0:T(8,128)S(1)} %fusion.11), kind=kOutput, calls=%fused_computation.9 | convolution fusion | flops 75651072 | bytes 3416064 | tf_op jit(solution)/shard_map/ecf,efd->ecd/dot_general | solution.py:254
  92.1 5.0 %all-to-all-start.3 = ((bf16[1,24,16,256]{3,1,0,2:T(8,128)(2,1)}), bf16[1,24,16,256]{3,1,0,2:T(8,128)(2,1)S(1)}, u32[]{:S(2)}, u32[]{:S(2)}) async-start(bf16[1,24,16,256]{3,1,0,2:T(8,128)(2,1)} %fusion.4), calls=%async_computation.3 | async-start | bytes 393216 | tf_op jit(solution)/shard_map/all_to_all | solution.py:259
  97.8 1.6 %select_reduce_fusion = bf16[768,96]{0,1:T(8,128)(2,1)S(1)} fusion(f32[96,8]{1,0:T(8,128)S(1)} %copy.237, s32[96,8]{1,0:T(8,128)} %copy-done.2), kind=kLoop, calls=%fused_computation.2 | loop fusion | flops 1695744 | bytes 153600 | tf_op jit(solution)/shard_map/reduce_sum | solution.py:229
  99.6 5.9 %all-to-all-done.3 = bf16[1,24,16,256]{3,1,0,2:T(8,128)(2,1)S(1)} async-done(((bf16[1,24,16,256]{3,1,0,2:T(8,128)(2,1)}), bf16[1,24,16,256]{3,1,0,2:T(8,128)(2,1)S(1)}, u32[]{:S(2)}, u32[]{:S(2)}) %all-to-all-start.3) | async-done | bytes 196640 | tf_op jit(solution)/shard_map/all_to_all | solution.py:259
  106.5 5.1 %collective-permute-done.6 = bf16[96,256]{1,0:T(8,128)(2,1)S(1)} collective-permute-done((bf16[96,256]{1,0:T(8,128)(2,1)S(1)}, bf16[96,256]{1,0:T(8,128)(2,1)S(1)}, u32[]{:S(2)}, u32[]{:S(2)}) %collective-permute-start.6) | collective-permute-done | bytes 49184 | tf_op jit(solution)/shard_map/ppermute | solution.py:44
  112.2 3.5 %collective-permute-done.7 = bf16[96,256]{1,0:T(8,128)(2,1)S(1)} collective-permute-done((bf16[96,256]{1,0:T(8,128)(2,1)S(1)}, bf16[96,256]{1,0:T(8,128)(2,1)S(1)}, u32[]{:S(2)}, u32[]{:S(2)}) %collective-permute-start.7) | collective-permute-done | bytes 49184 | tf_op jit(solution)/shard_map/ppermute | solution.py:44
  115.8 1.3 %collective-permute-start.8 = (bf16[96,256]{1,0:T(8,128)(2,1)S(1)}, bf16[96,256]{1,0:T(8,128)(2,1)S(1)}, u32[]{:S(2)}, u32[]{:S(2)}) collective-permute-start(bf16[96,256]{1,0:T(8,128)(2,1)S(1)} %add_reduce-precision_fusion.1), channel_id=1, source_target_pairs={{0,4},{1,5},{2,6},{3,7},{4,0},{5,1},{6,2},{7,3},{128,132},{129,133... | collective-permute-start | bytes 147464 | tf_op jit(solution)/shard_map/ppermute | solution.py:44
  117.1 4.4 %collective-permute-done.8 = bf16[96,256]{1,0:T(8,128)(2,1)S(1)} collective-permute-done((bf16[96,256]{1,0:T(8,128)(2,1)S(1)}, bf16[96,256]{1,0:T(8,128)(2,1)S(1)}, u32[]{:S(2)}, u32[]{:S(2)}) %collective-permute-start.8) | collective-permute-done | bytes 49184 | tf_op jit(solution)/shard_map/ppermute | solution.py:44
  121.5 0.8 collective-permute-start.9
  122.3 3.4 %collective-permute-done.9 = bf16[96,256]{1,0:T(8,128)(2,1)S(1)} collective-permute-done((bf16[96,256]{1,0:T(8,128)(2,1)S(1)}, bf16[96,256]{1,0:T(8,128)(2,1)S(1)}, u32[]{:S(2)}, u32[]{:S(2)}) %collective-permute-start.9) | collective-permute-done | bytes 49184 | tf_op jit(solution)/shard_map/ppermute | solution.py:44
  (101 shorter events, 15.9 us)
Async XLA Ops:
  0.0 49.0 %copy-start = (bf16[512,256]{1,0:T(8,128)(2,1)S(1)}, bf16[512,256]{1,0:T(8,128)(2,1)}, u32[]{:S(2)}) copy-start(bf16[512,256]{1,0:T(8,128)(2,1)} %param.17) | copy-start | bytes 786436
  1.4 14.6 %all-to-all-start = ((bf16[8,6,2,128]{3,2,1,0:T(2,128)(2,1)}), bf16[8,6,2,128]{3,2,1,0:T(2,128)(2,1)S(1)}, u32[]{:S(2)}, u32[]{:S(2)}) async-start(bf16[8,6,2,128]{3,2,1,0:T(2,128)(2,1)} %bitcast.2), calls=%async_computation | async-start | bytes 49152 | tf_op jit(solution)/shard_map/all_to_all | solution.py:130
  9.6 2.7 %copy-start.4 = (bf16[6,4,256]{2,1,0:T(4,128)(2,1)S(1)}, bf16[6,4,256]{2,1,0:T(4,128)(2,1)}, u32[]{:S(2)}) copy-start(bf16[6,4,256]{2,1,0:T(4,128)(2,1)} %param.13) | copy-start | bytes 36868
  9.6 2.8 %copy-start.6 = (s32[6]{0:T(128)S(1)}, s32[6]{0:T(128)}, u32[]{:S(2)}) copy-start(s32[6]{0:T(128)} %param.15) | copy-start | bytes 76
  18.8 4.2 %collective-permute-start = (f32[6,8,130]{2,1,0:T(8,128)S(1)}, f32[6,8,130]{2,1,0:T(8,128)S(1)}, u32[]{:S(2)}, u32[]{:S(2)}) collective-permute-start(f32[6,8,130]{2,1,0:T(8,128)S(1)} %copy.218), channel_id=1, source_target_pairs={{0,2},{1,3},{2,0},{3,1},{4,6},{5,7},{6,4},{7,5},{8,10},{9,11},{10,... | collective-permute-start | bytes 74888 | tf_op jit(solution)/shard_map/ppermute | solution.py:33
  19.5 5.2 %copy-start.3 = (s32[96,8]{0,1:T(8,128)S(1)}, s32[96,8]{0,1:T(8,128)}, u32[]{:S(2)}) copy-start(s32[96,8]{0,1:T(8,128)} %param.20) | copy-start | bytes 9220
  24.0 8.0 %collective-permute-start.1 = (f32[6,4,130]{0,1,2:T(4,128)S(1)}, f32[6,4,130]{0,1,2:T(4,128)S(1)}, u32[]{:S(2)}, u32[]{:S(2)}) collective-permute-start(f32[6,4,130]{0,1,2:T(4,128)S(1)} %constant_dynamic-slice_fusion.4), channel_id=1, source_target_pairs={{0,1},{1,0},{2,3},{3,2},{4,5},{5,4},{6,7},{7,6},{8,9},{9,8},{10,11... | collective-permute-start | bytes 37448 | tf_op jit(solution)/shard_map/ppermute | solution.py:33
  32.3 36.7 %copy-start.1 = (bf16[96,256]{1,0:T(8,128)(2,1)S(1)}, bf16[96,256]{1,0:T(8,128)(2,1)}, u32[]{:S(2)}) copy-start(bf16[96,256]{1,0:T(8,128)(2,1)} %param.18) | copy-start | bytes 147460
  33.0 16.0 %all-to-all-start.1 = ((bf16[16,6,512]{2,1,0:T(8,128)(2,1)}), bf16[16,6,512]{2,1,0:T(8,128)(2,1)S(1)}, u32[]{:S(2)}, u32[]{:S(2)}) async-start(bf16[16,6,512]{2,1,0:T(8,128)(2,1)} %broadcast_in_dim.81), calls=%async_computation.1 | async-start | bytes 262144 | tf_op jit(solution)/shard_map/all_to_all | solution.py:18
  41.6 27.9 %copy-start.5 = (f32[256]{0:T(256)S(1)}, f32[256]{0:T(256)}, u32[]{:S(2)}) copy-start(f32[256]{0:T(256)} %param.19) | copy-start | bytes 3076
  49.2 5.8 %collective-permute-start.2 = (bf16[96,256]{1,0:T(8,128)(2,1)S(1)}, bf16[96,256]{1,0:T(8,128)(2,1)S(1)}, u32[]{:S(2)}, u32[]{:S(2)}) collective-permute-start(bf16[96,256]{1,0:T(8,128)(2,1)S(1)} %convolution_convert_fusion.2), channel_id=1, source_target_pairs={{0,1},{1,0},{2,3},{3,2},{4,5},{5,4},{6,7},{7,6},{128,129},{129,128... | collective-permute-start | bytes 147464 | tf_op jit(solution)/shard_map/ppermute | solution.py:44
  55.0 4.2 %collective-permute-start.3 = (bf16[96,256]{1,0:T(8,128)(2,1)S(1)}, bf16[96,256]{1,0:T(8,128)(2,1)S(1)}, u32[]{:S(2)}, u32[]{:S(2)}) collective-permute-start(bf16[96,256]{1,0:T(8,128)(2,1)S(1)} %add_reduce-precision_fusion.6), channel_id=1, source_target_pairs={{0,2},{1,3},{2,0},{3,1},{4,6},{5,7},{6,4},{7,5},{128,130},{129,131... | collective-permute-start | bytes 147464 | tf_op jit(solution)/shard_map/ppermute | solution.py:44
  55.7 4.8 %copy-start.2 = (s32[96,8]{1,0:T(8,128)}, s32[96,8]{1,0:T(8,128)S(1)}, u32[]{:S(2)}) copy-start(s32[96,8]{1,0:T(8,128)S(1)} %fusion.34) | copy-start | bytes 9220
  59.2 5.7 %collective-permute-start.4 = (bf16[96,256]{1,0:T(8,128)(2,1)S(1)}, bf16[96,256]{1,0:T(8,128)(2,1)S(1)}, u32[]{:S(2)}, u32[]{:S(2)}) collective-permute-start(bf16[96,256]{1,0:T(8,128)(2,1)S(1)} %add_reduce-precision_fusion.5), channel_id=1, source_target_pairs={{0,4},{1,5},{2,6},{3,7},{4,0},{5,1},{6,2},{7,3},{128,132},{129,133... | collective-permute-start | bytes 147464 | tf_op jit(solution)/shard_map/ppermute | solution.py:44
  64.9 4.2 %collective-permute-start.5 = (bf16[96,256]{1,0:T(8,128)(2,1)S(1)}, bf16[96,256]{1,0:T(8,128)(2,1)S(1)}, u32[]{:S(2)}, u32[]{:S(2)}) collective-permute-start(bf16[96,256]{1,0:T(8,128)(2,1)S(1)} %add_reduce-precision_fusion.4), channel_id=1, source_target_pairs={{0,128},{1,129},{2,130},{3,131},{4,132},{5,133},{6,134},{7,135},{1... | collective-permute-start | bytes 147464 | tf_op jit(solution)/shard_map/ppermute | solution.py:44
  70.4 15.1 %all-to-all-start.2 = ((bf16[16,27,256]{2,1,0:T(8,128)(2,1)}), bf16[16,27,256]{2,1,0:T(8,128)(2,1)}, u32[]{:S(2)}, u32[]{:S(2)}) async-start(bf16[16,27,256]{2,1,0:T(8,128)(2,1)} %fusion.17), calls=%async_computation.2 | async-start | bytes 524288 | tf_op jit(solution)/shard_map/all_to_all | solution.py:241
  92.1 13.4 %all-to-all-start.3 = ((bf16[1,24,16,256]{3,1,0,2:T(8,128)(2,1)}), bf16[1,24,16,256]{3,1,0,2:T(8,128)(2,1)S(1)}, u32[]{:S(2)}, u32[]{:S(2)}) async-start(bf16[1,24,16,256]{3,1,0,2:T(8,128)(2,1)} %fusion.4), calls=%async_computation.3 | async-start | bytes 393216 | tf_op jit(solution)/shard_map/all_to_all | solution.py:259
  105.7 5.8 %collective-permute-start.6 = (bf16[96,256]{1,0:T(8,128)(2,1)S(1)}, bf16[96,256]{1,0:T(8,128)(2,1)S(1)}, u32[]{:S(2)}, u32[]{:S(2)}) collective-permute-start(bf16[96,256]{1,0:T(8,128)(2,1)S(1)} %fusion.68), channel_id=1, source_target_pairs={{0,1},{1,0},{2,3},{3,2},{4,5},{5,4},{6,7},{7,6},{128,129},{129,128... | collective-permute-start | bytes 147464 | tf_op jit(solution)/shard_map/ppermute | solution.py:44
  111.6 4.2 %collective-permute-start.7 = (bf16[96,256]{1,0:T(8,128)(2,1)S(1)}, bf16[96,256]{1,0:T(8,128)(2,1)S(1)}, u32[]{:S(2)}, u32[]{:S(2)}) collective-permute-start(bf16[96,256]{1,0:T(8,128)(2,1)S(1)} %add_reduce-precision_fusion.2), channel_id=1, source_target_pairs={{0,2},{1,3},{2,0},{3,1},{4,6},{5,7},{6,4},{7,5},{128,130},{129,131... | collective-permute-start | bytes 147464 | tf_op jit(solution)/shard_map/ppermute | solution.py:44
  115.8 5.7 %collective-permute-start.8 = (bf16[96,256]{1,0:T(8,128)(2,1)S(1)}, bf16[96,256]{1,0:T(8,128)(2,1)S(1)}, u32[]{:S(2)}, u32[]{:S(2)}) collective-permute-start(bf16[96,256]{1,0:T(8,128)(2,1)S(1)} %add_reduce-precision_fusion.1), channel_id=1, source_target_pairs={{0,4},{1,5},{2,6},{3,7},{4,0},{5,1},{6,2},{7,3},{128,132},{129,133... | collective-permute-start | bytes 147464 | tf_op jit(solution)/shard_map/ppermute | solution.py:44
  121.5 4.2 %collective-permute-start.9 = (bf16[96,256]{1,0:T(8,128)(2,1)S(1)}, bf16[96,256]{1,0:T(8,128)(2,1)S(1)}, u32[]{:S(2)}, u32[]{:S(2)}) collective-permute-start(bf16[96,256]{1,0:T(8,128)(2,1)S(1)} %add_reduce-precision_fusion), channel_id=1, source_target_pairs={{0,128},{1,129},{2,130},{3,131},{4,132},{5,133},{6,134},{7,135},{1... | collective-permute-start | bytes 147464 | tf_op jit(solution)/shard_map/ppermute | solution.py:44

commit v10 on v9

--- a/solution.py
+++ b/solution.py
@@ -37,14 +37,16 @@
     return copy_for_each(shard, axis).astype(jnp.float32).sum(axis=0)
 
 
-def doubled_sum(shard, axis):
+def doubled_sum(shard, axis, steps):
     count = lax.axis_size(axis)
-    step = 1
-    while step < count:
+    for step in steps:
         partner = lax.ppermute(shard, axis, [(i, i ^ step) for i in range(count)])
         shard = lax.reduce_precision(shard + partner, exponent_bits=8, mantissa_bits=7)
-        step *= 2
     return shard
+
+
+def neighbour_steps(head_size):
+    return (head_size, head_size + 1, 2, 6)
 
 
 def of_everyone(shard, axis):
@@ -193,7 +195,9 @@
     cols_dev = residual.shape[1]
     all_attention = gathered_copies(attention, "batch", 0)
     head_terms = jnp.dot(all_attention, out_weight, preferred_element_type=jnp.float32)
-    projected = doubled_sum(head_terms.astype(jnp.bfloat16), ("sect", "head")).astype(
+    projected = doubled_sum(
+        head_terms.astype(jnp.bfloat16), ("sect", "head"), neighbour_steps(head_size)
+    ).astype(
         jnp.float32
     )
     hidden_state = residual.astype(jnp.float32) + projected
@@ -267,7 +271,9 @@
     )
     weights_used = weights_used.reshape(token_count, send_count)
     combined = jnp.dot(weights_used, came_back, preferred_element_type=jnp.float32)
-    expert_mix = doubled_sum(combined.astype(jnp.bfloat16), ("sect", "head")).astype(jnp.float32)
+    expert_mix = doubled_sum(
+        combined.astype(jnp.bfloat16), ("sect", "head"), neighbour_steps(head_size)
+    ).astype(jnp.float32)
     return (hidden_state + expert_mix).astype(jnp.bfloat16)
 
 

time: 127 us -> 126 us (level)
  starting transfers between devices: 34.2 us -> 32.5 us
    ppermute x8, starting transfers between devices: 6.97 us -> 5.25 us  [doubled_sum(): partner = lax.ppermute(shard, axis, [(i, i ^ step) for i in range(count)])]
where the time goes in v10:
time: 126 us; the launch traced here: 125 us
  waiting for transfers between devices  61.7 us (49%)
  starting transfers between devices  32.5 us (26%)
  local copies, waits for them, and re-layouts  13 us (10%)
  other arithmetic  9.99 us (8%)
  matrix products  7.59 us (6%)
    ppermute x8, waiting for transfers between devices, doubled_sum(): partner = lax.ppermute(shard, axis, [(i, i ^ step) for i in range(count)])  31.9 us
    ppermute x2, waiting for transfers between devices, from_partner(): lax.ppermute(shard, axis, [(i, i ^ 1 << distance) for i in range(lax.axis...  10.3 us
    all_to_all x1, starting transfers between devices, copy_for_each(): return lax.all_to_all(copies, axis, split_axis=0, concat_axis=0, tiled=True)  8.59 us
    all_to_all x1, starting transfers between devices, on_device(): lax.all_to_all(per_target, 'head', split_axis=0, concat_axis=0, tiled=True)  6.93 us
    all_to_all x1, waiting for transfers between devices, on_device(): lax.all_to_all(leaving.astype(jnp.bfloat16), 'batch', split_axis=2, conca...  5.87 us
    all_to_all x1, starting transfers between devices, on_device(): lax.all_to_all(outgoing, 'batch', split_axis=0, concat_axis=0, tiled=True)  5.39 us
    ppermute x8, starting transfers between devices, doubled_sum(): partner = lax.ppermute(shard, axis, [(i, i ^ step) for i in range(count)])  5.25 us
    all_to_all x1, waiting for transfers between devices, copy_for_each(): return lax.all_to_all(copies, axis, split_axis=0, concat_axis=0, tiled=True)  5.15 us
  transfers between devices with their start and end apart: 14, of which 14 were waited for; matrix products, arithmetic and copies ran while one was open for 12% of the time, Pallas kernels for 0%

profile of v10, /device:TPU:32, one launch (start us, length us, event | category | flops | bytes accessed | tf_op | source)
XLA Modules:
  0.0 125.2 jit_solution(11673021778929547782)
XLA Ops:
  0.0 0.7 reshape.212
  1.4 6.9 %all-to-all-start = ((bf16[8,6,2,128]{3,2,1,0:T(2,128)(2,1)}), bf16[8,6,2,128]{3,2,1,0:T(2,128)(2,1)S(1)}, u32[]{:S(2)}, u32[]{:S(2)}) async-start(bf16[8,6,2,128]{3,2,1,0:T(2,128)(2,1)} %bitcast.2), calls=%async_computation | async-start | bytes 49152 | tf_op jit(solution)/shard_map/all_to_all | solution.py:132
  9.6 2.7 %fusion.65 = (bf16[6,16,64,128]{3,2,1,0:T(8,128)(2,1)S(1)}, bf16[6,16,64,128]{3,2,1,0:T(8,128)(2,1)S(1)}) fusion(bf16[6,16,64,256]{3,2,1,0:T(8,128)(2,1)} %param.14), kind=kLoop, calls=%fused_computation.134 | loop fusion | bytes 6291456 | tf_op jit(solution)/shard_map/slice | solution.py:150
  12.6 3.4 %all-to-all-done = bf16[8,6,2,128]{3,2,1,0:T(2,128)(2,1)S(1)} async-done(((bf16[8,6,2,128]{3,2,1,0:T(2,128)(2,1)}), bf16[8,6,2,128]{3,2,1,0:T(2,128)(2,1)S(1)}, u32[]{:S(2)}, u32[]{:S(2)}) %all-to-all-start) | async-done | bytes 24608 | tf_op jit(solution)/shard_map/all_to_all | solution.py:132
  19.7 3.3 %collective-permute-done = f32[6,8,130]{2,1,0:T(8,128)S(1)} collective-permute-done((f32[6,8,130]{2,1,0:T(8,128)S(1)}, f32[6,8,130]{2,1,0:T(8,128)S(1)}, u32[]{:S(2)}, u32[]{:S(2)}) %collective-permute-start) | collective-permute-done | bytes 24992 | tf_op jit(solution)/shard_map/ppermute | solution.py:33
  24.0 0.7 collective-permute-start.1
  25.0 7.1 %collective-permute-done.1 = f32[6,4,130]{0,1,2:T(4,128)S(1)} collective-permute-done((f32[6,4,130]{0,1,2:T(4,128)S(1)}, f32[6,4,130]{0,1,2:T(4,128)S(1)}, u32[]{:S(2)}, u32[]{:S(2)}) %collective-permute-start.1) | collective-permute-done | bytes 12512 | tf_op jit(solution)/shard_map/ppermute | solution.py:33
  33.0 8.6 %all-to-all-start.1 = ((bf16[16,6,512]{2,1,0:T(8,128)(2,1)}), bf16[16,6,512]{2,1,0:T(8,128)(2,1)S(1)}, u32[]{:S(2)}, u32[]{:S(2)}) async-start(bf16[16,6,512]{2,1,0:T(8,128)(2,1)} %broadcast_in_dim.81), calls=%async_computation.1 | async-start | bytes 262144 | tf_op jit(solution)/shard_map/all_to_all | solution.py:18
  41.7 1.8 %reduce-window.6 = s32[64,6,128]{2,0,1:T(8,128)S(1)} reduce-window(s32[64,6,128]{2,0,1:T(8,128)S(1)} %fusion.28, s32[]{:T(128)} %constant.114.clone.1), window={size=1x1x128 pad=0_0x0_0x127_0}, to_apply=%region_3.4 | reduce-window | flops 6242304 | bytes 393220 | tf_op jit(solution)/shard_map/reduce-window
  43.8 5.2 %all-to-all-done.1 = bf16[16,6,512]{2,1,0:T(8,128)(2,1)S(1)} async-done(((bf16[16,6,512]{2,1,0:T(8,128)(2,1)}), bf16[16,6,512]{2,1,0:T(8,128)(2,1)S(1)}, u32[]{:S(2)}, u32[]{:S(2)}) %all-to-all-start.1) | async-done | bytes 98336 | tf_op jit(solution)/shard_map/all_to_all | solution.py:18
  49.2 0.8 collective-permute-start.2
  50.2 3.3 %collective-permute-done.2 = bf16[96,256]{1,0:T(8,128)(2,1)S(1)} collective-permute-done((bf16[96,256]{1,0:T(8,128)(2,1)S(1)}, bf16[96,256]{1,0:T(8,128)(2,1)S(1)}, u32[]{:S(2)}, u32[]{:S(2)}) %collective-permute-start.2) | collective-permute-done | bytes 49184 | tf_op jit(solution)/shard_map/ppermute | solution.py:43
  54.1 4.7 %collective-permute-done.3 = bf16[96,256]{1,0:T(8,128)(2,1)S(1)} collective-permute-done((bf16[96,256]{1,0:T(8,128)(2,1)S(1)}, bf16[96,256]{1,0:T(8,128)(2,1)S(1)}, u32[]{:S(2)}, u32[]{:S(2)}) %collective-permute-start.3) | collective-permute-done | bytes 49184 | tf_op jit(solution)/shard_map/ppermute | solution.py:43
  59.5 0.8 fusion.2
  60.6 2.5 %collective-permute-done.4 = bf16[96,256]{1,0:T(8,128)(2,1)S(1)} collective-permute-done((bf16[96,256]{1,0:T(8,128)(2,1)S(1)}, bf16[96,256]{1,0:T(8,128)(2,1)S(1)}, u32[]{:S(2)}, u32[]{:S(2)}) %collective-permute-start.4) | collective-permute-done | bytes 49184 | tf_op jit(solution)/shard_map/ppermute | solution.py:43
  63.1 1.3 %collective-permute-start.5 = (bf16[96,256]{1,0:T(8,128)(2,1)S(1)}, bf16[96,256]{1,0:T(8,128)(2,1)S(1)}, u32[]{:S(2)}, u32[]{:S(2)}) collective-permute-start(bf16[96,256]{1,0:T(8,128)(2,1)S(1)} %add_reduce-precision_fusion.4), channel_id=1, source_target_pairs={{0,6},{1,7},{2,4},{3,5},{4,2},{5,3},{6,0},{7,1},{128,134},{129,135... | collective-permute-start | bytes 147464 | tf_op jit(solution)/shard_map/ppermute | solution.py:43
  64.3 4.1 %collective-permute-done.5 = bf16[96,256]{1,0:T(8,128)(2,1)S(1)} collective-permute-done((bf16[96,256]{1,0:T(8,128)(2,1)S(1)}, bf16[96,256]{1,0:T(8,128)(2,1)S(1)}, u32[]{:S(2)}, u32[]{:S(2)}) %collective-permute-start.5) | collective-permute-done | bytes 49184 | tf_op jit(solution)/shard_map/ppermute | solution.py:43
  69.8 5.4 %all-to-all-start.2 = ((bf16[16,27,256]{2,1,0:T(8,128)(2,1)}), bf16[16,27,256]{2,1,0:T(8,128)(2,1)}, u32[]{:S(2)}, u32[]{:S(2)}) async-start(bf16[16,27,256]{2,1,0:T(8,128)(2,1)} %fusion.17), calls=%async_computation.2 | async-start | bytes 524288 | tf_op jit(solution)/shard_map/all_to_all | solution.py:245
  75.2 3.4 %copy.249 = bf16[4096,384]{1,0:T(8,128)(2,1)S(1)} copy(bf16[4096,384]{0,1:T(8,128)(2,1)} %bitcast.125) | data formatting | bytes 6291456 | tf_op jit(solution)/shard_map/ecf,efd->ecd/dot_general | solution.py:258
  78.6 1.3 %reduce_sum.61 = f32[96]{0:T(128)} reduce(f32[96,8]{0,1:T(8,128)} %param.21, f32[]{:T(128)} %constant.129.clone.1), dimensions={1}, to_apply=%region_6.7 | reduce | flops 672 | bytes 3460 | tf_op jit(solution)/shard_map/reduce_sum | solution.py:232
  79.9 5.0 %all-to-all-done.2 = bf16[16,27,256]{2,1,0:T(8,128)(2,1)} async-done(((bf16[16,27,256]{2,1,0:T(8,128)(2,1)}), bf16[16,27,256]{2,1,0:T(8,128)(2,1)}, u32[]{:S(2)}, u32[]{:S(2)}) %all-to-all-start.2) | async-done | bytes 221216 | tf_op jit(solution)/shard_map/all_to_all | solution.py:245
  85.0 0.8 convert_reduce_fusion
  85.8 3.8 %fusion.11 = f32[1,24,2,384]{3,1,2,0:T(8,128)S(1)} fusion(bf16[16,256,2,384]{3,2,1,0:T(2,128)(2,1)} %bitcast.145, bf16[16,27,256]{2,1,0:T(8,128)(2,1)} %all-to-all-done.2, f32[24]{0:T(128)S(1)} %add_rsqrt_fusion), kind=kOutput, calls=%fused_computation.14 | convolution fusion | flops 151013376 | bytes 6561888 | tf_op jit(solution)/shard_map/becd,ebdgf->ecgf/dot_general | solution.py:250
  89.6 1.9 %fusion.4 = bf16[1,24,16,256]{3,1,0,2:T(8,128)(2,1)} fusion(bf16[16,256,384]{2,1,0:T(8,128)(2,1)S(1)} %bitcast.122, f32[1,24,2,384]{3,1,2,0:T(8,128)S(1)} %fusion.11), kind=kOutput, calls=%fused_computation.9 | convolution fusion | flops 75651072 | bytes 3416064 | tf_op jit(solution)/shard_map/ecf,efd->ecd/dot_general | solution.py:258
  91.5 5.0 %all-to-all-start.3 = ((bf16[1,24,16,256]{3,1,0,2:T(8,128)(2,1)}), bf16[1,24,16,256]{3,1,0,2:T(8,128)(2,1)S(1)}, u32[]{:S(2)}, u32[]{:S(2)}) async-start(bf16[1,24,16,256]{3,1,0,2:T(8,128)(2,1)} %fusion.4), calls=%async_computation.3 | async-start | bytes 393216 | tf_op jit(solution)/shard_map/all_to_all | solution.py:263
  97.2 1.6 %select_reduce_fusion = bf16[768,96]{0,1:T(8,128)(2,1)S(1)} fusion(f32[96,8]{1,0:T(8,128)S(1)} %copy.237, s32[96,8]{1,0:T(8,128)} %copy-done.2), kind=kLoop, calls=%fused_computation.2 | loop fusion | flops 1695744 | bytes 153600 | tf_op jit(solution)/shard_map/reduce_sum | solution.py:233
  99.1 5.9 %all-to-all-done.3 = bf16[1,24,16,256]{3,1,0,2:T(8,128)(2,1)S(1)} async-done(((bf16[1,24,16,256]{3,1,0,2:T(8,128)(2,1)}), bf16[1,24,16,256]{3,1,0,2:T(8,128)(2,1)S(1)}, u32[]{:S(2)}, u32[]{:S(2)}) %all-to-all-start.3) | async-done | bytes 196640 | tf_op jit(solution)/shard_map/all_to_all | solution.py:263
  105.3 4.2 %collective-permute-done.6 = bf16[96,256]{1,0:T(8,128)(2,1)S(1)} collective-permute-done((bf16[96,256]{1,0:T(8,128)(2,1)S(1)}, bf16[96,256]{1,0:T(8,128)(2,1)S(1)}, u32[]{:S(2)}, u32[]{:S(2)}) %collective-permute-start.6) | collective-permute-done | bytes 49184 | tf_op jit(solution)/shard_map/ppermute | solution.py:43
  110.1 4.8 %collective-permute-done.7 = bf16[96,256]{1,0:T(8,128)(2,1)S(1)} collective-permute-done((bf16[96,256]{1,0:T(8,128)(2,1)S(1)}, bf16[96,256]{1,0:T(8,128)(2,1)S(1)}, u32[]{:S(2)}, u32[]{:S(2)}) %collective-permute-start.7) | collective-permute-done | bytes 49184 | tf_op jit(solution)/shard_map/ppermute | solution.py:43
  115.0 4.1 %collective-permute-done.8 = bf16[96,256]{1,0:T(8,128)(2,1)S(1)} collective-permute-done((bf16[96,256]{1,0:T(8,128)(2,1)S(1)}, bf16[96,256]{1,0:T(8,128)(2,1)S(1)}, u32[]{:S(2)}, u32[]{:S(2)}) %collective-permute-start.8) | collective-permute-done | bytes 49184 | tf_op jit(solution)/shard_map/ppermute | solution.py:43
  119.1 1.3 %collective-permute-start.9 = (bf16[96,256]{1,0:T(8,128)(2,1)S(1)}, bf16[96,256]{1,0:T(8,128)(2,1)S(1)}, u32[]{:S(2)}, u32[]{:S(2)}) collective-permute-start(bf16[96,256]{1,0:T(8,128)(2,1)S(1)} %add_reduce-precision_fusion), channel_id=1, source_target_pairs={{0,6},{1,7},{2,4},{3,5},{4,2},{5,3},{6,0},{7,1},{128,134},{129,135... | collective-permute-start | bytes 147464 | tf_op jit(solution)/shard_map/ppermute | solution.py:43
  120.4 4.1 %collective-permute-done.9 = bf16[96,256]{1,0:T(8,128)(2,1)S(1)} collective-permute-done((bf16[96,256]{1,0:T(8,128)(2,1)S(1)}, bf16[96,256]{1,0:T(8,128)(2,1)S(1)}, u32[]{:S(2)}, u32[]{:S(2)}) %collective-permute-start.9) | collective-permute-done | bytes 49184 | tf_op jit(solution)/shard_map/ppermute | solution.py:43
  (101 shorter events, 14.3 us)
Async XLA Ops:
  0.0 49.0 %copy-start = (bf16[512,256]{1,0:T(8,128)(2,1)S(1)}, bf16[512,256]{1,0:T(8,128)(2,1)}, u32[]{:S(2)}) copy-start(bf16[512,256]{1,0:T(8,128)(2,1)} %param.17) | copy-start | bytes 786436
  1.4 14.6 %all-to-all-start = ((bf16[8,6,2,128]{3,2,1,0:T(2,128)(2,1)}), bf16[8,6,2,128]{3,2,1,0:T(2,128)(2,1)S(1)}, u32[]{:S(2)}, u32[]{:S(2)}) async-start(bf16[8,6,2,128]{3,2,1,0:T(2,128)(2,1)} %bitcast.2), calls=%async_computation | async-start | bytes 49152 | tf_op jit(solution)/shard_map/all_to_all | solution.py:132
  9.6 2.7 %copy-start.4 = (bf16[6,4,256]{2,1,0:T(4,128)(2,1)S(1)}, bf16[6,4,256]{2,1,0:T(4,128)(2,1)}, u32[]{:S(2)}) copy-start(bf16[6,4,256]{2,1,0:T(4,128)(2,1)} %param.13) | copy-start | bytes 36868
  9.6 2.8 %copy-start.6 = (s32[6]{0:T(128)S(1)}, s32[6]{0:T(128)}, u32[]{:S(2)}) copy-start(s32[6]{0:T(128)} %param.15) | copy-start | bytes 76
  18.8 4.2 %collective-permute-start = (f32[6,8,130]{2,1,0:T(8,128)S(1)}, f32[6,8,130]{2,1,0:T(8,128)S(1)}, u32[]{:S(2)}, u32[]{:S(2)}) collective-permute-start(f32[6,8,130]{2,1,0:T(8,128)S(1)} %copy.218), channel_id=1, source_target_pairs={{0,2},{1,3},{2,0},{3,1},{4,6},{5,7},{6,4},{7,5},{8,10},{9,11},{10,... | collective-permute-start | bytes 74888 | tf_op jit(solution)/shard_map/ppermute | solution.py:33
  19.5 5.2 %copy-start.3 = (s32[96,8]{0,1:T(8,128)S(1)}, s32[96,8]{0,1:T(8,128)}, u32[]{:S(2)}) copy-start(s32[96,8]{0,1:T(8,128)} %param.20) | copy-start | bytes 9220
  24.0 8.0 %collective-permute-start.1 = (f32[6,4,130]{0,1,2:T(4,128)S(1)}, f32[6,4,130]{0,1,2:T(4,128)S(1)}, u32[]{:S(2)}, u32[]{:S(2)}) collective-permute-start(f32[6,4,130]{0,1,2:T(4,128)S(1)} %constant_dynamic-slice_fusion.4), channel_id=1, source_target_pairs={{0,1},{1,0},{2,3},{3,2},{4,5},{5,4},{6,7},{7,6},{8,9},{9,8},{10,11... | collective-permute-start | bytes 37448 | tf_op jit(solution)/shard_map/ppermute | solution.py:33
  32.3 36.2 %copy-start.1 = (bf16[96,256]{1,0:T(8,128)(2,1)S(1)}, bf16[96,256]{1,0:T(8,128)(2,1)}, u32[]{:S(2)}) copy-start(bf16[96,256]{1,0:T(8,128)(2,1)} %param.18) | copy-start | bytes 147460
  33.0 16.0 %all-to-all-start.1 = ((bf16[16,6,512]{2,1,0:T(8,128)(2,1)}), bf16[16,6,512]{2,1,0:T(8,128)(2,1)S(1)}, u32[]{:S(2)}, u32[]{:S(2)}) async-start(bf16[16,6,512]{2,1,0:T(8,128)(2,1)} %broadcast_in_dim.81), calls=%async_computation.1 | async-start | bytes 262144 | tf_op jit(solution)/shard_map/all_to_all | solution.py:18
  41.6 27.3 %copy-start.5 = (f32[256]{0:T(256)S(1)}, f32[256]{0:T(256)}, u32[]{:S(2)}) copy-start(f32[256]{0:T(256)} %param.19) | copy-start | bytes 3076
  49.2 4.3 %collective-permute-start.2 = (bf16[96,256]{1,0:T(8,128)(2,1)S(1)}, bf16[96,256]{1,0:T(8,128)(2,1)S(1)}, u32[]{:S(2)}, u32[]{:S(2)}) collective-permute-start(bf16[96,256]{1,0:T(8,128)(2,1)S(1)} %convolution_convert_fusion.2), channel_id=1, source_target_pairs={{0,128},{1,129},{2,130},{3,131},{4,132},{5,133},{6,134},{7,135},{1... | collective-permute-start | bytes 147464 | tf_op jit(solution)/shard_map/ppermute | solution.py:43
  53.5 5.4 %collective-permute-start.3 = (bf16[96,256]{1,0:T(8,128)(2,1)S(1)}, bf16[96,256]{1,0:T(8,128)(2,1)S(1)}, u32[]{:S(2)}, u32[]{:S(2)}) collective-permute-start(bf16[96,256]{1,0:T(8,128)(2,1)S(1)} %add_reduce-precision_fusion.6), channel_id=1, source_target_pairs={{0,129},{1,128},{2,131},{3,130},{4,133},{5,132},{6,135},{7,134},{1... | collective-permute-start | bytes 147464 | tf_op jit(solution)/shard_map/ppermute | solution.py:43
  54.1 5.4 %copy-start.2 = (s32[96,8]{1,0:T(8,128)}, s32[96,8]{1,0:T(8,128)S(1)}, u32[]{:S(2)}) copy-start(s32[96,8]{1,0:T(8,128)S(1)} %fusion.34) | copy-start | bytes 9220
  58.9 4.2 %collective-permute-start.4 = (bf16[96,256]{1,0:T(8,128)(2,1)S(1)}, bf16[96,256]{1,0:T(8,128)(2,1)S(1)}, u32[]{:S(2)}, u32[]{:S(2)}) collective-permute-start(bf16[96,256]{1,0:T(8,128)(2,1)S(1)} %add_reduce-precision_fusion.5), channel_id=1, source_target_pairs={{0,2},{1,3},{2,0},{3,1},{4,6},{5,7},{6,4},{7,5},{128,130},{129,131... | collective-permute-start | bytes 147464 | tf_op jit(solution)/shard_map/ppermute | solution.py:43
  63.1 5.4 %collective-permute-start.5 = (bf16[96,256]{1,0:T(8,128)(2,1)S(1)}, bf16[96,256]{1,0:T(8,128)(2,1)S(1)}, u32[]{:S(2)}, u32[]{:S(2)}) collective-permute-start(bf16[96,256]{1,0:T(8,128)(2,1)S(1)} %add_reduce-precision_fusion.4), channel_id=1, source_target_pairs={{0,6},{1,7},{2,4},{3,5},{4,2},{5,3},{6,0},{7,1},{128,134},{129,135... | collective-permute-start | bytes 147464 | tf_op jit(solution)/shard_map/ppermute | solution.py:43
  69.8 15.1 %all-to-all-start.2 = ((bf16[16,27,256]{2,1,0:T(8,128)(2,1)}), bf16[16,27,256]{2,1,0:T(8,128)(2,1)}, u32[]{:S(2)}, u32[]{:S(2)}) async-start(bf16[16,27,256]{2,1,0:T(8,128)(2,1)} %fusion.17), calls=%async_computation.2 | async-start | bytes 524288 | tf_op jit(solution)/shard_map/all_to_all | solution.py:245
  91.5 13.4 %all-to-all-start.3 = ((bf16[1,24,16,256]{3,1,0,2:T(8,128)(2,1)}), bf16[1,24,16,256]{3,1,0,2:T(8,128)(2,1)S(1)}, u32[]{:S(2)}, u32[]{:S(2)}) async-start(bf16[1,24,16,256]{3,1,0,2:T(8,128)(2,1)} %fusion.4), calls=%async_computation.3 | async-start | bytes 393216 | tf_op jit(solution)/shard_map/all_to_all | solution.py:263
  105.2 4.3 %collective-permute-start.6 = (bf16[96,256]{1,0:T(8,128)(2,1)S(1)}, bf16[96,256]{1,0:T(8,128)(2,1)S(1)}, u32[]{:S(2)}, u32[]{:S(2)}) collective-permute-start(bf16[96,256]{1,0:T(8,128)(2,1)S(1)} %fusion.68), channel_id=1, source_target_pairs={{0,128},{1,129},{2,130},{3,131},{4,132},{5,133},{6,134},{7,135},{1... | collective-permute-start | bytes 147464 | tf_op jit(solution)/shard_map/ppermute | solution.py:43
  109.5 5.4 %collective-permute-start.7 = (bf16[96,256]{1,0:T(8,128)(2,1)S(1)}, bf16[96,256]{1,0:T(8,128)(2,1)S(1)}, u32[]{:S(2)}, u32[]{:S(2)}) collective-permute-start(bf16[96,256]{1,0:T(8,128)(2,1)S(1)} %add_reduce-precision_fusion.2), channel_id=1, source_target_pairs={{0,129},{1,128},{2,131},{3,130},{4,133},{5,132},{6,135},{7,134},{1... | collective-permute-start | bytes 147464 | tf_op jit(solution)/shard_map/ppermute | solution.py:43
  114.9 4.2 %collective-permute-start.8 = (bf16[96,256]{1,0:T(8,128)(2,1)S(1)}, bf16[96,256]{1,0:T(8,128)(2,1)S(1)}, u32[]{:S(2)}, u32[]{:S(2)}) collective-permute-start(bf16[96,256]{1,0:T(8,128)(2,1)S(1)} %add_reduce-precision_fusion.1), channel_id=1, source_target_pairs={{0,2},{1,3},{2,0},{3,1},{4,6},{5,7},{6,4},{7,5},{128,130},{129,131... | collective-permute-start | bytes 147464 | tf_op jit(solution)/shard_map/ppermute | solution.py:43
  119.1 5.4 %collective-permute-start.9 = (bf16[96,256]{1,0:T(8,128)(2,1)S(1)}, bf16[96,256]{1,0:T(8,128)(2,1)S(1)}, u32[]{:S(2)}, u32[]{:S(2)}) collective-permute-start(bf16[96,256]{1,0:T(8,128)(2,1)S(1)} %add_reduce-precision_fusion), channel_id=1, source_target_pairs={{0,6},{1,7},{2,4},{3,5},{4,2},{5,3},{6,0},{7,1},{128,134},{129,135... | collective-permute-start | bytes 147464 | tf_op jit(solution)/shard_map/ppermute | solution.py:43

commit v11 on v10

--- a/solution.py
+++ b/solution.py
@@ -124,12 +124,15 @@
     page_len = page_cache.shape[2]
     scaling = 1.0 / math.sqrt(head_dim)
     kv_per_sect = kv_heads // sect_size
-    by_kv = jnp.moveaxis(queries.reshape(*queries.shape[:2], kv_per_sect, head_dim), 2, 0)
-    per_target = jnp.broadcast_to(
-        by_kv[:, None], (kv_per_sect, head_size // kv_per_sect, *by_kv.shape[1:])
-    ).reshape(head_size, *by_kv.shape[1:])
+    own_slot = (jnp.arange(head_size) == lax.axis_index("head")).astype(queries.dtype)
+    collected = own_slot[:, None, None, None] * queries[None]
+    for step in (2, 6, 1):
+        collected = collected + lax.ppermute(
+            collected, "head", [(i, i ^ step) for i in range(head_size)]
+        )
+    kv_local = kv_index % kv_per_sect
     group_query = in_order(
-        lax.all_to_all(per_target, "head", split_axis=0, concat_axis=0, tiled=True), 1
+        lax.dynamic_slice_in_dim(collected, kv_local * head_dim, head_dim, 3), 1
     )
     heads_dev = group_query.shape[1] // group_size
     block_cols = heads_dev * head_dim

time: 126 us -> 131 us (1.040); the launches traced: 125 us -> 128 us
  starting transfers between devices: 32.5 us -> 42.2 us
  waiting for transfers between devices: 61.7 us -> 54.3 us
  other arithmetic: 9.99 us -> 11.8 us
    ppermute x8, waiting for transfers between devices: 31.9 us -> 24.1 us  [doubled_sum(): partner = lax.ppermute(shard, axis, [(i, i ^ step) for i in range(count)])]
    ppermute x8, starting transfers between devices: 5.25 us -> 12.9 us  [doubled_sum(): partner = lax.ppermute(shard, axis, [(i, i ^ step) for i in range(count)])]
    ppermute x0 -> x3, starting transfers between devices: none -> 7.04 us  [on_device(): lax.ppermute(collected, 'head', [(i, i ^ step) for i in range(head_size)])]
    all_to_all x1 -> x0, starting transfers between devices: 6.93 us -> none  [on_device(): lax.all_to_all(per_target, 'head', split_axis=0, concat_axis=0, tiled=True)]
    ppermute x0 -> x3, waiting for transfers between devices: none -> 5.56 us  [on_device(): lax.ppermute(collected, 'head', [(i, i ^ step) for i in range(head_size)])]
    all_to_all x1 -> x0, waiting for transfers between devices: 3.43 us -> none  [on_device(): lax.all_to_all(per_target, 'head', split_axis=0, concat_axis=0, tiled=True)]
    ppermute x2, waiting for transfers between devices: 10.3 us -> 8.35 us  [from_partner(): lax.ppermute(shard, axis, [(i, i ^ 1 << distance) for i in range(lax.axis...]
    ppermute x2, starting transfers between devices: 1.39 us -> 3.36 us  [from_partner(): lax.ppermute(shard, axis, [(i, i ^ 1 << distance) for i in range(lax.axis...]
  transfers between devices with their start and end apart: 14 -> 16, of which waited for: 14 -> 15; matrix products, arithmetic and copies ran while one was open for 12% -> 12% of each run, Pallas kernels for 0% -> 0%
where the time goes in v11:
time: 131 us; the launch traced here: 128 us
  waiting for transfers between devices  54.3 us (41%)
  starting transfers between devices  42.2 us (32%)
  local copies, waits for them, and re-layouts  12.1 us (9%)
  other arithmetic  11.8 us (9%)
  matrix products  7.57 us (6%)
    ppermute x8, waiting for transfers between devices, doubled_sum(): partner = lax.ppermute(shard, axis, [(i, i ^ step) for i in range(count)])  24.1 us
    ppermute x8, starting transfers between devices, doubled_sum(): partner = lax.ppermute(shard, axis, [(i, i ^ step) for i in range(count)])  12.9 us
    all_to_all x1, starting transfers between devices, copy_for_each(): return lax.all_to_all(copies, axis, split_axis=0, concat_axis=0, tiled=True)  8.59 us
    ppermute x2, waiting for transfers between devices, from_partner(): lax.ppermute(shard, axis, [(i, i ^ 1 << distance) for i in range(lax.axis...  8.35 us
    ppermute x3, starting transfers between devices, on_device(): lax.ppermute(collected, 'head', [(i, i ^ step) for i in range(head_size)])  7.04 us
    all_to_all x1, waiting for transfers between devices, on_device(): lax.all_to_all(leaving.astype(jnp.bfloat16), 'batch', split_axis=2, conca...  6.09 us
    ppermute x3, waiting for transfers between devices, on_device(): lax.ppermute(collected, 'head', [(i, i ^ step) for i in range(head_size)])  5.56 us
    all_to_all x1, starting transfers between devices, on_device(): lax.all_to_all(outgoing, 'batch', split_axis=0, concat_axis=0, tiled=True)  5.4 us
  transfers between devices with their start and end apart: 16, of which 15 were waited for; matrix products, arithmetic and copies ran while one was open for 12% of the time, Pallas kernels for 0%

profile of v11, /device:TPU:32, one launch (start us, length us, event | category | flops | bytes accessed | tf_op | source)
XLA Modules:
  0.0 128.4 jit_solution(1207190969656259674)
XLA Ops:
  3.7 3.2 %fusion.68 = (bf16[6,16,64,128]{3,2,1,0:T(8,128)(2,1)S(1)}, bf16[6,16,64,128]{3,2,1,0:T(8,128)(2,1)S(1)}) fusion(bf16[6,16,64,256]{3,2,1,0:T(8,128)(2,1)} %param.14), kind=kLoop, calls=%fused_computation.139 | loop fusion | bytes 6291456 | tf_op jit(solution)/shard_map/slice | solution.py:153
  7.2 2.2 %collective-permute-start.1 = (bf16[8,6,2,256]{3,2,0,1:T(2,128)(2,1)S(1)}, bf16[8,6,2,256]{3,2,0,1:T(2,128)(2,1)S(1)}, u32[]{:S(2)}, u32[]{:S(2)}) collective-permute-start(bf16[8,6,2,256]{3,2,0,1:T(2,128)(2,1)S(1)} %fusion.65), channel_id=1, source_target_pairs={{0,6},{1,7},{2,4},{3,5},{4,2},{5,3},{6,0},{7,1},{8,14},{9,15},{10,... | collective-permute-start | bytes 147464 | tf_op jit(solution)/shard_map/ppermute | solution.py:130
  9.4 3.2 %collective-permute-done.1 = bf16[8,6,2,256]{3,2,0,1:T(2,128)(2,1)S(1)} collective-permute-done((bf16[8,6,2,256]{3,2,0,1:T(2,128)(2,1)S(1)}, bf16[8,6,2,256]{3,2,0,1:T(2,128)(2,1)S(1)}, u32[]{:S(2)}, u32[]{:S(2)}) %collective-permute-start.1) | collective-permute-done | bytes 49184 | tf_op jit(solution)/shard_map/ppermute | solution.py:130
  12.7 3.3 %collective-permute-start.2 = (bf16[8,6,2,256]{3,2,0,1:T(2,128)(2,1)S(1)}, bf16[8,6,2,256]{3,2,0,1:T(2,128)(2,1)}, u32[]{:S(2)}, u32[]{:S(2)}) collective-permute-start(bf16[8,6,2,256]{3,2,0,1:T(2,128)(2,1)S(1)} %fusion.83), channel_id=1, source_target_pairs={{0,1},{1,0},{2,3},{3,2},{4,5},{5,4},{6,7},{7,6},{8,9},{9,8},{10,11... | collective-permute-start | bytes 147464 | tf_op jit(solution)/shard_map/ppermute | solution.py:130
  16.1 2.4 %collective-permute-done.2 = bf16[8,6,2,256]{3,2,0,1:T(2,128)(2,1)} collective-permute-done((bf16[8,6,2,256]{3,2,0,1:T(2,128)(2,1)S(1)}, bf16[8,6,2,256]{3,2,0,1:T(2,128)(2,1)}, u32[]{:S(2)}, u32[]{:S(2)}) %collective-permute-start.2) | collective-permute-done | bytes 49184 | tf_op jit(solution)/shard_map/ppermute | solution.py:130
  22.4 3.8 %collective-permute-done.3 = f32[6,8,130]{2,1,0:T(8,128)S(1)} collective-permute-done((f32[6,8,130]{2,1,0:T(8,128)S(1)}, f32[6,8,130]{2,1,0:T(8,128)S(1)}, u32[]{:S(2)}, u32[]{:S(2)}) %collective-permute-start.3) | collective-permute-done | bytes 24992 | tf_op jit(solution)/shard_map/ppermute | solution.py:33
  27.2 3.3 %collective-permute-start.4 = (f32[6,4,130]{0,1,2:T(4,128)S(1)}, f32[6,4,130]{0,1,2:T(4,128)S(1)}, u32[]{:S(2)}, u32[]{:S(2)}) collective-permute-start(f32[6,4,130]{0,1,2:T(4,128)S(1)} %constant_dynamic-slice_fusion.5), channel_id=1, source_target_pairs={{0,1},{1,0},{2,3},{3,2},{4,5},{5,4},{6,7},{7,6},{8,9},{9,8},{10,11... | collective-permute-start | bytes 37448 | tf_op jit(solution)/shard_map/ppermute | solution.py:33
  30.7 4.5 %collective-permute-done.4 = f32[6,4,130]{0,1,2:T(4,128)S(1)} collective-permute-done((f32[6,4,130]{0,1,2:T(4,128)S(1)}, f32[6,4,130]{0,1,2:T(4,128)S(1)}, u32[]{:S(2)}, u32[]{:S(2)}) %collective-permute-start.4) | collective-permute-done | bytes 12512 | tf_op jit(solution)/shard_map/ppermute | solution.py:33
  36.2 8.6 %all-to-all-start = ((bf16[16,6,512]{2,1,0:T(8,128)(2,1)}), bf16[16,6,512]{2,1,0:T(8,128)(2,1)S(1)}, u32[]{:S(2)}, u32[]{:S(2)}) async-start(bf16[16,6,512]{2,1,0:T(8,128)(2,1)} %broadcast_in_dim.76), calls=%async_computation | async-start | bytes 262144 | tf_op jit(solution)/shard_map/all_to_all | solution.py:18
  44.9 1.8 %reduce-window.6 = s32[64,6,128]{2,0,1:T(8,128)S(1)} reduce-window(s32[64,6,128]{2,0,1:T(8,128)S(1)} %fusion.28, s32[]{:T(128)} %constant.120.clone.1), window={size=1x1x128 pad=0_0x0_0x127_0}, to_apply=%region_3.4 | reduce-window | flops 6242304 | bytes 393220 | tf_op jit(solution)/shard_map/reduce-window
  47.0 5.2 %all-to-all-done = bf16[16,6,512]{2,1,0:T(8,128)(2,1)S(1)} async-done(((bf16[16,6,512]{2,1,0:T(8,128)(2,1)}), bf16[16,6,512]{2,1,0:T(8,128)(2,1)S(1)}, u32[]{:S(2)}, u32[]{:S(2)}) %all-to-all-start) | async-done | bytes 98336 | tf_op jit(solution)/shard_map/all_to_all | solution.py:18
  52.4 1.7 %collective-permute-start.5 = (bf16[96,256]{1,0:T(8,128)(2,1)S(1)}, bf16[96,256]{1,0:T(8,128)(2,1)S(1)}, u32[]{:S(2)}, u32[]{:S(2)}) collective-permute-start(bf16[96,256]{1,0:T(8,128)(2,1)S(1)} %convolution_convert_fusion.2), channel_id=1, source_target_pairs={{0,128},{1,129},{2,130},{3,131},{4,132},{5,133},{6,134},{7,135},{1... | collective-permute-start | bytes 147464 | tf_op jit(solution)/shard_map/ppermute | solution.py:43
  54.3 2.4 %collective-permute-done.5 = bf16[96,256]{1,0:T(8,128)(2,1)S(1)} collective-permute-done((bf16[96,256]{1,0:T(8,128)(2,1)S(1)}, bf16[96,256]{1,0:T(8,128)(2,1)S(1)}, u32[]{:S(2)}, u32[]{:S(2)}) %collective-permute-start.5) | collective-permute-done | bytes 49184 | tf_op jit(solution)/shard_map/ppermute | solution.py:43
  56.7 3.1 %collective-permute-start.6 = (bf16[96,256]{1,0:T(8,128)(2,1)S(1)}, bf16[96,256]{1,0:T(8,128)(2,1)S(1)}, u32[]{:S(2)}, u32[]{:S(2)}) collective-permute-start(bf16[96,256]{1,0:T(8,128)(2,1)S(1)} %add_reduce-precision_fusion.6), channel_id=1, source_target_pairs={{0,129},{1,128},{2,131},{3,130},{4,133},{5,132},{6,135},{7,134},{1... | collective-permute-start | bytes 147464 | tf_op jit(solution)/shard_map/ppermute | solution.py:43
  59.9 2.2 %collective-permute-done.6 = bf16[96,256]{1,0:T(8,128)(2,1)S(1)} collective-permute-done((bf16[96,256]{1,0:T(8,128)(2,1)S(1)}, bf16[96,256]{1,0:T(8,128)(2,1)S(1)}, u32[]{:S(2)}, u32[]{:S(2)}) %collective-permute-start.6) | collective-permute-done | bytes 49184 | tf_op jit(solution)/shard_map/ppermute | solution.py:43
  63.2 3.0 %collective-permute-done.7 = bf16[96,256]{1,0:T(8,128)(2,1)S(1)} collective-permute-done((bf16[96,256]{1,0:T(8,128)(2,1)S(1)}, bf16[96,256]{1,0:T(8,128)(2,1)S(1)}, u32[]{:S(2)}, u32[]{:S(2)}) %collective-permute-start.7) | collective-permute-done | bytes 49184 | tf_op jit(solution)/shard_map/ppermute | solution.py:43
  66.3 2.2 %collective-permute-start.8 = (bf16[96,256]{1,0:T(8,128)(2,1)S(1)}, bf16[96,256]{1,0:T(8,128)(2,1)S(1)}, u32[]{:S(2)}, u32[]{:S(2)}) collective-permute-start(bf16[96,256]{1,0:T(8,128)(2,1)S(1)} %add_reduce-precision_fusion.4), channel_id=1, source_target_pairs={{0,6},{1,7},{2,4},{3,5},{4,2},{5,3},{6,0},{7,1},{128,134},{129,135... | collective-permute-start | bytes 147464 | tf_op jit(solution)/shard_map/ppermute | solution.py:43
  68.5 3.2 %collective-permute-done.8 = bf16[96,256]{1,0:T(8,128)(2,1)S(1)} collective-permute-done((bf16[96,256]{1,0:T(8,128)(2,1)S(1)}, bf16[96,256]{1,0:T(8,128)(2,1)S(1)}, u32[]{:S(2)}, u32[]{:S(2)}) %collective-permute-start.8) | collective-permute-done | bytes 49184 | tf_op jit(solution)/shard_map/ppermute | solution.py:43
  73.0 5.4 %all-to-all-start.1 = ((bf16[16,27,256]{2,1,0:T(8,128)(2,1)}), bf16[16,27,256]{2,1,0:T(8,128)(2,1)}, u32[]{:S(2)}, u32[]{:S(2)}) async-start(bf16[16,27,256]{2,1,0:T(8,128)(2,1)} %fusion.17), calls=%async_computation.1 | async-start | bytes 524288 | tf_op jit(solution)/shard_map/all_to_all | solution.py:248
  78.4 3.4 %copy.233 = bf16[4096,384]{1,0:T(8,128)(2,1)S(1)} copy(bf16[4096,384]{0,1:T(8,128)(2,1)} %bitcast.124) | data formatting | bytes 6291456 | tf_op jit(solution)/shard_map/ecf,efd->ecd/dot_general | solution.py:261
  83.1 5.0 %all-to-all-done.1 = bf16[16,27,256]{2,1,0:T(8,128)(2,1)} async-done(((bf16[16,27,256]{2,1,0:T(8,128)(2,1)}), bf16[16,27,256]{2,1,0:T(8,128)(2,1)}, u32[]{:S(2)}, u32[]{:S(2)}) %all-to-all-start.1) | async-done | bytes 221216 | tf_op jit(solution)/shard_map/all_to_all | solution.py:248
  89.0 3.8 %fusion.11 = f32[1,24,2,384]{3,1,2,0:T(8,128)S(1)} fusion(bf16[16,256,2,384]{3,2,1,0:T(2,128)(2,1)} %bitcast.142, bf16[16,27,256]{2,1,0:T(8,128)(2,1)} %all-to-all-done.1, f32[24]{0:T(128)S(1)} %add_rsqrt_fusion), kind=kOutput, calls=%fused_computation.14 | convolution fusion | flops 151013376 | bytes 6561888 | tf_op jit(solution)/shard_map/becd,ebdgf->ecgf/dot_general | solution.py:253
  92.8 1.9 %fusion.4 = bf16[1,24,16,256]{3,1,0,2:T(8,128)(2,1)} fusion(bf16[16,256,384]{2,1,0:T(8,128)(2,1)S(1)} %bitcast.121, f32[1,24,2,384]{3,1,2,0:T(8,128)S(1)} %fusion.11), kind=kOutput, calls=%fused_computation.9 | convolution fusion | flops 75651072 | bytes 3416064 | tf_op jit(solution)/shard_map/ecf,efd->ecd/dot_general | solution.py:261
  94.7 5.0 %all-to-all-start.2 = ((bf16[1,24,16,256]{3,1,0,2:T(8,128)(2,1)}), bf16[1,24,16,256]{3,1,0,2:T(8,128)(2,1)S(1)}, u32[]{:S(2)}, u32[]{:S(2)}) async-start(bf16[1,24,16,256]{3,1,0,2:T(8,128)(2,1)} %fusion.4), calls=%async_computation.2 | async-start | bytes 393216 | tf_op jit(solution)/shard_map/all_to_all | solution.py:266
  100.4 1.6 %select_reduce_fusion = bf16[768,96]{0,1:T(8,128)(2,1)S(1)} fusion(f32[96,8]{1,0:T(8,128)S(1)} %copy.221, s32[96,8]{1,0:T(8,128)} %copy-done.2), kind=kLoop, calls=%fused_computation.2 | loop fusion | flops 1695744 | bytes 153600 | tf_op jit(solution)/shard_map/reduce_sum | solution.py:236
  102.3 6.1 %all-to-all-done.2 = bf16[1,24,16,256]{3,1,0,2:T(8,128)(2,1)S(1)} async-done(((bf16[1,24,16,256]{3,1,0,2:T(8,128)(2,1)}), bf16[1,24,16,256]{3,1,0,2:T(8,128)(2,1)S(1)}, u32[]{:S(2)}, u32[]{:S(2)}) %all-to-all-start.2) | async-done | bytes 196640 | tf_op jit(solution)/shard_map/all_to_all | solution.py:266
  109.0 3.7 %collective-permute-done.9 = bf16[96,256]{1,0:T(8,128)(2,1)S(1)} collective-permute-done((bf16[96,256]{1,0:T(8,128)(2,1)S(1)}, bf16[96,256]{1,0:T(8,128)(2,1)S(1)}, u32[]{:S(2)}, u32[]{:S(2)}) %collective-permute-start.9) | collective-permute-done | bytes 49184 | tf_op jit(solution)/shard_map/ppermute | solution.py:43
  112.8 3.1 %collective-permute-start.10 = (bf16[96,256]{1,0:T(8,128)(2,1)S(1)}, bf16[96,256]{1,0:T(8,128)(2,1)S(1)}, u32[]{:S(2)}, u32[]{:S(2)}) collective-permute-start(bf16[96,256]{1,0:T(8,128)(2,1)S(1)} %add_reduce-precision_fusion.2), channel_id=1, source_target_pairs={{0,129},{1,128},{2,131},{3,130},{4,133},{5,132},{6,135},{7,134},{1... | collective-permute-start | bytes 147464 | tf_op jit(solution)/shard_map/ppermute | solution.py:43
  115.9 2.3 %collective-permute-done.10 = bf16[96,256]{1,0:T(8,128)(2,1)S(1)} collective-permute-done((bf16[96,256]{1,0:T(8,128)(2,1)S(1)}, bf16[96,256]{1,0:T(8,128)(2,1)S(1)}, u32[]{:S(2)}, u32[]{:S(2)}) %collective-permute-start.10) | collective-permute-done | bytes 49184 | tf_op jit(solution)/shard_map/ppermute | solution.py:43
  118.3 4.1 %collective-permute-done.11 = bf16[96,256]{1,0:T(8,128)(2,1)S(1)} collective-permute-done((bf16[96,256]{1,0:T(8,128)(2,1)S(1)}, bf16[96,256]{1,0:T(8,128)(2,1)S(1)}, u32[]{:S(2)}, u32[]{:S(2)}) %collective-permute-start.11) | collective-permute-done | bytes 49184 | tf_op jit(solution)/shard_map/ppermute | solution.py:43
  122.4 2.2 %collective-permute-start.12 = (bf16[96,256]{1,0:T(8,128)(2,1)S(1)}, bf16[96,256]{1,0:T(8,128)(2,1)S(1)}, u32[]{:S(2)}, u32[]{:S(2)}) collective-permute-start(bf16[96,256]{1,0:T(8,128)(2,1)S(1)} %add_reduce-precision_fusion), channel_id=1, source_target_pairs={{0,6},{1,7},{2,4},{3,5},{4,2},{5,3},{6,0},{7,1},{128,134},{129,135... | collective-permute-start | bytes 147464 | tf_op jit(solution)/shard_map/ppermute | solution.py:43
  124.6 3.2 %collective-permute-done.12 = bf16[96,256]{1,0:T(8,128)(2,1)S(1)} collective-permute-done((bf16[96,256]{1,0:T(8,128)(2,1)S(1)}, bf16[96,256]{1,0:T(8,128)(2,1)S(1)}, u32[]{:S(2)}, u32[]{:S(2)}) %collective-permute-start.12) | collective-permute-done | bytes 49184 | tf_op jit(solution)/shard_map/ppermute | solution.py:43
  (108 shorter events, 18.0 us)
Async XLA Ops:
  0.0 52.2 %copy-start = (bf16[512,256]{1,0:T(8,128)(2,1)S(1)}, bf16[512,256]{1,0:T(8,128)(2,1)}, u32[]{:S(2)}) copy-start(bf16[512,256]{1,0:T(8,128)(2,1)} %param.17) | copy-start | bytes 786436
  0.9 6.2 %collective-permute-start = (bf16[8,6,2,256]{3,2,0,1:T(2,128)(2,1)S(1)}, bf16[8,6,2,256]{3,2,0,1:T(2,128)(2,1)S(1)}, u32[]{:S(2)}, u32[]{:S(2)}) collective-permute-start(bf16[8,6,2,256]{3,2,0,1:T(2,128)(2,1)S(1)} %broadcast_multiply_fusion), channel_id=1, source_target_pairs={{0,2},{1,3},{2,0},{3,1},{4,6},{5,7},{6,4},{7,5},{8,10},{9,11},{10,... | collective-permute-start | bytes 147464 | tf_op jit(solution)/shard_map/ppermute | solution.py:130
  3.7 3.2 %copy-start.7 = (s32[6]{0:T(128)S(1)}, s32[6]{0:T(128)}, u32[]{:S(2)}) copy-start(s32[6]{0:T(128)} %param.15) | copy-start | bytes 76
  3.7 3.3 %copy-start.3 = (bf16[6,2,256]{2,1,0:T(2,128)(2,1)S(1)}, bf16[6,2,256]{2,1,0:T(2,128)(2,1)}, u32[]{:S(2)}) copy-start(bf16[6,2,256]{2,1,0:T(2,128)(2,1)} %param.12) | copy-start | bytes 18436
  3.7 5.7 %copy-start.5 = (bf16[6,4,256]{2,1,0:T(4,128)(2,1)S(1)}, bf16[6,4,256]{2,1,0:T(4,128)(2,1)}, u32[]{:S(2)}) copy-start(bf16[6,4,256]{2,1,0:T(4,128)(2,1)} %param.13) | copy-start | bytes 36868
  7.2 5.4 %collective-permute-start.1 = (bf16[8,6,2,256]{3,2,0,1:T(2,128)(2,1)S(1)}, bf16[8,6,2,256]{3,2,0,1:T(2,128)(2,1)S(1)}, u32[]{:S(2)}, u32[]{:S(2)}) collective-permute-start(bf16[8,6,2,256]{3,2,0,1:T(2,128)(2,1)S(1)} %fusion.65), channel_id=1, source_target_pairs={{0,6},{1,7},{2,4},{3,5},{4,2},{5,3},{6,0},{7,1},{8,14},{9,15},{10,... | collective-permute-start | bytes 147464 | tf_op jit(solution)/shard_map/ppermute | solution.py:130
  12.7 5.8 %collective-permute-start.2 = (bf16[8,6,2,256]{3,2,0,1:T(2,128)(2,1)S(1)}, bf16[8,6,2,256]{3,2,0,1:T(2,128)(2,1)}, u32[]{:S(2)}, u32[]{:S(2)}) collective-permute-start(bf16[8,6,2,256]{3,2,0,1:T(2,128)(2,1)S(1)} %fusion.83), channel_id=1, source_target_pairs={{0,1},{1,0},{2,3},{3,2},{4,5},{5,4},{6,7},{7,6},{8,9},{9,8},{10,11... | collective-permute-start | bytes 147464 | tf_op jit(solution)/shard_map/ppermute | solution.py:130
  22.1 4.2 %collective-permute-start.3 = (f32[6,8,130]{2,1,0:T(8,128)S(1)}, f32[6,8,130]{2,1,0:T(8,128)S(1)}, u32[]{:S(2)}, u32[]{:S(2)}) collective-permute-start(f32[6,8,130]{2,1,0:T(8,128)S(1)} %copy.202), channel_id=1, source_target_pairs={{0,2},{1,3},{2,0},{3,1},{4,6},{5,7},{6,4},{7,5},{8,10},{9,11},{10,... | collective-permute-start | bytes 74888 | tf_op jit(solution)/shard_map/ppermute | solution.py:33
  22.2 8.3 %copy-start.4 = (s32[96,8]{0,1:T(8,128)S(1)}, s32[96,8]{0,1:T(8,128)}, u32[]{:S(2)}) copy-start(s32[96,8]{0,1:T(8,128)} %param.20) | copy-start | bytes 9220
  27.2 8.0 %collective-permute-start.4 = (f32[6,4,130]{0,1,2:T(4,128)S(1)}, f32[6,4,130]{0,1,2:T(4,128)S(1)}, u32[]{:S(2)}, u32[]{:S(2)}) collective-permute-start(f32[6,4,130]{0,1,2:T(4,128)S(1)} %constant_dynamic-slice_fusion.5), channel_id=1, source_target_pairs={{0,1},{1,0},{2,3},{3,2},{4,5},{5,4},{6,7},{7,6},{8,9},{9,8},{10,11... | collective-permute-start | bytes 37448 | tf_op jit(solution)/shard_map/ppermute | solution.py:33
  35.5 36.2 %copy-start.1 = (bf16[96,256]{1,0:T(8,128)(2,1)S(1)}, bf16[96,256]{1,0:T(8,128)(2,1)}, u32[]{:S(2)}) copy-start(bf16[96,256]{1,0:T(8,128)(2,1)} %param.18) | copy-start | bytes 147460
  36.2 16.0 %all-to-all-start = ((bf16[16,6,512]{2,1,0:T(8,128)(2,1)}), bf16[16,6,512]{2,1,0:T(8,128)(2,1)S(1)}, u32[]{:S(2)}, u32[]{:S(2)}) async-start(bf16[16,6,512]{2,1,0:T(8,128)(2,1)} %broadcast_in_dim.76), calls=%async_computation | async-start | bytes 262144 | tf_op jit(solution)/shard_map/all_to_all | solution.py:18
  44.8 27.3 %copy-start.6 = (f32[256]{0:T(256)S(1)}, f32[256]{0:T(256)}, u32[]{:S(2)}) copy-start(f32[256]{0:T(256)} %param.19) | copy-start | bytes 3076
  52.4 4.3 %collective-permute-start.5 = (bf16[96,256]{1,0:T(8,128)(2,1)S(1)}, bf16[96,256]{1,0:T(8,128)(2,1)S(1)}, u32[]{:S(2)}, u32[]{:S(2)}) collective-permute-start(bf16[96,256]{1,0:T(8,128)(2,1)S(1)} %convolution_convert_fusion.2), channel_id=1, source_target_pairs={{0,128},{1,129},{2,130},{3,131},{4,132},{5,133},{6,134},{7,135},{1... | collective-permute-start | bytes 147464 | tf_op jit(solution)/shard_map/ppermute | solution.py:43
  56.7 5.4 %collective-permute-start.6 = (bf16[96,256]{1,0:T(8,128)(2,1)S(1)}, bf16[96,256]{1,0:T(8,128)(2,1)S(1)}, u32[]{:S(2)}, u32[]{:S(2)}) collective-permute-start(bf16[96,256]{1,0:T(8,128)(2,1)S(1)} %add_reduce-precision_fusion.6), channel_id=1, source_target_pairs={{0,129},{1,128},{2,131},{3,130},{4,133},{5,132},{6,135},{7,134},{1... | collective-permute-start | bytes 147464 | tf_op jit(solution)/shard_map/ppermute | solution.py:43
  59.9 2.3 %copy-start.2 = (s32[96,8]{1,0:T(8,128)}, s32[96,8]{1,0:T(8,128)S(1)}, u32[]{:S(2)}) copy-start(s32[96,8]{1,0:T(8,128)S(1)} %fusion.34) | copy-start | bytes 9220
  62.1 4.2 %collective-permute-start.7 = (bf16[96,256]{1,0:T(8,128)(2,1)S(1)}, bf16[96,256]{1,0:T(8,128)(2,1)S(1)}, u32[]{:S(2)}, u32[]{:S(2)}) collective-permute-start(bf16[96,256]{1,0:T(8,128)(2,1)S(1)} %add_reduce-precision_fusion.5), channel_id=1, source_target_pairs={{0,2},{1,3},{2,0},{3,1},{4,6},{5,7},{6,4},{7,5},{128,130},{129,131... | collective-permute-start | bytes 147464 | tf_op jit(solution)/shard_map/ppermute | solution.py:43
  66.3 5.4 %collective-permute-start.8 = (bf16[96,256]{1,0:T(8,128)(2,1)S(1)}, bf16[96,256]{1,0:T(8,128)(2,1)S(1)}, u32[]{:S(2)}, u32[]{:S(2)}) collective-permute-start(bf16[96,256]{1,0:T(8,128)(2,1)S(1)} %add_reduce-precision_fusion.4), channel_id=1, source_target_pairs={{0,6},{1,7},{2,4},{3,5},{4,2},{5,3},{6,0},{7,1},{128,134},{129,135... | collective-permute-start | bytes 147464 | tf_op jit(solution)/shard_map/ppermute | solution.py:43
  73.0 15.1 %all-to-all-start.1 = ((bf16[16,27,256]{2,1,0:T(8,128)(2,1)}), bf16[16,27,256]{2,1,0:T(8,128)(2,1)}, u32[]{:S(2)}, u32[]{:S(2)}) async-start(bf16[16,27,256]{2,1,0:T(8,128)(2,1)} %fusion.17), calls=%async_computation.1 | async-start | bytes 524288 | tf_op jit(solution)/shard_map/all_to_all | solution.py:248
  94.7 13.6 %all-to-all-start.2 = ((bf16[1,24,16,256]{3,1,0,2:T(8,128)(2,1)}), bf16[1,24,16,256]{3,1,0,2:T(8,128)(2,1)S(1)}, u32[]{:S(2)}, u32[]{:S(2)}) async-start(bf16[1,24,16,256]{3,1,0,2:T(8,128)(2,1)} %fusion.4), calls=%async_computation.2 | async-start | bytes 393216 | tf_op jit(solution)/shard_map/all_to_all | solution.py:266
  108.6 4.2 %collective-permute-start.9 = (bf16[96,256]{1,0:T(8,128)(2,1)S(1)}, bf16[96,256]{1,0:T(8,128)(2,1)S(1)}, u32[]{:S(2)}, u32[]{:S(2)}) collective-permute-start(bf16[96,256]{1,0:T(8,128)(2,1)S(1)} %fusion.71), channel_id=1, source_target_pairs={{0,128},{1,129},{2,130},{3,131},{4,132},{5,133},{6,134},{7,135},{1... | collective-permute-start | bytes 147464 | tf_op jit(solution)/shard_map/ppermute | solution.py:43
  112.8 5.4 %collective-permute-start.10 = (bf16[96,256]{1,0:T(8,128)(2,1)S(1)}, bf16[96,256]{1,0:T(8,128)(2,1)S(1)}, u32[]{:S(2)}, u32[]{:S(2)}) collective-permute-start(bf16[96,256]{1,0:T(8,128)(2,1)S(1)} %add_reduce-precision_fusion.2), channel_id=1, source_target_pairs={{0,129},{1,128},{2,131},{3,130},{4,133},{5,132},{6,135},{7,134},{1... | collective-permute-start | bytes 147464 | tf_op jit(solution)/shard_map/ppermute | solution.py:43
  118.2 4.2 %collective-permute-start.11 = (bf16[96,256]{1,0:T(8,128)(2,1)S(1)}, bf16[96,256]{1,0:T(8,128)(2,1)S(1)}, u32[]{:S(2)}, u32[]{:S(2)}) collective-permute-start(bf16[96,256]{1,0:T(8,128)(2,1)S(1)} %add_reduce-precision_fusion.1), channel_id=1, source_target_pairs={{0,2},{1,3},{2,0},{3,1},{4,6},{5,7},{6,4},{7,5},{128,130},{129,131... | collective-permute-start | bytes 147464 | tf_op jit(solution)/shard_map/ppermute | solution.py:43
  122.4 5.4 %collective-permute-start.12 = (bf16[96,256]{1,0:T(8,128)(2,1)S(1)}, bf16[96,256]{1,0:T(8,128)(2,1)S(1)}, u32[]{:S(2)}, u32[]{:S(2)}) collective-permute-start(bf16[96,256]{1,0:T(8,128)(2,1)S(1)} %add_reduce-precision_fusion), channel_id=1, source_target_pairs={{0,6},{1,7},{2,4},{3,5},{4,2},{5,3},{6,0},{7,1},{128,134},{129,135... | collective-permute-start | bytes 147464 | tf_op jit(solution)/shard_map/ppermute | solution.py:43
